TPU v7x, 512 devices: a whole 4x4x16 slice. The times are simulated.
512 devices in a mesh: dp: 4 (over x), tensor: 128 (over y, z, core).
Axes of the slice: x: 4, y: 4, z: 16, core: 2. Of those that a mesh axis runs over, the one named last changes fastest.
Arguments:
- stream: bfloat16 [32768, 2560], P(('dp', 'tensor')), parts along dimension 0, may hold values from -6 to 6
- queries: bfloat16 [512, 2560], P(('dp', 'tensor')), parts along dimension 0, may hold values from -170 to 170
- fresh_entries: bfloat16 [512, 1024], P(('dp', 'tensor')), parts along dimension 0, may hold values from -6 to 6
- paged_store_cache: bfloat16 [2560, 2, 128, 512], P(('dp', 'tensor')), parts along dimension 0, may hold values from -6 to 6
- page_table: int32 [512, 32], P('dp'), parts along dimension 0, may hold values from -1 to 639, as said below
- cache_length: int32 [512], P('dp'), parts along dimension 0, may hold values from 1 to 4096, as said below
- out_proj: bfloat16 [2560, 2560], P(None, 'tensor'), may hold values from -0.125 to 0.125
- norm_gain: bfloat16 [2560], replicated, may hold values from 0.099609375 to 1.8984375
- router: bfloat16 [2560, 64], replicated, may hold values from -0.125 to 0.125
- routes: int32 [32768, 6], P(('dp', 'tensor')), parts along dimension 0, may hold values from 0 to 63, as said below
- gate_up: bfloat16 [2, 24576, 2560], P(None, 'tensor'), may hold values from -0.125 to 0.125
- down_proj: bfloat16 [24576, 2560], P('tensor'), may hold values from -0.15625 to 0.15625
Outputs:
- layer_out: bfloat16 [32768, 2560], P(('dp', 'tensor')), parts along dimension 0
There are 4 independent parts, one for each index of `dp`. A program takes and returns all parts, laid end to end along the dimension named above; an argument that names none is the same for every part. Nothing has to cross between parts.
Inputs may be any that keep to these rules, and one draw needn't show every extreme that they name: `routes`: each row names 6 different experts. The rows of one device name each expert at most 6 times, and on every device one and the same expert below 16 is named exactly 6 times. `page_table`: row r lists in order the pages of request r's cache, ceil(cache_length[r] / 128) of them, then -1; every page belongs to exactly one request. `cache_length`: some request's cache holds exactly 4096 tokens.
All inputs are finite; a program needn't handle non-finite values.
Results may differ from a plain program's by a relative error of at most 0.0045.
Values may be sent and summed in bfloat16 or wider, within the bound.
No kernel may reach another device: no remote copies, remote signals or barrier semaphores. Data moves between devices by JAX's collectives and lax.ppermute only.
A program may use at most 64 MiB of HBM per device.

v0:
```python
import math

import jax
import jax.numpy as jnp
from jax import lax
from jax.sharding import PartitionSpec as P

QUERY_HEADS = 20
KEY_VALUE_HEADS = 4
HEAD_SIZE = 128
GROUP = 8
CAP = 6


NEG_FILL = -1e30
EPSILON = 1e-05


def finish_context(maxima, totals, accum, local_queries, local_entries):
    entry_count = local_queries.shape[0]
    key_value_width = KEY_VALUE_HEADS * HEAD_SIZE
    query_vector = local_queries.reshape(
        entry_count, KEY_VALUE_HEADS, QUERY_HEADS // KEY_VALUE_HEADS, HEAD_SIZE
    )
    token_key = local_entries[:, :key_value_width].reshape(entry_count, KEY_VALUE_HEADS, HEAD_SIZE)
    token_value = (
        local_entries[:, key_value_width:]
        .reshape(entry_count, KEY_VALUE_HEADS, HEAD_SIZE)
        .astype(jnp.float32)
    )
    own_score = jnp.einsum(
        "rhgd,rhd->rhg", query_vector, token_key, preferred_element_type=jnp.float32
    ) * (1.0 / math.sqrt(HEAD_SIZE))
    joined = jnp.maximum(maxima, own_score)
    old_coef = jnp.exp(maxima - joined)
    own_weight = jnp.exp(own_score - joined)
    totals = totals * old_coef + own_weight
    accum = accum * old_coef[..., None] + own_weight[..., None] * token_value[:, :, None, :]
    return (
        (accum / totals[..., None])
        .reshape(entry_count, QUERY_HEADS * HEAD_SIZE)
        .astype(jnp.bfloat16)
    )


def local_parts(query_all, paged_store_cache, page_table, cache_length, my_index):
    request_page_count = paged_store_cache.shape[0]
    page_length = paged_store_cache.shape[2]
    longest = page_table.shape[1]
    query_groups = QUERY_HEADS // KEY_VALUE_HEADS
    global_ids = my_index * request_page_count + jnp.arange(request_page_count, dtype=jnp.int32)
    matched = page_table[None, :, :] == global_ids[:, None, None]
    owner = jnp.any(matched, axis=2)
    position = jnp.sum(
        jnp.where(matched, jnp.arange(longest, dtype=jnp.int32)[None, None, :], 0), axis=(1, 2)
    )
    length_here = jnp.sum(jnp.where(owner, cache_length[None, :], 0), axis=1)
    query_page_scores = jnp.dot(
        owner.astype(jnp.bfloat16), query_all, preferred_element_type=jnp.float32
    ).astype(jnp.bfloat16)
    query_page_scores = query_page_scores.reshape(
        request_page_count, KEY_VALUE_HEADS, query_groups, HEAD_SIZE
    )
    key_matrix = paged_store_cache[:, 0].reshape(
        request_page_count, page_length, KEY_VALUE_HEADS, HEAD_SIZE
    )
    value_matrix = (
        paged_store_cache[:, 1]
        .reshape(request_page_count, page_length, KEY_VALUE_HEADS, HEAD_SIZE)
        .astype(jnp.float32)
    )
    scores = jnp.einsum(
        "phgd,pthd->phgt", query_page_scores, key_matrix, preferred_element_type=jnp.float32
    ) * (1.0 / math.sqrt(HEAD_SIZE))
    offsets = jnp.arange(page_length, dtype=jnp.int32)
    valid = position[:, None] * page_length + offsets[None, :] < length_here[:, None]
    scores = jnp.where(valid[:, None, None, :], scores, NEG_FILL)
    page_max = jnp.max(scores, axis=-1)
    weights = jnp.exp(scores - page_max[..., None])
    page_total = jnp.sum(weights, axis=-1)
    page_accum = jnp.einsum("phgt,pthd->phgd", weights, value_matrix)
    owned = owner[:, :, None, None]
    request_max = jnp.max(jnp.where(owned, page_max[:, None], NEG_FILL), axis=0)
    coef = jnp.where(owned, jnp.exp(page_max[:, None] - request_max[None]), 0.0)
    request_total = jnp.sum(coef * page_total[:, None], axis=0)
    request_accum = jnp.einsum("prhg,phgd->rhgd", coef, page_accum)
    return (request_max, request_total, request_accum)


def local(
    stream,
    queries,
    fresh_entries,
    paged_store_cache,
    page_table,
    cache_length,
    out_proj,
    norm_gain,
    router,
    routes,
    gate_up,
    down_proj,
):
    tensor_count = lax.axis_size("tensor")
    my_index = lax.axis_index("tensor")
    dec_rows = queries.shape[0]
    query_all, entries_all = (
        lax.all_gather(queries, "tensor", axis=0, tiled=True),
        lax.all_gather(fresh_entries, "tensor", axis=0, tiled=True),
    )
    request_max, request_total, request_accum = local_parts(
        query_all, paged_store_cache, page_table, cache_length, my_index
    )
    maxima = lax.pmax(request_max, "tensor")
    rescale = jnp.exp(request_max - maxima)
    totals, accum = lax.psum(
        (request_total * rescale, request_accum * rescale[..., None]), "tensor"
    )
    context = finish_context(maxima, totals, accum, query_all, entries_all)
    projected = jnp.dot(context, out_proj, preferred_element_type=jnp.float32)
    column_block = projected.shape[1]
    arrived = lax.all_to_all(
        projected.reshape(tensor_count, dec_rows, column_block),
        "tensor",
        split_axis=0,
        concat_axis=2,
        tiled=True,
    )
    widened = stream.astype(jnp.float32)
    widened = widened.at[:dec_rows].add(arrived[0])
    resid = lax.optimization_barrier(widened.astype(jnp.bfloat16))
    widened = resid.astype(jnp.float32)
    inverse = lax.rsqrt(jnp.mean(widened * widened, axis=-1, keepdims=True) + EPSILON)
    normed = (widened * inverse * norm_gain.astype(jnp.float32)).astype(jnp.bfloat16)
    logits = jnp.dot(normed, router, preferred_element_type=jnp.float32)
    chosen = jnp.take_along_axis(logits, routes, axis=1)
    gate_probs = jax.nn.softmax(chosen, axis=-1)
    expert_count = tensor_count // GROUP
    expert_ids = jnp.arange(expert_count, dtype=jnp.int32)
    matched = routes[:, :, None] == expert_ids[None, None, :]
    routed = jnp.any(matched, axis=1)
    gate_weight = jnp.sum(jnp.where(matched, gate_probs[:, :, None], 0.0), axis=1)
    routed_count = routed.astype(jnp.int32)
    ranking = jnp.cumsum(routed_count, axis=0) - routed_count
    slot_ids = jnp.arange(CAP, dtype=jnp.int32)
    selector = routed.T[:, None, :] & (ranking.T[:, None, :] == slot_ids[None, :, None])
    slot_rows = jnp.einsum(
        "eci,id->ecd", selector.astype(jnp.bfloat16), normed, preferred_element_type=jnp.float32
    ).astype(jnp.bfloat16)
    outgoing = jnp.repeat(slot_rows, GROUP, axis=0)
    contract_last = (((1,), (1,)), ((), ()))
    incoming = lax.all_to_all(outgoing, "tensor", split_axis=0, concat_axis=0, tiled=True)
    shape_in = incoming.shape
    flat_rows = incoming.reshape(-1, shape_in[2])
    gate_part = lax.dot_general(
        flat_rows, gate_up[0], contract_last, preferred_element_type=jnp.float32
    )
    upward = lax.dot_general(
        flat_rows, gate_up[1], contract_last, preferred_element_type=jnp.float32
    )
    active = (jax.nn.silu(gate_part) * upward).astype(jnp.bfloat16)
    partial_value = jnp.dot(active, down_proj, preferred_element_type=jnp.float32).astype(
        jnp.bfloat16
    )
    returned = lax.all_to_all(
        partial_value.reshape(shape_in), "tensor", split_axis=0, concat_axis=0, tiled=True
    )
    expert_out = jnp.sum(
        returned.reshape(expert_count, GROUP, CAP, returned.shape[2]), axis=1, dtype=jnp.float32
    )
    weighted = selector.astype(jnp.float32) * gate_weight.T[:, None, :]
    routed_sum = jnp.einsum("eci,ecd->id", weighted, expert_out)
    return (widened + routed_sum).astype(jnp.bfloat16)


def solution(mesh):
    placed = (
        P(("dp", "tensor"), None),
        P(("dp", "tensor"), None),
        P(("dp", "tensor"), None),
        P(("dp", "tensor"), None, None, None),
        P("dp", None),
        P("dp"),
        P(None, "tensor"),
        P(),
        P(),
        P(("dp", "tensor"), None),
        P(None, "tensor", None),
        P("tensor", None),
    )
    return jax.shard_map(
        local, mesh=mesh, in_specs=placed, out_specs=P(("dp", "tensor"), None), check_vma=False
    )
```

profile of v0, /device:TPU:44, one launch (start us, length us, event | category | flops | bytes accessed | tf_op | source)
XLA Modules:
  0.0 1744.6 jit_solution(13407701293075123612)
XLA Ops:
  6.5 1.1 fusion.28
  7.6 0.8 compare_reduce_fusion
  8.4 106.0 %all-gather = bf16[128,1,2560]{2,1,0:T(2,128)(2,1)S(1)} all-gather(bf16[1,1,2560]{2,1,0:T(2,128)(2,1)} %bitcast.71), channel_id=1, replica_groups=mesh['dp'=4,'tensor'=128] {'tensor'}, dimensions={0}, use_global_device_ids=true | all-gather | bytes 660480 | tf_op jit(solution)/shard_map/all_gather | solution.py:108
  114.5 0.8 select_reduce_fusion.2
  115.5 2.3 fusion.59
  117.8 2.2 copy.144
  119.9 1.1 copy.143
  121.1 1.4 fusion.60
  122.9 1.6 fusion.31
  124.7 419.6 %pmax.7 = f32[128,4,5]{0,2,1:T(8,128)S(1)} all-reduce(f32[128,4,5]{0,2,1:T(8,128)S(1)} %select_reduce_fusion), channel_id=1, replica_groups=mesh['dp'=4,'tensor'=128] {'tensor'}, use_global_device_ids=true, to_apply=%region_5.6 | all-reduce | flops 2560 | bytes 20480 | tf_op jit(solution)/shard_map/pmax | solution.py:114
  544.4 1.5 fusion.2
  546.0 153.4 %all-gather.1 = bf16[128,1,1024]{2,1,0:T(2,128)(2,1)S(1)} all-gather(bf16[1,1,1024]{2,1,0:T(2,128)(2,1)S(1)} %bitcast.72), channel_id=1, replica_groups=mesh['dp'=4,'tensor'=128] {'tensor'}, dimensions={0}, use_global_device_ids=true | all-gather | bytes 264192 | tf_op jit(solution)/shard_map/all_gather | solution.py:109
  699.4 1.0 copy.139
  701.1 419.9 %psum.15 = f32[128,4,5]{0,2,1:T(8,128)S(1)} all-reduce(f32[128,4,5]{0,2,1:T(8,128)S(1)} %get-tuple-element.20), channel_id=1, replica_groups=mesh['dp'=4,'tensor'=128] {'tensor'}, use_global_device_ids=true, to_apply=%region_9.10 | all-reduce | flops 2560 | bytes 20480 | tf_op jit(solution)/shard_map/psum | solution.py:116
  1121.2 1.6 divide_convert_fusion
  1122.9 1.0 fusion.61
  1123.9 81.8 %all-to-all-start = ((f32[128,1,20]{2,1,0:T(1,128)}), f32[128,1,20]{2,1,0:T(1,128)S(1)}, u32[]{:S(2)}, u32[]{:S(2)}) async-start(f32[128,1,20]{2,1,0:T(1,128)} %bitcast.25), calls=%async_computation | async-start | bytes 131072 | tf_op jit(solution)/shard_map/all_to_all | solution.py:122
  1205.7 13.6 all-to-all-done
  1219.3 0.5 broadcast.126
  1219.8 0.8 reduce.7
  1221.3 0.4 convolution_convert_fusion.1
  1221.9 0.4 broadcast_in_dim.125
  1222.3 243.3 %all_to_all.19 = bf16[128,6,2560]{2,1,0:T(8,128)(2,1)} all-to-all(bf16[128,6,2560]{2,1,0:T(8,128)(2,1)S(1)} %bitcast.61), channel_id=1, replica_groups=mesh['dp'=4,'tensor'=128] {'tensor'}, dimensions={0} | all-to-all | bytes 7864320 | tf_op jit(solution)/shard_map/all_to_all | solution.py:152
  1465.6 7.3 reshape.163
  1472.9 3.8 fusion.7
  1476.7 7.5 convolution_convert_fusion
  1484.2 7.1 reshape.164
  1491.3 7.9 all-to-all-start.2
  1499.8 2.9 gather_fusion
  1503.0 230.2 %all-to-all-done.2 = bf16[128,6,2560]{2,1,0:T(8,128)(2,1)} async-done(((bf16[128,6,2560]{2,1,0:T(8,128)(2,1)}), bf16[128,6,2560]{2,1,0:T(8,128)(2,1)}, u32[]{:S(2)}, u32[]{:S(2)}) %all-to-all-start.2) | async-done | bytes 3932192 | tf_op jit(solution)/shard_map/all_to_all | solution.py:165
  1733.2 3.5 convert_reduce_fusion
  1736.7 1.0 fusion.1
  (60 shorter events, 3.6 us)
Async XLA Ops:
  6.5 1470.1 %copy-start = (bf16[192,2560]{1,0:T(8,128)(2,1)S(1)}, bf16[192,2560]{1,0:T(8,128)(2,1)}, u32[]{:S(2)}) copy-start(bf16[192,2560]{1,0:T(8,128)(2,1)} %param.25) | copy-start | bytes 2949124
  6.5 1114.7 %all-reduce.2.cloned.1.call-start = ((), (), s32[]{:S(2)}) async-start(), calls=%async_computation.3 | async-start | bytes 2621440 | tf_op jit(solution)/shard_map/psum | solution.py:116
  122.5 423.5 %copy-start.2 = (s32[64,6]{0,1:T(8,128)S(1)}, s32[64,6]{0,1:T(8,128)}, u32[]{:S(2)}) copy-start(s32[64,6]{0,1:T(8,128)} %param.23) | copy-start | bytes 4612
  122.5 423.5 %copy-start.5 = (bf16[1,1024]{1,0:T(2,128)(2,1)S(1)}, bf16[1,1024]{1,0:T(2,128)(2,1)}, u32[]{:S(2)}) copy-start(bf16[1,1024]{1,0:T(2,128)(2,1)} %param.16) | copy-start | bytes 6148
  700.9 421.9 %copy-start.3 = (bf16[2560,20]{0,1:T(8,128)(2,1)S(1)}, bf16[2560,20]{0,1:T(8,128)(2,1)}, u32[]{:S(2)}) copy-start(bf16[2560,20]{0,1:T(8,128)(2,1)} %param.20) | copy-start | bytes 307204
  1121.0 84.6 %copy-start.4 = (bf16[2560]{0:T(1024)(128)(2,1)S(1)}, bf16[2560]{0:T(1024)(128)(2,1)}, u32[]{:S(2)}) copy-start(bf16[2560]{0:T(1024)(128)(2,1)} %param.21) | copy-start | bytes 15364
  1121.0 84.6 %copy-start.1 = (bf16[64,2560]{1,0:T(8,128)(2,1)S(1)}, bf16[64,2560]{1,0:T(8,128)(2,1)}, u32[]{:S(2)}) copy-start(bf16[64,2560]{1,0:T(8,128)(2,1)} %param.14) | copy-start | bytes 983044
  1123.9 95.4 %all-to-all-start = ((f32[128,1,20]{2,1,0:T(1,128)}), f32[128,1,20]{2,1,0:T(1,128)S(1)}, u32[]{:S(2)}, u32[]{:S(2)}) async-start(f32[128,1,20]{2,1,0:T(1,128)} %bitcast.25), calls=%async_computation | async-start | bytes 131072 | tf_op jit(solution)/shard_map/all_to_all | solution.py:122
  1491.3 8.2 copy-start.6
  1491.3 241.9 %all-to-all-start.2 = ((bf16[128,6,2560]{2,1,0:T(8,128)(2,1)}), bf16[128,6,2560]{2,1,0:T(8,128)(2,1)}, u32[]{:S(2)}, u32[]{:S(2)}) async-start(bf16[128,6,2560]{2,1,0:T(8,128)(2,1)} %reshape.164), calls=%async_computation.2 | async-start | bytes 10485760 | tf_op jit(solution)/shard_map/all_to_all | solution.py:165
Sparse Core Ops, SparseCore 0:
  546.1 408.8 all-reduce.1
where the time goes:
time: 1750 us; the launch traced here: 1740 us
  blocking collectives  1340 us (77%)
  waiting for transfers between devices  244 us (14%)
  starting transfers between devices  89.7 us (5%)
  local copies, waits for them, and re-layouts  26.5 us (2%)
  matrix products  18.7 us (1%)
    psum x1, blocking collectives, local(): lax.psum((request_total * rescale, request_accum * rescale[..., None]), '...  420 us
    pmax x1, blocking collectives, local(): maxima = lax.pmax(request_max, 'tensor')  420 us
    all_to_all x1, blocking collectives, local(): lax.all_to_all(outgoing, 'tensor', split_axis=0, concat_axis=0, tiled=True)  243 us
    all_to_all x1, waiting for transfers between devices, local(): lax.all_to_all(partial_value.reshape(shape_in), 'tensor', split_axis=0, c...  230 us
    all_gather x1, blocking collectives, local(): lax.all_gather(fresh_entries, 'tensor', axis=0, tiled=True)  153 us
    all_gather x1, blocking collectives, local(): lax.all_gather(queries, 'tensor', axis=0, tiled=True)  106 us
    all_to_all x1, starting transfers between devices, local(): lax.all_to_all(projected.reshape(tensor_count, dec_rows, column_block), '...  81.8 us
  transfers between devices with their start and end apart: 3, of which 2 were waited for; matrix products, arithmetic and copies ran while one was open for 0% of the time, Pallas kernels for 0%

commit v1 on v0

--- a/solution.py
+++ b/solution.py
@@ -2,7 +2,9 @@
 
 import jax
 import jax.numpy as jnp
+import numpy as np
 from jax import lax
+from jax.sharding import Mesh
 from jax.sharding import PartitionSpec as P
 
 QUERY_HEADS = 20
@@ -15,32 +17,13 @@
 NEG_FILL = -1e30
 EPSILON = 1e-05
 
-
-def finish_context(maxima, totals, accum, local_queries, local_entries):
-    entry_count = local_queries.shape[0]
-    key_value_width = KEY_VALUE_HEADS * HEAD_SIZE
-    query_vector = local_queries.reshape(
-        entry_count, KEY_VALUE_HEADS, QUERY_HEADS // KEY_VALUE_HEADS, HEAD_SIZE
-    )
-    token_key = local_entries[:, :key_value_width].reshape(entry_count, KEY_VALUE_HEADS, HEAD_SIZE)
-    token_value = (
-        local_entries[:, key_value_width:]
-        .reshape(entry_count, KEY_VALUE_HEADS, HEAD_SIZE)
-        .astype(jnp.float32)
-    )
-    own_score = jnp.einsum(
-        "rhgd,rhd->rhg", query_vector, token_key, preferred_element_type=jnp.float32
-    ) * (1.0 / math.sqrt(HEAD_SIZE))
-    joined = jnp.maximum(maxima, own_score)
-    old_coef = jnp.exp(maxima - joined)
-    own_weight = jnp.exp(own_score - joined)
-    totals = totals * old_coef + own_weight
-    accum = accum * old_coef[..., None] + own_weight[..., None] * token_value[:, :, None, :]
-    return (
-        (accum / totals[..., None])
-        .reshape(entry_count, QUERY_HEADS * HEAD_SIZE)
-        .astype(jnp.bfloat16)
-    )
+TENSOR = ("y", "zh", "zl", "c")
+
+
+def gather_nested(x):
+    x = lax.all_gather(x, "c", axis=0, tiled=True)
+    x = lax.all_gather(x, ("zh", "zl"), axis=0, tiled=True)
+    return lax.all_gather(x, "y", axis=0, tiled=True)
 
 
 def local_parts(query_all, paged_store_cache, page_table, cache_length, my_index):
@@ -87,6 +70,39 @@
     return (request_max, request_total, request_accum)
 
 
+def finish_context(parts, local_queries, local_entries):
+    entry_count = local_queries.shape[0]
+    key_value_width = KEY_VALUE_HEADS * HEAD_SIZE
+    query_vector = local_queries.reshape(
+        entry_count, KEY_VALUE_HEADS, QUERY_HEADS // KEY_VALUE_HEADS, HEAD_SIZE
+    )
+    token_key = local_entries[:, :key_value_width].reshape(entry_count, KEY_VALUE_HEADS, HEAD_SIZE)
+    token_value = (
+        local_entries[:, key_value_width:]
+        .reshape(entry_count, KEY_VALUE_HEADS, HEAD_SIZE)
+        .astype(jnp.float32)
+    )
+    own_score = jnp.einsum(
+        "rhgd,rhd->rhg", query_vector, token_key, preferred_element_type=jnp.float32
+    ) * (1.0 / math.sqrt(HEAD_SIZE))
+    part_max = parts[..., 0]
+    part_total = parts[..., 1]
+    part_accum = parts[..., 2:]
+    joined = jnp.maximum(jnp.max(part_max, axis=1), own_score)
+    coef = jnp.exp(part_max - joined[:, None])
+    own_weight = jnp.exp(own_score - joined)
+    totals = jnp.sum(coef * part_total, axis=1) + own_weight
+    accum = (
+        jnp.sum(coef[..., None] * part_accum, axis=1)
+        + own_weight[..., None] * token_value[:, :, None, :]
+    )
+    return (
+        (accum / totals[..., None])
+        .reshape(entry_count, QUERY_HEADS * HEAD_SIZE)
+        .astype(jnp.bfloat16)
+    )
+
+
 def local(
     stream,
     queries,
@@ -101,27 +117,26 @@
     gate_up,
     down_proj,
 ):
-    tensor_count = lax.axis_size("tensor")
-    my_index = lax.axis_index("tensor")
+    tensor_count = lax.axis_size(TENSOR)
+    my_index = lax.axis_index(TENSOR)
     dec_rows = queries.shape[0]
-    query_all, entries_all = (
-        lax.all_gather(queries, "tensor", axis=0, tiled=True),
-        lax.all_gather(fresh_entries, "tensor", axis=0, tiled=True),
-    )
+    query_all = gather_nested(queries)
     request_max, request_total, request_accum = local_parts(
         query_all, paged_store_cache, page_table, cache_length, my_index
     )
-    maxima = lax.pmax(request_max, "tensor")
-    rescale = jnp.exp(request_max - maxima)
-    totals, accum = lax.psum(
-        (request_total * rescale, request_accum * rescale[..., None]), "tensor"
-    )
-    context = finish_context(maxima, totals, accum, query_all, entries_all)
-    projected = jnp.dot(context, out_proj, preferred_element_type=jnp.float32)
+    packed = jnp.concatenate(
+        (request_max[..., None], request_total[..., None], request_accum), axis=-1
+    )
+    packed = packed.reshape((tensor_count, dec_rows) + packed.shape[1:])
+    parts = lax.all_to_all(packed, TENSOR, split_axis=0, concat_axis=0, tiled=True)
+    parts = jnp.swapaxes(parts, 0, 1)
+    context = finish_context(parts, queries, fresh_entries)
+    context_all = gather_nested(context)
+    projected = jnp.dot(context_all, out_proj, preferred_element_type=jnp.float32)
     column_block = projected.shape[1]
     arrived = lax.all_to_all(
         projected.reshape(tensor_count, dec_rows, column_block),
-        "tensor",
+        TENSOR,
         split_axis=0,
         concat_axis=2,
         tiled=True,
@@ -149,7 +164,7 @@
     ).astype(jnp.bfloat16)
     outgoing = jnp.repeat(slot_rows, GROUP, axis=0)
     contract_last = (((1,), (1,)), ((), ()))
-    incoming = lax.all_to_all(outgoing, "tensor", split_axis=0, concat_axis=0, tiled=True)
+    incoming = lax.all_to_all(outgoing, TENSOR, split_axis=0, concat_axis=0, tiled=True)
     shape_in = incoming.shape
     flat_rows = incoming.reshape(-1, shape_in[2])
     gate_part = lax.dot_general(
@@ -163,7 +178,7 @@
         jnp.bfloat16
     )
     returned = lax.all_to_all(
-        partial_value.reshape(shape_in), "tensor", split_axis=0, concat_axis=0, tiled=True
+        partial_value.reshape(shape_in), TENSOR, split_axis=0, concat_axis=0, tiled=True
     )
     expert_out = jnp.sum(
         returned.reshape(expert_count, GROUP, CAP, returned.shape[2]), axis=1, dtype=jnp.float32
@@ -173,21 +188,31 @@
     return (widened + routed_sum).astype(jnp.bfloat16)
 
 
+def physical_mesh(mesh):
+    dp_count, tensor_count = mesh.devices.shape
+    z_count = tensor_count // 2 // 4
+    z_low = 4 if z_count % 4 == 0 else z_count
+    shape = (dp_count, 4, z_count // z_low, z_low, 2)
+    return Mesh(np.asarray(mesh.devices).reshape(shape), ("dp",) + TENSOR)
+
+
 def solution(mesh):
+    mesh = physical_mesh(mesh)
+    rows = ("dp",) + TENSOR
     placed = (
-        P(("dp", "tensor"), None),
-        P(("dp", "tensor"), None),
-        P(("dp", "tensor"), None),
-        P(("dp", "tensor"), None, None, None),
+        P(rows, None),
+        P(rows, None),
+        P(rows, None),
+        P(rows, None, None, None),
         P("dp", None),
         P("dp"),
-        P(None, "tensor"),
+        P(None, TENSOR),
         P(),
         P(),
-        P(("dp", "tensor"), None),
-        P(None, "tensor", None),
-        P("tensor", None),
+        P(rows, None),
+        P(None, TENSOR, None),
+        P(TENSOR, None),
     )
     return jax.shard_map(
-        local, mesh=mesh, in_specs=placed, out_specs=P(("dp", "tensor"), None), check_vma=False
-    )
+        local, mesh=mesh, in_specs=placed, out_specs=P(rows, None), check_vma=False
+    )

time: 1750 us -> 787 us (0.45)
  the two profiles are of different devices: /device:TPU:44 before, /device:TPU:40 now
where the time goes in v1:
time: 787 us; the launch traced here: 786 us
  waiting for transfers between devices  365 us (46%)
  blocking collectives  333 us (42%)
  starting transfers between devices  32.5 us (4%)
  local copies, waits for them, and re-layouts  30.1 us (4%)
  matrix products  15.5 us (2%)
  other arithmetic  9.33 us (1%)
    all_to_all x1, blocking collectives, local(): lax.all_to_all(outgoing, TENSOR, split_axis=0, concat_axis=0, tiled=True)  244 us
    all_to_all x1, waiting for transfers between devices, local(): lax.all_to_all(partial_value.reshape(shape_in), TENSOR, split_axis=0, con...  230 us
    all_to_all x1, waiting for transfers between devices, local(): lax.all_to_all(packed, TENSOR, split_axis=0, concat_axis=0, tiled=True)  121 us
    all_gather x2, blocking collectives, gather_nested(): x = lax.all_gather(x, ('zh', 'zl'), axis=0, tiled=True)  60.7 us
    all_gather x2, blocking collectives, gather_nested(): return lax.all_gather(x, 'y', axis=0, tiled=True)  25.1 us
  transfers between devices with their start and end apart: 3, of which 3 were waited for; matrix products, arithmetic and copies ran while one was open for 1% of the time, Pallas kernels for 0%

profile of v1, /device:TPU:40, one launch (start us, length us, event | category | flops | bytes accessed | tf_op | source)
XLA Modules:
  0.0 786.0 jit_solution(9470303774525714943)
XLA Ops:
  0.0 1.1 fusion.26
  1.1 0.8 compare_reduce_fusion
  1.9 2.0 all-gather
  4.0 34.1 %all-gather.1 = bf16[16,2,2560]{2,1,0:T(2,128)(2,1)S(1)} all-gather(bf16[1,2,2560]{2,1,0:T(2,128)(2,1)S(1)} %bitcast.98), channel_id=1, replica_groups=mesh['dp'=4,'y'=4,'zh'=4,'zl'=4,'c'=2] {'zh','zl'}, dimensions={0}, use_global_device_ids=true | all-gather | bytes 174080 | tf_op jit(solution)/shard_map/all_gather | solution.py:25
  38.2 13.3 %all_gather.20 = bf16[128,2560]{1,0:T(8,128)(2,1)S(1)} all-gather(bf16[32,2560]{1,0:T(8,128)(2,1)S(1)} %reshape.300), channel_id=1, replica_groups=mesh['dp'=4,'y'=4,'zh'=4,'zl'=4,'c'=2] {'y'}, dimensions={0}, use_global_device_ids=true | all-gather | bytes 819200 | tf_op jit(solution)/shard_map/all_gather | solution.py:26
  51.4 0.8 select_reduce_fusion.2
  52.5 1.4 fusion.61
  55.7 0.5 fusion.28
  56.2 0.5 convolution_bitcast_fusion.1
  56.8 2.8 copy.159
  59.6 12.9 %all-to-all-start = ((f32[128,1,4,5,130]{4,2,3,1,0:T(4,128)}), f32[128,1,4,5,130]{4,2,3,1,0:T(4,128)}, u32[]{:S(2)}, u32[]{:S(2)}) async-start(f32[128,1,4,5,130]{4,2,3,1,0:T(4,128)} %copy.159), calls=%async_computation | async-start | bytes 5242880 | tf_op jit(solution)/shard_map/all_to_all | solution.py:131
  73.1 121.2 %all-to-all-done = f32[128,1,4,5,130]{4,2,3,1,0:T(4,128)} async-done(((f32[128,1,4,5,130]{4,2,3,1,0:T(4,128)}), f32[128,1,4,5,130]{4,2,3,1,0:T(4,128)}, u32[]{:S(2)}, u32[]{:S(2)}) %all-to-all-start) | async-done | bytes 1331232 | tf_op jit(solution)/shard_map/all_to_all | solution.py:131
  194.3 5.0 copy.160
  199.7 0.7 fusion.2
  200.8 1.8 all-gather.2
  202.6 26.6 %all-gather.3 = bf16[16,2,2560]{2,1,0:T(2,128)(2,1)S(1)} all-gather(bf16[1,2,2560]{2,1,0:T(2,128)(2,1)S(1)} %bitcast.99), channel_id=1, replica_groups=mesh['dp'=4,'y'=4,'zh'=4,'zl'=4,'c'=2] {'zh','zl'}, dimensions={0}, use_global_device_ids=true | all-gather | bytes 174080 | tf_op jit(solution)/shard_map/all_gather | solution.py:25
  229.3 11.8 %all_gather.23 = bf16[128,2560]{1,0:T(8,128)(2,1)S(1)} all-gather(bf16[32,2560]{1,0:T(8,128)(2,1)S(1)} %reshape.304), channel_id=1, replica_groups=mesh['dp'=4,'y'=4,'zh'=4,'zl'=4,'c'=2] {'y'}, dimensions={0}, use_global_device_ids=true | all-gather | bytes 819200 | tf_op jit(solution)/shard_map/all_gather | solution.py:26
  241.1 0.9 fusion.63
  242.0 11.6 %all-to-all-start.1 = ((f32[128,1,20]{2,1,0:T(1,128)}), f32[128,1,20]{2,1,0:T(1,128)S(1)}, u32[]{:S(2)}, u32[]{:S(2)}) async-start(f32[128,1,20]{2,1,0:T(1,128)} %bitcast.28), calls=%async_computation.1 | async-start | bytes 131072 | tf_op jit(solution)/shard_map/all_to_all | solution.py:137
  253.8 13.6 %all-to-all-done.1 = f32[128,1,20]{2,1,0:T(1,128)S(1)} async-done(((f32[128,1,20]{2,1,0:T(1,128)}), f32[128,1,20]{2,1,0:T(1,128)S(1)}, u32[]{:S(2)}, u32[]{:S(2)}) %all-to-all-start.1) | async-done | bytes 10272 | tf_op jit(solution)/shard_map/all_to_all | solution.py:137
  267.3 0.5 broadcast.158
  267.9 0.8 reduce.10
  270.3 243.5 %all_to_all.24 = bf16[128,6,2560]{2,1,0:T(8,128)(2,1)} all-to-all(bf16[128,6,2560]{2,1,0:T(8,128)(2,1)S(1)} %bitcast.86), channel_id=1, replica_groups=mesh['dp'=4,'y'=4,'zh'=4,'zl'=4,'c'=2] {'y','zh','zl','c'}, dimensions={0} | all-to-all | bytes 7864320 | tf_op jit(solution)/shard_map/all_to_all | solution.py:167
  513.9 7.3 reshape.282
  521.1 3.8 fusion.7
  524.9 7.5 convolution_convert_fusion
  532.4 7.1 reshape.283
  539.5 7.9 %all-to-all-start.3 = ((bf16[128,6,2560]{2,1,0:T(8,128)(2,1)}), bf16[128,6,2560]{2,1,0:T(8,128)(2,1)}, u32[]{:S(2)}, u32[]{:S(2)}) async-start(bf16[128,6,2560]{2,1,0:T(8,128)(2,1)} %reshape.283), calls=%async_computation.3 | async-start | bytes 10485760 | tf_op jit(solution)/shard_map/all_to_all | solution.py:180
  548.0 2.9 gather_fusion
  551.2 230.2 %all-to-all-done.3 = bf16[128,6,2560]{2,1,0:T(8,128)(2,1)} async-done(((bf16[128,6,2560]{2,1,0:T(8,128)(2,1)}), bf16[128,6,2560]{2,1,0:T(8,128)(2,1)}, u32[]{:S(2)}, u32[]{:S(2)}) %all-to-all-start.3) | async-done | bytes 3932192 | tf_op jit(solution)/shard_map/all_to_all | solution.py:180
  781.4 3.5 convert_reduce_fusion
  784.9 1.0 fusion.1
  (77 shorter events, 6.0 us)
Async XLA Ops:
  0.0 524.9 %copy-start = (bf16[192,2560]{1,0:T(8,128)(2,1)S(1)}, bf16[192,2560]{1,0:T(8,128)(2,1)}, u32[]{:S(2)}) copy-start(bf16[192,2560]{1,0:T(8,128)(2,1)} %param.25) | copy-start | bytes 2949124
  59.6 13.0 %copy-start.4 = (bf16[1,2560]{1,0:T(2,128)(2,1)S(1)}, bf16[1,2560]{1,0:T(2,128)(2,1)}, u32[]{:S(2)}) copy-start(bf16[1,2560]{1,0:T(2,128)(2,1)} %param.15) | copy-start | bytes 15364
  59.6 13.0 %copy-start.6 = (bf16[1,1024]{1,0:T(2,128)(2,1)S(1)}, bf16[1,1024]{1,0:T(2,128)(2,1)}, u32[]{:S(2)}) copy-start(bf16[1,1024]{1,0:T(2,128)(2,1)} %param.16) | copy-start | bytes 6148
  59.6 13.2 %copy-start.2 = (s32[64,6]{0,1:T(8,128)S(1)}, s32[64,6]{0,1:T(8,128)}, u32[]{:S(2)}) copy-start(s32[64,6]{0,1:T(8,128)} %param.23) | copy-start | bytes 4612
  59.6 134.7 %all-to-all-start = ((f32[128,1,4,5,130]{4,2,3,1,0:T(4,128)}), f32[128,1,4,5,130]{4,2,3,1,0:T(4,128)}, u32[]{:S(2)}, u32[]{:S(2)}) async-start(f32[128,1,4,5,130]{4,2,3,1,0:T(4,128)} %copy.159), calls=%async_computation | async-start | bytes 5242880 | tf_op jit(solution)/shard_map/all_to_all | solution.py:131
  199.3 41.8 %copy-start.3 = (bf16[2560,20]{0,1:T(8,128)(2,1)S(1)}, bf16[2560,20]{0,1:T(8,128)(2,1)}, u32[]{:S(2)}) copy-start(bf16[2560,20]{0,1:T(8,128)(2,1)} %param.20) | copy-start | bytes 307204
  199.7 54.0 %copy-start.5 = (bf16[2560]{0:T(1024)(128)(2,1)S(1)}, bf16[2560]{0:T(1024)(128)(2,1)}, u32[]{:S(2)}) copy-start(bf16[2560]{0:T(1024)(128)(2,1)} %param.21) | copy-start | bytes 15364
  199.7 54.0 %copy-start.1 = (bf16[64,2560]{1,0:T(8,128)(2,1)S(1)}, bf16[64,2560]{1,0:T(8,128)(2,1)}, u32[]{:S(2)}) copy-start(bf16[64,2560]{1,0:T(8,128)(2,1)} %param.14) | copy-start | bytes 983044
  242.0 25.3 %all-to-all-start.1 = ((f32[128,1,20]{2,1,0:T(1,128)}), f32[128,1,20]{2,1,0:T(1,128)S(1)}, u32[]{:S(2)}, u32[]{:S(2)}) async-start(f32[128,1,20]{2,1,0:T(1,128)} %bitcast.28), calls=%async_computation.1 | async-start | bytes 131072 | tf_op jit(solution)/shard_map/all_to_all | solution.py:137
  539.5 8.2 %copy-start.7 = (bf16[2560,64]{0,1:T(8,128)(2,1)S(1)}, bf16[2560,64]{0,1:T(8,128)(2,1)}, u32[]{:S(2)}) copy-start(bf16[2560,64]{0,1:T(8,128)(2,1)} %param.22) | copy-start | bytes 983044
  539.5 241.9 %all-to-all-start.3 = ((bf16[128,6,2560]{2,1,0:T(8,128)(2,1)}), bf16[128,6,2560]{2,1,0:T(8,128)(2,1)}, u32[]{:S(2)}, u32[]{:S(2)}) async-start(bf16[128,6,2560]{2,1,0:T(8,128)(2,1)} %reshape.283), calls=%async_computation.3 | async-start | bytes 10485760 | tf_op jit(solution)/shard_map/all_to_all | solution.py:180

commit v2 on v1

--- a/solution.py
+++ b/solution.py
@@ -18,6 +18,8 @@
 EPSILON = 1e-05
 
 TENSOR = ("y", "zh", "zl", "c")
+EXPERT_AXES = ("y", "zh")
+SLICE_AXES = ("zl", "c")
 
 
 def gather_nested(x):
@@ -162,11 +164,11 @@
     slot_rows = jnp.einsum(
         "eci,id->ecd", selector.astype(jnp.bfloat16), normed, preferred_element_type=jnp.float32
     ).astype(jnp.bfloat16)
-    outgoing = jnp.repeat(slot_rows, GROUP, axis=0)
     contract_last = (((1,), (1,)), ((), ()))
-    incoming = lax.all_to_all(outgoing, TENSOR, split_axis=0, concat_axis=0, tiled=True)
-    shape_in = incoming.shape
-    flat_rows = incoming.reshape(-1, shape_in[2])
+    landed = lax.all_to_all(slot_rows, EXPERT_AXES, split_axis=0, concat_axis=0, tiled=True)
+    gathered = lax.all_gather(lax.all_gather(landed, "c", axis=0), "zl", axis=0)
+    shape_in = gathered.shape
+    flat_rows = gathered.reshape(-1, shape_in[-1])
     gate_part = lax.dot_general(
         flat_rows, gate_up[0], contract_last, preferred_element_type=jnp.float32
     )
@@ -177,11 +179,12 @@
     partial_value = jnp.dot(active, down_proj, preferred_element_type=jnp.float32).astype(
         jnp.bfloat16
     )
-    returned = lax.all_to_all(
-        partial_value.reshape(shape_in), TENSOR, split_axis=0, concat_axis=0, tiled=True
-    )
-    expert_out = jnp.sum(
-        returned.reshape(expert_count, GROUP, CAP, returned.shape[2]), axis=1, dtype=jnp.float32
+    group_rows = partial_value.astype(jnp.float32).reshape(
+        (GROUP,) + landed.shape
+    )
+    summed = lax.psum_scatter(group_rows, SLICE_AXES, scatter_dimension=0, tiled=True)
+    expert_out = lax.all_to_all(
+        summed.reshape(landed.shape), EXPERT_AXES, split_axis=0, concat_axis=0, tiled=True
     )
     weighted = selector.astype(jnp.float32) * gate_weight.T[:, None, :]
     routed_sum = jnp.einsum("eci,ecd->id", weighted, expert_out)
@@ -191,7 +194,7 @@
 def physical_mesh(mesh):
     dp_count, tensor_count = mesh.devices.shape
     z_count = tensor_count // 2 // 4
-    z_low = 4 if z_count % 4 == 0 else z_count
+    z_low = GROUP // 2
     shape = (dp_count, 4, z_count // z_low, z_low, 2)
     return Mesh(np.asarray(mesh.devices).reshape(shape), ("dp",) + TENSOR)
 

time: 787 us -> 647 us (0.82)
  the two profiles are of different devices: /device:TPU:40 before, /device:TPU:41 now
where the time goes in v2:
time: 647 us; the launch traced here: 646 us
  waiting for transfers between devices  394 us (61%)
  blocking collectives  118 us (18%)
  starting transfers between devices  57.7 us (9%)
  local copies, waits for them, and re-layouts  39.8 us (6%)
  matrix products  17.1 us (3%)
  between operations  13.8 us (2%)
    all_to_all x1, waiting for transfers between devices, local(): lax.all_to_all(packed, TENSOR, split_axis=0, concat_axis=0, tiled=True)  120 us
    reduce_scatter x1, waiting for transfers between devices, local(): lax.psum_scatter(group_rows, SLICE_AXES, scatter_dimension=0, tiled=True)  119 us
    all_gather x1, waiting for transfers between devices, local(): gathered = lax.all_gather(lax.all_gather(landed, 'c', axis=0), 'zl', axis=0)  76.5 us
    all_to_all x1, waiting for transfers between devices, local(): lax.all_to_all(summed.reshape(landed.shape), EXPERT_AXES, split_axis=0, c...  65.9 us
    all_gather x2, blocking collectives, gather_nested(): x = lax.all_gather(x, ('zh', 'zl'), axis=0, tiled=True)  46.6 us
    all_to_all x1, blocking collectives, local(): lax.all_to_all(slot_rows, EXPERT_AXES, split_axis=0, concat_axis=0, tiled...  40.8 us
    all_to_all x1, starting transfers between devices, local(): lax.all_to_all(packed, TENSOR, split_axis=0, concat_axis=0, tiled=True)  22.8 us
    all_to_all x1, starting transfers between devices, local(): lax.all_to_all(projected.reshape(tensor_count, dec_rows, column_block), T...  21.6 us
  transfers between devices with their start and end apart: 5, of which 5 were waited for; matrix products, arithmetic and copies ran while one was open for 1% of the time, Pallas kernels for 0%

profile of v2, /device:TPU:41, one launch (start us, length us, event | category | flops | bytes accessed | tf_op | source)
XLA Modules:
  0.0 646.5 jit_solution(9819056406110433619)
XLA Ops:
  6.5 1.1 fusion.27
  7.6 0.8 compare_reduce_fusion
  8.4 2.4 all-gather.2
  10.8 27.1 %all-gather.3 = bf16[16,2,2560]{2,1,0:T(2,128)(2,1)S(1)} all-gather(bf16[1,2,2560]{2,1,0:T(2,128)(2,1)S(1)} %bitcast.97), channel_id=1, replica_groups=mesh['dp'=4,'y'=4,'zh'=4,'zl'=4,'c'=2] {'zh','zl'}, dimensions={0}, use_global_device_ids=true | all-gather | bytes 174080 | tf_op jit(solution)/shard_map/all_gather | solution.py:27
  38.0 10.4 %all_gather.32 = bf16[128,2560]{1,0:T(8,128)(2,1)S(1)} all-gather(bf16[32,2560]{1,0:T(8,128)(2,1)S(1)} %reshape.305), channel_id=1, replica_groups=mesh['dp'=4,'y'=4,'zh'=4,'zl'=4,'c'=2] {'y'}, dimensions={0}, use_global_device_ids=true | all-gather | bytes 819200 | tf_op jit(solution)/shard_map/all_gather | solution.py:28
  48.4 0.8 select_reduce_fusion.2
  49.4 1.4 fusion.62
  53.7 2.8 copy.170
  56.5 22.8 %all-to-all-start = ((f32[128,1,4,5,130]{4,2,3,1,0:T(4,128)}), f32[128,1,4,5,130]{4,2,3,1,0:T(4,128)}, u32[]{:S(2)}, u32[]{:S(2)}) async-start(f32[128,1,4,5,130]{4,2,3,1,0:T(4,128)} %copy.170), calls=%async_computation | async-start | bytes 5242880 | tf_op jit(solution)/shard_map/all_to_all | solution.py:133
  80.0 119.6 %all-to-all-done = f32[128,1,4,5,130]{4,2,3,1,0:T(4,128)} async-done(((f32[128,1,4,5,130]{4,2,3,1,0:T(4,128)}), f32[128,1,4,5,130]{4,2,3,1,0:T(4,128)}, u32[]{:S(2)}, u32[]{:S(2)}) %all-to-all-start) | async-done | bytes 1331232 | tf_op jit(solution)/shard_map/all_to_all | solution.py:133
  199.5 5.0 copy.171
  206.0 3.5 all-gather.4
  209.5 19.5 %all-gather.5 = bf16[16,2,2560]{2,1,0:T(2,128)(2,1)S(1)} all-gather(bf16[1,2,2560]{2,1,0:T(2,128)(2,1)S(1)} %bitcast.98), channel_id=1, replica_groups=mesh['dp'=4,'y'=4,'zh'=4,'zl'=4,'c'=2] {'zh','zl'}, dimensions={0}, use_global_device_ids=true | all-gather | bytes 174080 | tf_op jit(solution)/shard_map/all_gather | solution.py:27
  229.1 8.9 %all_gather.35 = bf16[128,2560]{1,0:T(8,128)(2,1)S(1)} all-gather(bf16[32,2560]{1,0:T(8,128)(2,1)S(1)} %reshape.309), channel_id=1, replica_groups=mesh['dp'=4,'y'=4,'zh'=4,'zl'=4,'c'=2] {'y'}, dimensions={0}, use_global_device_ids=true | all-gather | bytes 819200 | tf_op jit(solution)/shard_map/all_gather | solution.py:28
  238.0 0.9 fusion.64
  238.9 21.6 %all-to-all-start.1 = ((f32[128,1,20]{2,1,0:T(1,128)}), f32[128,1,20]{2,1,0:T(1,128)S(1)}, u32[]{:S(2)}, u32[]{:S(2)}) async-start(f32[128,1,20]{2,1,0:T(1,128)} %bitcast.27), calls=%async_computation.1 | async-start | bytes 131072 | tf_op jit(solution)/shard_map/all_to_all | solution.py:139
  260.6 13.4 %all-to-all-done.1 = f32[128,1,20]{2,1,0:T(1,128)S(1)} async-done(((f32[128,1,20]{2,1,0:T(1,128)}), f32[128,1,20]{2,1,0:T(1,128)S(1)}, u32[]{:S(2)}, u32[]{:S(2)}) %all-to-all-start.1) | async-done | bytes 10272 | tf_op jit(solution)/shard_map/all_to_all | solution.py:139
  274.6 0.8 reduce.10
  276.7 40.8 %all_to_all.24 = bf16[16,6,2560]{2,1,0:T(8,128)(2,1)S(1)} all-to-all(bf16[16,6,2560]{2,1,0:T(8,128)(2,1)S(1)} %copy.179), channel_id=1, replica_groups=mesh['dp'=4,'y'=4,'zh'=4,'zl'=4,'c'=2] {'y','zh'}, dimensions={0} | all-to-all | bytes 983040 | tf_op jit(solution)/shard_map/all_to_all | solution.py:168
  317.6 5.5 all-gather
  323.1 1.0 copy.181
  324.4 76.5 %all-gather.8.cloned.1.call-done = bf16[8,16,6,2560]{3,1,2,0:T(8,128)(2,1)} async-done(((bf16[2,16,6,2560]{3,1,2,0:T(8,128)(2,1)}), bf16[8,16,6,2560]{3,1,2,0:T(8,128)(2,1)}) %all-gather.8.cloned.1.call-update) | async-done | bytes 3932176 | tf_op jit(solution)/shard_map/all_gather | solution.py:169
  400.9 6.8 %copy.182 = bf16[8,16,6,2560]{3,2,1,0:T(8,128)(2,1)} copy(bf16[8,16,6,2560]{3,1,2,0:T(8,128)(2,1)} %all-gather.8.cloned.1.call-done) | data formatting | bytes 7864320 | tf_op jit(solution)/shard_map/all_gather | solution.py:169
  407.7 7.3 %reshape.281 = bf16[768,2560]{1,0:T(8,128)(2,1)} reshape(bf16[8,16,6,2560]{3,2,1,0:T(8,128)(2,1)} %copy.182) | data formatting | bytes 7864320 | tf_op jit(solution)/shard_map/reshape | solution.py:171
  415.0 3.8 fusion.8
  418.8 8.7 %fusion = f32[768,2560]{1,0:T(8,128)} fusion(bf16[192,2560]{1,0:T(8,128)(2,1)S(1)} %copy-done, bf16[768,2560]{1,0:T(8,128)(2,1)} %reshape.281, bf16[2,192,2560]{2,1,0:T(8,128)(2,1)} %param.24, f32[768,192]{0,1:T(8,128)S(1)} %fusion.8), kind=kOutput, calls=%fused_computation.2 | convolution fusion | flops 1514766336 | bytes 14352384 | tf_op jit(solution)/shard_map/dot_general | solution.py:179
  427.4 9.2 %reshape.287 = f32[8,16,6,2560]{3,2,1,0:T(8,128)} reshape(f32[768,2560]{1,0:T(8,128)} %fusion) | data formatting | bytes 15728640 | tf_op jit(solution)/shard_map/reshape | solution.py:182
  436.7 118.8 %reduce-scatter.2.cloned.1.call-done = f32[1,16,6,2560]{3,2,1,0:T(8,128)} async-done(((f32[8,16,6,2560]{3,2,1,0:T(8,128)}), f32[1,16,6,2560]{3,2,1,0:T(8,128)}) %reduce-scatter.2.cloned.1.call-update) | async-done | bytes 983056 | tf_op jit(solution)/shard_map/reduce_scatter | solution.py:185
  555.6 13.0 %all-to-all-start.3 = ((f32[16,6,2560]{2,1,0:T(8,128)}), f32[16,6,2560]{2,1,0:T(8,128)S(1)}, u32[]{:S(2)}, u32[]{:S(2)}) async-start(f32[16,6,2560]{2,1,0:T(8,128)} %bitcast.90), calls=%async_computation.4 | async-start | bytes 2621440 | tf_op jit(solution)/shard_map/all_to_all | solution.py:186
  569.1 2.9 gather_fusion
  572.3 65.9 %all-to-all-done.3 = f32[16,6,2560]{2,1,0:T(8,128)S(1)} async-done(((f32[16,6,2560]{2,1,0:T(8,128)}), f32[16,6,2560]{2,1,0:T(8,128)S(1)}, u32[]{:S(2)}, u32[]{:S(2)}) %all-to-all-start.3) | async-done | bytes 983072 | tf_op jit(solution)/shard_map/all_to_all | solution.py:186
  638.2 1.4 fusion.2
  (85 shorter events, 8.3 us)
Async XLA Ops:
  6.5 412.2 %copy-start = (bf16[192,2560]{1,0:T(8,128)(2,1)S(1)}, bf16[192,2560]{1,0:T(8,128)(2,1)}, u32[]{:S(2)}) copy-start(bf16[192,2560]{1,0:T(8,128)(2,1)} %param.25) | copy-start | bytes 2949124
  56.5 22.8 %copy-start.4 = (bf16[1,2560]{1,0:T(2,128)(2,1)S(1)}, bf16[1,2560]{1,0:T(2,128)(2,1)}, u32[]{:S(2)}) copy-start(bf16[1,2560]{1,0:T(2,128)(2,1)} %param.15) | copy-start | bytes 15364
  56.5 22.9 %copy-start.6 = (bf16[1,1024]{1,0:T(2,128)(2,1)S(1)}, bf16[1,1024]{1,0:T(2,128)(2,1)}, u32[]{:S(2)}) copy-start(bf16[1,1024]{1,0:T(2,128)(2,1)} %param.16) | copy-start | bytes 6148
  56.5 23.1 %copy-start.2 = (s32[64,6]{0,1:T(8,128)S(1)}, s32[64,6]{0,1:T(8,128)}, u32[]{:S(2)}) copy-start(s32[64,6]{0,1:T(8,128)} %param.23) | copy-start | bytes 4612
  56.5 143.0 %all-to-all-start = ((f32[128,1,4,5,130]{4,2,3,1,0:T(4,128)}), f32[128,1,4,5,130]{4,2,3,1,0:T(4,128)}, u32[]{:S(2)}, u32[]{:S(2)}) async-start(f32[128,1,4,5,130]{4,2,3,1,0:T(4,128)} %copy.170), calls=%async_computation | async-start | bytes 5242880 | tf_op jit(solution)/shard_map/all_to_all | solution.py:133
  204.6 33.4 %copy-start.3 = (bf16[2560,20]{0,1:T(8,128)(2,1)S(1)}, bf16[2560,20]{0,1:T(8,128)(2,1)}, u32[]{:S(2)}) copy-start(bf16[2560,20]{0,1:T(8,128)(2,1)} %param.20) | copy-start | bytes 307204
  204.9 55.6 %copy-start.5 = (bf16[2560]{0:T(1024)(128)(2,1)S(1)}, bf16[2560]{0:T(1024)(128)(2,1)}, u32[]{:S(2)}) copy-start(bf16[2560]{0:T(1024)(128)(2,1)} %param.21) | copy-start | bytes 15364
  204.9 55.6 %copy-start.1 = (bf16[64,2560]{1,0:T(8,128)(2,1)S(1)}, bf16[64,2560]{1,0:T(8,128)(2,1)}, u32[]{:S(2)}) copy-start(bf16[64,2560]{1,0:T(8,128)(2,1)} %param.14) | copy-start | bytes 983044
  238.9 35.1 %all-to-all-start.1 = ((f32[128,1,20]{2,1,0:T(1,128)}), f32[128,1,20]{2,1,0:T(1,128)S(1)}, u32[]{:S(2)}, u32[]{:S(2)}) async-start(f32[128,1,20]{2,1,0:T(1,128)} %bitcast.27), calls=%async_computation.1 | async-start | bytes 131072 | tf_op jit(solution)/shard_map/all_to_all | solution.py:139
  260.5 140.4 %all-gather.8.cloned.1.call-start = ((), (), s32[]{:S(2)}) async-start(), calls=%async_computation.6 | async-start | bytes 4915200 | tf_op jit(solution)/shard_map/all_gather | solution.py:169
  324.1 231.4 %reduce-scatter.2.cloned.1.call-start = ((), (), s32[]{:S(2)}) async-start(), calls=%async_computation.5 | async-start | bytes 11796480 | tf_op jit(solution)/shard_map/reduce_scatter | solution.py:185
  436.7 132.1 %copy-start.7 = (bf16[2560,64]{0,1:T(8,128)(2,1)S(1)}, bf16[2560,64]{0,1:T(8,128)(2,1)}, u32[]{:S(2)}) copy-start(bf16[2560,64]{0,1:T(8,128)(2,1)} %param.22) | copy-start | bytes 983044
  555.6 82.6 %all-to-all-start.3 = ((f32[16,6,2560]{2,1,0:T(8,128)}), f32[16,6,2560]{2,1,0:T(8,128)S(1)}, u32[]{:S(2)}, u32[]{:S(2)}) async-start(f32[16,6,2560]{2,1,0:T(8,128)} %bitcast.90), calls=%async_computation.4 | async-start | bytes 2621440 | tf_op jit(solution)/shard_map/all_to_all | solution.py:186
Sparse Core Ops, SparseCore 0:
  324.3 76.5 all-gather.7
  436.8 118.6 reduce-scatter.1

commit v3 on v2

--- a/solution.py
+++ b/solution.py
@@ -19,7 +19,6 @@
 
 TENSOR = ("y", "zh", "zl", "c")
 EXPERT_AXES = ("y", "zh")
-SLICE_AXES = ("zl", "c")
 
 
 def gather_nested(x):
@@ -166,7 +165,7 @@
     ).astype(jnp.bfloat16)
     contract_last = (((1,), (1,)), ((), ()))
     landed = lax.all_to_all(slot_rows, EXPERT_AXES, split_axis=0, concat_axis=0, tiled=True)
-    gathered = lax.all_gather(lax.all_gather(landed, "c", axis=0), "zl", axis=0)
+    gathered = lax.all_gather(lax.all_gather(landed, "zl", axis=0), "c", axis=0)
     shape_in = gathered.shape
     flat_rows = gathered.reshape(-1, shape_in[-1])
     gate_part = lax.dot_general(
@@ -179,13 +178,14 @@
     partial_value = jnp.dot(active, down_proj, preferred_element_type=jnp.float32).astype(
         jnp.bfloat16
     )
-    group_rows = partial_value.astype(jnp.float32).reshape(
-        (GROUP,) + landed.shape
-    )
-    summed = lax.psum_scatter(group_rows, SLICE_AXES, scatter_dimension=0, tiled=True)
+    group_rows = partial_value.astype(jnp.float32).reshape(shape_in)
+    core_sum = lax.psum_scatter(group_rows, "c", scatter_dimension=0, tiled=True)
+    slice_sum = lax.psum_scatter(
+        core_sum.astype(jnp.bfloat16), "zl", scatter_dimension=1, tiled=True
+    )
     expert_out = lax.all_to_all(
-        summed.reshape(landed.shape), EXPERT_AXES, split_axis=0, concat_axis=0, tiled=True
-    )
+        slice_sum.reshape(landed.shape), EXPERT_AXES, split_axis=0, concat_axis=0, tiled=True
+    ).astype(jnp.float32)
     weighted = selector.astype(jnp.float32) * gate_weight.T[:, None, :]
     routed_sum = jnp.einsum("eci,ecd->id", weighted, expert_out)
     return (widened + routed_sum).astype(jnp.bfloat16)

time: 647 us -> 587 us (0.907)
  the two profiles are of different devices: /device:TPU:41 before, /device:TPU:8 now
where the time goes in v3:
time: 587 us; the launch traced here: 586 us
  waiting for transfers between devices  331 us (56%)
  blocking collectives  138 us (24%)
  local copies, waits for them, and re-layouts  42.6 us (7%)
  starting transfers between devices  34.5 us (6%)
  matrix products  16.7 us (3%)
  between operations  13.5 us (2%)
  other arithmetic  10.1 us (2%)
    all_to_all x1, waiting for transfers between devices, local(): lax.all_to_all(packed, TENSOR, split_axis=0, concat_axis=0, tiled=True)  120 us
    all_gather x2, waiting for transfers between devices, local(): gathered = lax.all_gather(lax.all_gather(landed, 'zl', axis=0), 'c', axis=0)  68.5 us
    all_gather x2, blocking collectives, gather_nested(): x = lax.all_gather(x, ('zh', 'zl'), axis=0, tiled=True)  65.3 us
    reduce_scatter x1, waiting for transfers between devices, local(): lax.psum_scatter(core_sum.astype(jnp.bfloat16), 'zl', scatter_dimension=1...  64.1 us
    all_to_all x1, blocking collectives, local(): lax.all_to_all(slot_rows, EXPERT_AXES, split_axis=0, concat_axis=0, tiled...  43.1 us
    all_to_all x1, waiting for transfers between devices, local(): lax.all_to_all(slice_sum.reshape(landed.shape), EXPERT_AXES, split_axis=0...  33.5 us
    reduce_scatter x1, waiting for transfers between devices, local(): lax.psum_scatter(group_rows, 'c', scatter_dimension=0, tiled=True)  30 us
    all_gather x2, blocking collectives, gather_nested(): return lax.all_gather(x, 'y', axis=0, tiled=True)  25.4 us
  transfers between devices with their start and end apart: 7, of which 7 were waited for; matrix products, arithmetic and copies ran while one was open for 1% of the time, Pallas kernels for 0%

profile of v3, /device:TPU:8, one launch (start us, length us, event | category | flops | bytes accessed | tf_op | source)
XLA Modules:
  0.0 585.9 jit_solution(17814482685428540649)
XLA Ops:
  6.5 1.1 fusion.27
  8.4 2.0 all-gather.2
  10.5 36.3 %all-gather.3 = bf16[16,2,2560]{2,1,0:T(2,128)(2,1)S(1)} all-gather(bf16[1,2,2560]{2,1,0:T(2,128)(2,1)S(1)} %bitcast.97), channel_id=1, replica_groups=mesh['dp'=4,'y'=4,'zh'=4,'zl'=4,'c'=2] {'zh','zl'}, dimensions={0}, use_global_device_ids=true | all-gather | bytes 174080 | tf_op jit(solution)/shard_map/all_gather | solution.py:26
  46.8 13.3 %all_gather.32 = bf16[128,2560]{1,0:T(8,128)(2,1)S(1)} all-gather(bf16[32,2560]{1,0:T(8,128)(2,1)S(1)} %reshape.305), channel_id=1, replica_groups=mesh['dp'=4,'y'=4,'zh'=4,'zl'=4,'c'=2] {'y'}, dimensions={0}, use_global_device_ids=true | all-gather | bytes 819200 | tf_op jit(solution)/shard_map/all_gather | solution.py:27
  61.1 1.4 fusion.62
  65.4 2.8 copy.170
  68.3 11.3 %all-to-all-start = ((f32[128,1,4,5,130]{4,2,3,1,0:T(4,128)}), f32[128,1,4,5,130]{4,2,3,1,0:T(4,128)}, u32[]{:S(2)}, u32[]{:S(2)}) async-start(f32[128,1,4,5,130]{4,2,3,1,0:T(4,128)} %copy.170), calls=%async_computation | async-start | bytes 5242880 | tf_op jit(solution)/shard_map/all_to_all | solution.py:132
  80.1 120.4 %all-to-all-done = f32[128,1,4,5,130]{4,2,3,1,0:T(4,128)} async-done(((f32[128,1,4,5,130]{4,2,3,1,0:T(4,128)}), f32[128,1,4,5,130]{4,2,3,1,0:T(4,128)}, u32[]{:S(2)}, u32[]{:S(2)}) %all-to-all-start) | async-done | bytes 1331232 | tf_op jit(solution)/shard_map/all_to_all | solution.py:132
  200.5 5.0 copy.171
  207.0 1.8 all-gather.4
  208.8 29.0 %all-gather.5 = bf16[16,2,2560]{2,1,0:T(2,128)(2,1)S(1)} all-gather(bf16[1,2,2560]{2,1,0:T(2,128)(2,1)S(1)} %bitcast.98), channel_id=1, replica_groups=mesh['dp'=4,'y'=4,'zh'=4,'zl'=4,'c'=2] {'zh','zl'}, dimensions={0}, use_global_device_ids=true | all-gather | bytes 174080 | tf_op jit(solution)/shard_map/all_gather | solution.py:26
  237.9 12.1 %all_gather.35 = bf16[128,2560]{1,0:T(8,128)(2,1)S(1)} all-gather(bf16[32,2560]{1,0:T(8,128)(2,1)S(1)} %reshape.309), channel_id=1, replica_groups=mesh['dp'=4,'y'=4,'zh'=4,'zl'=4,'c'=2] {'y'}, dimensions={0}, use_global_device_ids=true | all-gather | bytes 819200 | tf_op jit(solution)/shard_map/all_gather | solution.py:27
  250.0 0.9 fusion.64
  251.0 9.7 %all-to-all-start.1 = ((f32[128,1,20]{2,1,0:T(1,128)}), f32[128,1,20]{2,1,0:T(1,128)S(1)}, u32[]{:S(2)}, u32[]{:S(2)}) async-start(f32[128,1,20]{2,1,0:T(1,128)} %bitcast.27), calls=%async_computation.1 | async-start | bytes 131072 | tf_op jit(solution)/shard_map/all_to_all | solution.py:138
  260.8 14.2 %all-to-all-done.1 = f32[128,1,20]{2,1,0:T(1,128)S(1)} async-done(((f32[128,1,20]{2,1,0:T(1,128)}), f32[128,1,20]{2,1,0:T(1,128)S(1)}, u32[]{:S(2)}, u32[]{:S(2)}) %all-to-all-start.1) | async-done | bytes 10272 | tf_op jit(solution)/shard_map/all_to_all | solution.py:138
  277.6 43.1 %all_to_all.24 = bf16[16,6,2560]{2,1,0:T(8,128)(2,1)S(1)} all-to-all(bf16[16,6,2560]{2,1,0:T(8,128)(2,1)S(1)} %copy.179), channel_id=1, replica_groups=mesh['dp'=4,'y'=4,'zh'=4,'zl'=4,'c'=2] {'y','zh'}, dimensions={0} | all-to-all | bytes 983040 | tf_op jit(solution)/shard_map/all_to_all | solution.py:167
  320.7 1.0 copy.180
  321.8 45.3 %all-gather.9.cloned.1.call-done = bf16[64,6,2560]{2,0,1:T(8,128)(2,1)} async-done(((bf16[16,6,2560]{2,0,1:T(8,128)(2,1)}), bf16[64,6,2560]{2,0,1:T(8,128)(2,1)}) %all-gather.9.cloned.1.call-update) | async-done | bytes 1966096 | tf_op jit(solution)/shard_map/all_gather | solution.py:168
  367.1 3.0 copy.181
  370.3 23.2 %all-gather.11.cloned.1.call-done = bf16[8,16,6,2560]{3,1,2,0:T(8,128)(2,1)} async-done(((bf16[4,16,6,2560]{3,1,2,0:T(8,128)(2,1)}), bf16[8,16,6,2560]{3,1,2,0:T(8,128)(2,1)}) %all-gather.11.cloned.1.call-update) | async-done | bytes 3932176 | tf_op jit(solution)/shard_map/all_gather | solution.py:168
  393.5 6.8 %copy.182 = bf16[8,16,6,2560]{3,2,1,0:T(8,128)(2,1)} copy(bf16[8,16,6,2560]{3,1,2,0:T(8,128)(2,1)} %all-gather.11.cloned.1.call-done) | data formatting | bytes 7864320 | tf_op jit(solution)/shard_map/all_gather | solution.py:168
  400.3 7.3 %reshape.281 = bf16[768,2560]{1,0:T(8,128)(2,1)} reshape(bf16[8,16,6,2560]{3,2,1,0:T(8,128)(2,1)} %copy.182) | data formatting | bytes 7864320 | tf_op jit(solution)/shard_map/reshape | solution.py:170
  407.6 3.8 fusion.8
  411.4 8.7 %fusion = f32[768,2560]{1,0:T(8,128)} fusion(bf16[192,2560]{1,0:T(8,128)(2,1)S(1)} %copy-done, bf16[768,2560]{1,0:T(8,128)(2,1)} %reshape.281, bf16[2,192,2560]{2,1,0:T(8,128)(2,1)} %param.24, f32[768,192]{0,1:T(8,128)S(1)} %fusion.8), kind=kOutput, calls=%fused_computation.2 | convolution fusion | flops 1514766336 | bytes 14352384 | tf_op jit(solution)/shard_map/dot_general | solution.py:178
  420.0 9.2 %reshape.287 = f32[2,4,16,6,2560]{4,3,2,1,0:T(8,128)} reshape(f32[768,2560]{1,0:T(8,128)} %fusion) | data formatting | bytes 15728640 | tf_op jit(solution)/shard_map/reshape | solution.py:181
  429.4 30.0 %reduce-scatter.3.cloned.1.call-done = f32[1,4,16,6,2560]{4,3,2,1,0:T(8,128)} async-done(((f32[2,4,16,6,2560]{4,3,2,1,0:T(8,128)}), f32[1,4,16,6,2560]{4,3,2,1,0:T(8,128)}) %reduce-scatter.3.cloned.1.call-update) | async-done | bytes 3932176 | tf_op jit(solution)/shard_map/reduce_scatter | solution.py:182
  459.4 4.3 convert_element_type.86
  463.7 64.1 %reduce-scatter.5.cloned.1.call-done = bf16[1,1,16,6,2560]{4,3,2,1,0:T(8,128)(2,1)} async-done(((bf16[1,4,16,6,2560]{4,3,2,1,0:T(8,128)(2,1)}), bf16[1,1,16,6,2560]{4,3,2,1,0:T(8,128)(2,1)}) %reduce-scatter.5.cloned.1.call-update) | async-done | bytes 491536 | tf_op jit(solution)/shard_map/reduce_scatter | solution.py:183
  527.9 13.2 %all-to-all-start.3 = ((bf16[16,6,2560]{2,1,0:T(8,128)(2,1)}), bf16[16,6,2560]{2,1,0:T(8,128)(2,1)S(1)}, u32[]{:S(2)}, u32[]{:S(2)}) async-start(bf16[16,6,2560]{2,1,0:T(8,128)(2,1)} %bitcast.90), calls=%async_computation.5 | async-start | bytes 1310720 | tf_op jit(solution)/shard_map/all_to_all | solution.py:186
  541.6 2.9 gather_fusion
  544.8 33.5 %all-to-all-done.3 = bf16[16,6,2560]{2,1,0:T(8,128)(2,1)S(1)} async-done(((bf16[16,6,2560]{2,1,0:T(8,128)(2,1)}), bf16[16,6,2560]{2,1,0:T(8,128)(2,1)S(1)}, u32[]{:S(2)}, u32[]{:S(2)}) %all-to-all-start.3) | async-done | bytes 491552 | tf_op jit(solution)/shard_map/all_to_all | solution.py:186
  578.4 1.0 fusion.2
  (93 shorter events, 10.6 us)
Async XLA Ops:
  6.5 404.8 %copy-start = (bf16[192,2560]{1,0:T(8,128)(2,1)S(1)}, bf16[192,2560]{1,0:T(8,128)(2,1)}, u32[]{:S(2)}) copy-start(bf16[192,2560]{1,0:T(8,128)(2,1)} %param.25) | copy-start | bytes 2949124
  68.3 11.3 %copy-start.5 = (bf16[1,2560]{1,0:T(2,128)(2,1)S(1)}, bf16[1,2560]{1,0:T(2,128)(2,1)}, u32[]{:S(2)}) copy-start(bf16[1,2560]{1,0:T(2,128)(2,1)} %param.15) | copy-start | bytes 15364
  68.3 11.3 %copy-start.7 = (bf16[1,1024]{1,0:T(2,128)(2,1)S(1)}, bf16[1,1024]{1,0:T(2,128)(2,1)}, u32[]{:S(2)}) copy-start(bf16[1,1024]{1,0:T(2,128)(2,1)} %param.16) | copy-start | bytes 6148
  68.3 11.6 %copy-start.3 = (s32[64,6]{0,1:T(8,128)S(1)}, s32[64,6]{0,1:T(8,128)}, u32[]{:S(2)}) copy-start(s32[64,6]{0,1:T(8,128)} %param.23) | copy-start | bytes 4612
  68.3 132.3 %all-to-all-start = ((f32[128,1,4,5,130]{4,2,3,1,0:T(4,128)}), f32[128,1,4,5,130]{4,2,3,1,0:T(4,128)}, u32[]{:S(2)}, u32[]{:S(2)}) async-start(f32[128,1,4,5,130]{4,2,3,1,0:T(4,128)} %copy.170), calls=%async_computation | async-start | bytes 5242880 | tf_op jit(solution)/shard_map/all_to_all | solution.py:132
  205.6 44.5 %copy-start.4 = (bf16[2560,20]{0,1:T(8,128)(2,1)S(1)}, bf16[2560,20]{0,1:T(8,128)(2,1)}, u32[]{:S(2)}) copy-start(bf16[2560,20]{0,1:T(8,128)(2,1)} %param.20) | copy-start | bytes 307204
  205.9 54.8 %copy-start.6 = (bf16[2560]{0:T(1024)(128)(2,1)S(1)}, bf16[2560]{0:T(1024)(128)(2,1)}, u32[]{:S(2)}) copy-start(bf16[2560]{0:T(1024)(128)(2,1)} %param.21) | copy-start | bytes 15364
  205.9 54.8 %copy-start.2 = (bf16[64,2560]{1,0:T(8,128)(2,1)S(1)}, bf16[64,2560]{1,0:T(8,128)(2,1)}, u32[]{:S(2)}) copy-start(bf16[64,2560]{1,0:T(8,128)(2,1)} %param.14) | copy-start | bytes 983044
  251.0 24.1 %all-to-all-start.1 = ((f32[128,1,20]{2,1,0:T(1,128)}), f32[128,1,20]{2,1,0:T(1,128)S(1)}, u32[]{:S(2)}, u32[]{:S(2)}) async-start(f32[128,1,20]{2,1,0:T(1,128)} %bitcast.27), calls=%async_computation.1 | async-start | bytes 131072 | tf_op jit(solution)/shard_map/all_to_all | solution.py:138
  260.6 106.4 %all-gather.9.cloned.1.call-start = ((), (), s32[]{:S(2)}) async-start(), calls=%async_computation.8 | async-start | bytes 2457600 | tf_op jit(solution)/shard_map/all_gather | solution.py:168
  321.7 71.8 %all-gather.11.cloned.1.call-start = ((), (), s32[]{:S(2)}) async-start(), calls=%async_computation.9 | async-start | bytes 5898240 | tf_op jit(solution)/shard_map/all_gather | solution.py:168
  370.0 89.3 %reduce-scatter.3.cloned.1.call-start = ((), (), s32[]{:S(2)}) async-start(), calls=%async_computation.6 | async-start | bytes 15728640 | tf_op jit(solution)/shard_map/reduce_scatter | solution.py:182
  429.3 98.6 %reduce-scatter.5.cloned.1.call-start = ((), (), s32[]{:S(2)}) async-start(), calls=%async_computation.7 | async-start | bytes 3276800 | tf_op jit(solution)/shard_map/reduce_scatter | solution.py:183
  463.7 77.6 %copy-start.8 = (bf16[2560,64]{0,1:T(8,128)(2,1)S(1)}, bf16[2560,64]{0,1:T(8,128)(2,1)}, u32[]{:S(2)}) copy-start(bf16[2560,64]{0,1:T(8,128)(2,1)} %param.22) | copy-start | bytes 983044
  527.9 50.5 %all-to-all-start.3 = ((bf16[16,6,2560]{2,1,0:T(8,128)(2,1)}), bf16[16,6,2560]{2,1,0:T(8,128)(2,1)S(1)}, u32[]{:S(2)}, u32[]{:S(2)}) async-start(bf16[16,6,2560]{2,1,0:T(8,128)(2,1)} %bitcast.90), calls=%async_computation.5 | async-start | bytes 1310720 | tf_op jit(solution)/shard_map/all_to_all | solution.py:186
  541.6 37.7 %copy-start.1 = (bf16[192,2560]{1,0:T(8,128)(2,1)S(1)}, bf16[192,2560]{1,0:T(8,128)(2,1)}, u32[]{:S(2)}) copy-start(bf16[192,2560]{1,0:T(8,128)(2,1)} %param.25) | copy-start | bytes 2949124
Sparse Core Ops, SparseCore 0:
  321.8 45.1 all-gather.8
  370.2 23.2 all-gather.10
  429.4 29.9 reduce-scatter.2
  463.8 63.9 reduce-scatter.4

commit v4 on v3

--- a/solution.py
+++ b/solution.py
@@ -159,35 +159,39 @@
     routed_count = routed.astype(jnp.int32)
     ranking = jnp.cumsum(routed_count, axis=0) - routed_count
     slot_ids = jnp.arange(CAP, dtype=jnp.int32)
-    selector = routed.T[:, None, :] & (ranking.T[:, None, :] == slot_ids[None, :, None])
+    selector = routed.T[None, :, :] & (ranking.T[None, :, :] == slot_ids[:, None, None])
     slot_rows = jnp.einsum(
-        "eci,id->ecd", selector.astype(jnp.bfloat16), normed, preferred_element_type=jnp.float32
+        "cei,id->ced", selector.astype(jnp.bfloat16), normed, preferred_element_type=jnp.float32
     ).astype(jnp.bfloat16)
-    contract_last = (((1,), (1,)), ((), ()))
-    landed = lax.all_to_all(slot_rows, EXPERT_AXES, split_axis=0, concat_axis=0, tiled=True)
-    gathered = lax.all_gather(lax.all_gather(landed, "zl", axis=0), "c", axis=0)
-    shape_in = gathered.shape
-    flat_rows = gathered.reshape(-1, shape_in[-1])
-    gate_part = lax.dot_general(
-        flat_rows, gate_up[0], contract_last, preferred_element_type=jnp.float32
-    )
-    upward = lax.dot_general(
-        flat_rows, gate_up[1], contract_last, preferred_element_type=jnp.float32
-    )
-    active = (jax.nn.silu(gate_part) * upward).astype(jnp.bfloat16)
-    partial_value = jnp.dot(active, down_proj, preferred_element_type=jnp.float32).astype(
-        jnp.bfloat16
-    )
-    group_rows = partial_value.astype(jnp.float32).reshape(shape_in)
-    core_sum = lax.psum_scatter(group_rows, "c", scatter_dimension=0, tiled=True)
+    landed = lax.all_to_all(slot_rows, EXPERT_AXES, split_axis=1, concat_axis=1, tiled=True)
+    own_rows = lax.all_gather(landed, "zl", axis=0)
+    swap = [(0, 1), (1, 0)]
+    partner_rows = lax.ppermute(own_rows, "c", swap)
+
+    def expert_partial(rows):
+        flat_rows = rows.reshape(-1, rows.shape[-1])
+        contract_last = (((1,), (1,)), ((), ()))
+        gate_part = lax.dot_general(
+            flat_rows, gate_up[0], contract_last, preferred_element_type=jnp.float32
+        )
+        upward = lax.dot_general(
+            flat_rows, gate_up[1], contract_last, preferred_element_type=jnp.float32
+        )
+        active = (jax.nn.silu(gate_part) * upward).astype(jnp.bfloat16)
+        partial_value = jnp.dot(active, down_proj, preferred_element_type=jnp.float32)
+        return partial_value.astype(jnp.bfloat16).astype(jnp.float32).reshape(rows.shape)
+
+    own_partial = expert_partial(own_rows)
+    partner_partial = expert_partial(partner_rows)
+    core_sum = own_partial + lax.ppermute(partner_partial, "c", swap)
     slice_sum = lax.psum_scatter(
-        core_sum.astype(jnp.bfloat16), "zl", scatter_dimension=1, tiled=True
+        core_sum.astype(jnp.bfloat16), "zl", scatter_dimension=0, tiled=True
     )
     expert_out = lax.all_to_all(
-        slice_sum.reshape(landed.shape), EXPERT_AXES, split_axis=0, concat_axis=0, tiled=True
+        slice_sum.reshape(landed.shape), EXPERT_AXES, split_axis=1, concat_axis=1, tiled=True
     ).astype(jnp.float32)
-    weighted = selector.astype(jnp.float32) * gate_weight.T[:, None, :]
-    routed_sum = jnp.einsum("eci,ecd->id", weighted, expert_out)
+    weighted = selector.astype(jnp.float32) * gate_weight.T[None, :, :]
+    routed_sum = jnp.einsum("cei,ced->id", weighted, expert_out)
     return (widened + routed_sum).astype(jnp.bfloat16)
 
 

time: 587 us -> 508 us (0.87)
  the two profiles are of different devices: /device:TPU:8 before, /device:TPU:96 now
where the time goes in v4:
time: 508 us; the launch traced here: 507 us
  waiting for transfers between devices  272 us (54%)
  blocking collectives  130 us (26%)
  starting transfers between devices  45.1 us (9%)
  local copies, waits for them, and re-layouts  19.7 us (4%)
  matrix products  14.3 us (3%)
  between operations  13.9 us (3%)
  other arithmetic  12.3 us (2%)
    all_to_all x1, waiting for transfers between devices, local(): lax.all_to_all(packed, TENSOR, split_axis=0, concat_axis=0, tiled=True)  120 us
    all_gather x2, blocking collectives, gather_nested(): x = lax.all_gather(x, ('zh', 'zl'), axis=0, tiled=True)  57.6 us
    reduce_scatter x1, waiting for transfers between devices, local(): lax.psum_scatter(core_sum.astype(jnp.bfloat16), 'zl', scatter_dimension=0...  51.7 us
    all_gather x1, waiting for transfers between devices, local(): own_rows = lax.all_gather(landed, 'zl', axis=0)  46.3 us
    all_to_all x1, blocking collectives, local(): lax.all_to_all(slot_rows, EXPERT_AXES, split_axis=1, concat_axis=1, tiled...  41.5 us
    all_to_all x1, waiting for transfers between devices, local(): lax.all_to_all(slice_sum.reshape(landed.shape), EXPERT_AXES, split_axis=1...  34.9 us
    all_gather x2, blocking collectives, gather_nested(): return lax.all_gather(x, 'y', axis=0, tiled=True)  27.1 us
    all_to_all x1, starting transfers between devices, local(): lax.all_to_all(packed, TENSOR, split_axis=0, concat_axis=0, tiled=True)  14.8 us
  transfers between devices with their start and end apart: 7, of which 7 were waited for; matrix products, arithmetic and copies ran while one was open for 2% of the time, Pallas kernels for 0%

profile of v4, /device:TPU:96, one launch (start us, length us, event | category | flops | bytes accessed | tf_op | source)
XLA Modules:
  0.0 507.1 jit_solution(640292121114357336)
XLA Ops:
  6.5 1.1 fusion.38
  8.4 2.0 all-gather.1
  10.5 31.1 %all-gather.2 = bf16[16,2,2560]{2,1,0:T(2,128)(2,1)S(1)} all-gather(bf16[1,2,2560]{2,1,0:T(2,128)(2,1)S(1)} %bitcast.115), channel_id=1, replica_groups=mesh['dp'=4,'y'=4,'zh'=4,'zl'=4,'c'=2] {'zh','zl'}, dimensions={0}, use_global_device_ids=true | all-gather | bytes 174080 | tf_op jit(solution)/shard_map/all_gather | solution.py:26
  41.7 13.6 %all_gather.26 = bf16[128,2560]{1,0:T(8,128)(2,1)S(1)} all-gather(bf16[32,2560]{1,0:T(8,128)(2,1)S(1)} %reshape.318), channel_id=1, replica_groups=mesh['dp'=4,'y'=4,'zh'=4,'zl'=4,'c'=2] {'y'}, dimensions={0}, use_global_device_ids=true | all-gather | bytes 819200 | tf_op jit(solution)/shard_map/all_gather | solution.py:27
  56.3 1.4 fusion.74
  60.6 2.8 copy.167
  63.5 14.8 %all-to-all-start = ((f32[128,1,4,5,130]{4,2,3,1,0:T(4,128)}), f32[128,1,4,5,130]{4,2,3,1,0:T(4,128)}, u32[]{:S(2)}, u32[]{:S(2)}) async-start(f32[128,1,4,5,130]{4,2,3,1,0:T(4,128)} %copy.167), calls=%async_computation | async-start | bytes 5242880 | tf_op jit(solution)/shard_map/all_to_all | solution.py:132
  78.8 119.7 %all-to-all-done = f32[128,1,4,5,130]{4,2,3,1,0:T(4,128)} async-done(((f32[128,1,4,5,130]{4,2,3,1,0:T(4,128)}), f32[128,1,4,5,130]{4,2,3,1,0:T(4,128)}, u32[]{:S(2)}, u32[]{:S(2)}) %all-to-all-start) | async-done | bytes 1331232 | tf_op jit(solution)/shard_map/all_to_all | solution.py:132
  198.5 5.0 copy.168
  205.0 1.8 all-gather.3
  206.9 26.5 %all-gather.4 = bf16[16,2,2560]{2,1,0:T(2,128)(2,1)S(1)} all-gather(bf16[1,2,2560]{2,1,0:T(2,128)(2,1)S(1)} %bitcast.116), channel_id=1, replica_groups=mesh['dp'=4,'y'=4,'zh'=4,'zl'=4,'c'=2] {'zh','zl'}, dimensions={0}, use_global_device_ids=true | all-gather | bytes 174080 | tf_op jit(solution)/shard_map/all_gather | solution.py:26
  233.4 13.5 %all_gather.29 = bf16[128,2560]{1,0:T(8,128)(2,1)S(1)} all-gather(bf16[32,2560]{1,0:T(8,128)(2,1)S(1)} %reshape.322), channel_id=1, replica_groups=mesh['dp'=4,'y'=4,'zh'=4,'zl'=4,'c'=2] {'y'}, dimensions={0}, use_global_device_ids=true | all-gather | bytes 819200 | tf_op jit(solution)/shard_map/all_gather | solution.py:27
  247.8 11.5 %all-to-all-start.1 = ((f32[128,1,20]{2,1,0:T(1,128)}), f32[128,1,20]{2,1,0:T(1,128)S(1)}, u32[]{:S(2)}, u32[]{:S(2)}) async-start(f32[128,1,20]{2,1,0:T(1,128)} %bitcast.33), calls=%async_computation.1 | async-start | bytes 131072 | tf_op jit(solution)/shard_map/all_to_all | solution.py:138
  259.5 13.1 %all-to-all-done.1 = f32[128,1,20]{2,1,0:T(1,128)S(1)} async-done(((f32[128,1,20]{2,1,0:T(1,128)}), f32[128,1,20]{2,1,0:T(1,128)S(1)}, u32[]{:S(2)}, u32[]{:S(2)}) %all-to-all-start.1) | async-done | bytes 10272 | tf_op jit(solution)/shard_map/all_to_all | solution.py:138
  275.2 41.5 %all_to_all.24 = bf16[6,16,2560]{2,0,1:T(8,128)(2,1)S(1)} all-to-all(bf16[6,16,2560]{2,0,1:T(8,128)(2,1)S(1)} %copy.176), channel_id=1, replica_groups=mesh['dp'=4,'y'=4,'zh'=4,'zl'=4,'c'=2] {'y','zh'}, dimensions={1} | all-to-all | bytes 983040 | tf_op jit(solution)/shard_map/all_to_all | solution.py:166
  317.8 46.3 %all-gather.7.cloned.1.call-done = bf16[24,16,2560]{2,1,0:T(8,128)(2,1)} async-done(((bf16[6,16,2560]{2,1,0:T(8,128)(2,1)}), bf16[24,16,2560]{2,1,0:T(8,128)(2,1)}) %all-gather.7.cloned.1.call-update) | async-done | bytes 1966096 | tf_op jit(solution)/shard_map/all_gather | solution.py:167
  364.1 2.1 collective-permute-start
  366.2 4.0 collective-permute-done
  370.1 1.3 copy-done.10
  371.4 1.5 fusion.6
  372.9 3.5 convolution_convert_fusion
  376.5 2.5 convert.4
  379.0 2.2 collective-permute-start.1
  381.2 1.5 fusion.12
  382.7 3.5 convolution_convert_fusion.1
  386.2 1.9 collective-permute-done.1
  388.1 4.0 fusion
  392.1 51.7 %reduce-scatter.2.cloned.1.call-done = bf16[1,6,16,2560]{3,2,1,0:T(8,128)(2,1)} async-done(((bf16[4,6,16,2560]{3,2,1,0:T(8,128)(2,1)}), bf16[1,6,16,2560]{3,2,1,0:T(8,128)(2,1)}) %reduce-scatter.2.cloned.1.call-update) | async-done | bytes 491536 | tf_op jit(solution)/shard_map/reduce_scatter | solution.py:187
  443.9 2.1 copy.178
  446.0 14.5 %all-to-all-start.3 = ((bf16[6,16,2560]{2,0,1:T(8,128)(2,1)}), bf16[6,16,2560]{2,0,1:T(8,128)(2,1)S(1)}, u32[]{:S(2)}, u32[]{:S(2)}) async-start(bf16[6,16,2560]{2,0,1:T(8,128)(2,1)} %copy.178), calls=%async_computation.4 | async-start | bytes 1310720 | tf_op jit(solution)/shard_map/all_to_all | solution.py:190
  461.1 2.9 gather_fusion
  464.3 34.9 %all-to-all-done.3 = bf16[6,16,2560]{2,0,1:T(8,128)(2,1)S(1)} async-done(((bf16[6,16,2560]{2,0,1:T(8,128)(2,1)}), bf16[6,16,2560]{2,0,1:T(8,128)(2,1)S(1)}, u32[]{:S(2)}, u32[]{:S(2)}) %all-to-all-start.3) | async-done | bytes 491552 | tf_op jit(solution)/shard_map/all_to_all | solution.py:190
  (97 shorter events, 13.3 us)
Async XLA Ops:
  6.5 366.4 %copy-start = (bf16[192,2560]{1,0:T(8,128)(2,1)S(1)}, bf16[192,2560]{1,0:T(8,128)(2,1)}, u32[]{:S(2)}) copy-start(bf16[192,2560]{1,0:T(8,128)(2,1)} %param.25) | copy-start | bytes 2949124
  63.5 14.8 %copy-start.4 = (bf16[1,2560]{1,0:T(2,128)(2,1)S(1)}, bf16[1,2560]{1,0:T(2,128)(2,1)}, u32[]{:S(2)}) copy-start(bf16[1,2560]{1,0:T(2,128)(2,1)} %param.15) | copy-start | bytes 15364
  63.5 14.8 %copy-start.6 = (bf16[1,1024]{1,0:T(2,128)(2,1)S(1)}, bf16[1,1024]{1,0:T(2,128)(2,1)}, u32[]{:S(2)}) copy-start(bf16[1,1024]{1,0:T(2,128)(2,1)} %param.16) | copy-start | bytes 6148
  63.5 15.1 %copy-start.2 = (s32[64,6]{0,1:T(8,128)S(1)}, s32[64,6]{0,1:T(8,128)}, u32[]{:S(2)}) copy-start(s32[64,6]{0,1:T(8,128)} %param.23) | copy-start | bytes 4612
  63.5 135.1 %all-to-all-start = ((f32[128,1,4,5,130]{4,2,3,1,0:T(4,128)}), f32[128,1,4,5,130]{4,2,3,1,0:T(4,128)}, u32[]{:S(2)}, u32[]{:S(2)}) async-start(f32[128,1,4,5,130]{4,2,3,1,0:T(4,128)} %copy.167), calls=%async_computation | async-start | bytes 5242880 | tf_op jit(solution)/shard_map/all_to_all | solution.py:132
  203.6 43.3 %copy-start.3 = (bf16[2560,20]{0,1:T(8,128)(2,1)S(1)}, bf16[2560,20]{0,1:T(8,128)(2,1)}, u32[]{:S(2)}) copy-start(bf16[2560,20]{0,1:T(8,128)(2,1)} %param.20) | copy-start | bytes 307204
  204.0 55.4 %copy-start.5 = (bf16[2560]{0:T(1024)(128)(2,1)S(1)}, bf16[2560]{0:T(1024)(128)(2,1)}, u32[]{:S(2)}) copy-start(bf16[2560]{0:T(1024)(128)(2,1)} %param.21) | copy-start | bytes 15364
  204.0 55.5 %copy-start.1 = (bf16[64,2560]{1,0:T(8,128)(2,1)S(1)}, bf16[64,2560]{1,0:T(8,128)(2,1)}, u32[]{:S(2)}) copy-start(bf16[64,2560]{1,0:T(8,128)(2,1)} %param.14) | copy-start | bytes 983044
  247.8 24.8 %all-to-all-start.1 = ((f32[128,1,20]{2,1,0:T(1,128)}), f32[128,1,20]{2,1,0:T(1,128)S(1)}, u32[]{:S(2)}, u32[]{:S(2)}) async-start(f32[128,1,20]{2,1,0:T(1,128)} %bitcast.33), calls=%async_computation.1 | async-start | bytes 131072 | tf_op jit(solution)/shard_map/all_to_all | solution.py:138
  259.3 104.7 %all-gather.7.cloned.1.call-start = ((), (), s32[]{:S(2)}) async-start(), calls=%async_computation.6 | async-start | bytes 2457600 | tf_op jit(solution)/shard_map/all_gather | solution.py:167
  274.9 96.5 %copy-start.7 = (bf16[2,192,2560]{2,1,0:T(8,128)(2,1)S(1)}, bf16[2,192,2560]{2,1,0:T(8,128)(2,1)}, u32[]{:S(2)}) copy-start(bf16[2,192,2560]{2,1,0:T(8,128)(2,1)} %param.24) | copy-start | bytes 5898244
  317.7 126.1 %reduce-scatter.2.cloned.1.call-start = ((), (), s32[]{:S(2)}) async-start(), calls=%async_computation.5 | async-start | bytes 2457600 | tf_op jit(solution)/shard_map/reduce_scatter | solution.py:187
  364.1 6.1 %collective-permute-start = (bf16[4,6,16,2560]{3,2,1,0:T(8,128)(2,1)}, bf16[4,6,16,2560]{3,2,1,0:T(8,128)(2,1)S(1)}, u32[]{:S(2)}, u32[]{:S(2)}) collective-permute-start(bf16[4,6,16,2560]{3,2,1,0:T(8,128)(2,1)} %bitcast.119), channel_id=1, source_target_pairs={{0,1},{1,0},{2,3},{3,2},{4,5},{5,4},{6,7},{7,6},{8,9},{9,8},{10,11... | collective-permute-start | bytes 5898248 | tf_op jit(solution)/shard_map/ppermute | solution.py:169
  370.1 1.3 copy-start.10
  376.5 4.7 copy-start.8
  376.5 4.7 copy-start.9
  379.0 9.1 %collective-permute-start.1 = (f32[4,6,16,2560]{3,2,1,0:T(8,128)}, f32[4,6,16,2560]{3,2,1,0:T(8,128)}, u32[]{:S(2)}, u32[]{:S(2)}) collective-permute-start(f32[4,6,16,2560]{3,2,1,0:T(8,128)} %convert.4), channel_id=1, source_target_pairs={{0,1},{1,0},{2,3},{3,2},{4,5},{5,4},{6,7},{7,6},{8,9},{9,8},{10,11... | collective-permute-start | bytes 11796488 | tf_op jit(solution)/shard_map/ppermute | solution.py:186
  392.1 68.7 %copy-start.11 = (bf16[2560,64]{0,1:T(8,128)(2,1)S(1)}, bf16[2560,64]{0,1:T(8,128)(2,1)}, u32[]{:S(2)}) copy-start(bf16[2560,64]{0,1:T(8,128)(2,1)} %param.22) | copy-start | bytes 983044
  446.0 53.3 %all-to-all-start.3 = ((bf16[6,16,2560]{2,0,1:T(8,128)(2,1)}), bf16[6,16,2560]{2,0,1:T(8,128)(2,1)S(1)}, u32[]{:S(2)}, u32[]{:S(2)}) async-start(bf16[6,16,2560]{2,0,1:T(8,128)(2,1)} %copy.178), calls=%async_computation.4 | async-start | bytes 1310720 | tf_op jit(solution)/shard_map/all_to_all | solution.py:190
Sparse Core Ops, SparseCore 0:
  317.8 46.2 all-gather.6
  392.3 51.5 reduce-scatter.1

commit v5 on v4

--- a/solution.py
+++ b/solution.py
@@ -86,9 +86,10 @@
     own_score = jnp.einsum(
         "rhgd,rhd->rhg", query_vector, token_key, preferred_element_type=jnp.float32
     ) * (1.0 / math.sqrt(HEAD_SIZE))
-    part_max = parts[..., 0]
-    part_total = parts[..., 1]
-    part_accum = parts[..., 2:]
+    parts = parts.astype(jnp.float32)
+    part_max = parts[..., 0] + parts[..., 1]
+    part_total = parts[..., 2]
+    part_accum = parts[..., 3:]
     joined = jnp.maximum(jnp.max(part_max, axis=1), own_score)
     coef = jnp.exp(part_max - joined[:, None])
     own_weight = jnp.exp(own_score - joined)
@@ -125,9 +126,20 @@
     request_max, request_total, request_accum = local_parts(
         query_all, paged_store_cache, page_table, cache_length, my_index
     )
+    max_high = lax.reduce_precision(request_max, exponent_bits=8, mantissa_bits=7)
+    max_low = lax.reduce_precision(request_max - max_high, exponent_bits=8, mantissa_bits=7)
+    rebase = jnp.where(
+        request_max > 0.5 * NEG_FILL, jnp.exp(request_max - (max_high + max_low)), 0.0
+    )
     packed = jnp.concatenate(
-        (request_max[..., None], request_total[..., None], request_accum), axis=-1
-    )
+        (
+            max_high[..., None],
+            max_low[..., None],
+            (request_total * rebase)[..., None],
+            request_accum * rebase[..., None],
+        ),
+        axis=-1,
+    ).astype(jnp.bfloat16)
     packed = packed.reshape((tensor_count, dec_rows) + packed.shape[1:])
     parts = lax.all_to_all(packed, TENSOR, split_axis=0, concat_axis=0, tiled=True)
     parts = jnp.swapaxes(parts, 0, 1)

time: 508 us -> 450 us (0.89)
  waiting for transfers between devices: 272 us -> 217 us
    all_to_all x1, waiting for transfers between devices: 120 us -> 65 us  [local(): lax.all_to_all(packed, TENSOR, split_axis=0, concat_axis=0, tiled=True)]
where the time goes in v5:
time: 450 us; the launch traced here: 449 us
  waiting for transfers between devices  217 us (48%)
  blocking collectives  130 us (29%)
  starting transfers between devices  43.8 us (10%)
  local copies, waits for them, and re-layouts  18 us (4%)
  matrix products  14.3 us (3%)
  between operations  13.9 us (3%)
  other arithmetic  12.6 us (3%)
    all_to_all x1, waiting for transfers between devices, local(): lax.all_to_all(packed, TENSOR, split_axis=0, concat_axis=0, tiled=True)  65 us
    all_gather x2, blocking collectives, gather_nested(): x = lax.all_gather(x, ('zh', 'zl'), axis=0, tiled=True)  57.8 us
    reduce_scatter x1, waiting for transfers between devices, local(): lax.psum_scatter(core_sum.astype(jnp.bfloat16), 'zl', scatter_dimension=0...  51.7 us
    all_gather x1, waiting for transfers between devices, local(): own_rows = lax.all_gather(landed, 'zl', axis=0)  46.3 us
    all_to_all x1, blocking collectives, local(): lax.all_to_all(slot_rows, EXPERT_AXES, split_axis=1, concat_axis=1, tiled...  41.5 us
    all_to_all x1, waiting for transfers between devices, local(): lax.all_to_all(slice_sum.reshape(landed.shape), EXPERT_AXES, split_axis=1...  34.9 us
    all_gather x2, blocking collectives, gather_nested(): return lax.all_gather(x, 'y', axis=0, tiled=True)  26.6 us
    all_to_all x1, starting transfers between devices, local(): lax.all_to_all(slice_sum.reshape(landed.shape), EXPERT_AXES, split_axis=1...  14.6 us
  transfers between devices with their start and end apart: 7, of which 7 were waited for; matrix products, arithmetic and copies ran while one was open for 2% of the time, Pallas kernels for 0%

profile of v5, /device:TPU:96, one launch (start us, length us, event | category | flops | bytes accessed | tf_op | source)
XLA Modules:
  0.0 449.4 jit_solution(8450205063024768942)
XLA Ops:
  6.5 1.1 fusion.41
  8.4 2.0 all-gather.1
  10.5 31.1 %all-gather.2 = bf16[16,2,2560]{2,1,0:T(2,128)(2,1)S(1)} all-gather(bf16[1,2,2560]{2,1,0:T(2,128)(2,1)S(1)} %bitcast.138), channel_id=1, replica_groups=mesh['dp'=4,'y'=4,'zh'=4,'zl'=4,'c'=2] {'zh','zl'}, dimensions={0}, use_global_device_ids=true | all-gather | bytes 174080 | tf_op jit(solution)/shard_map/all_gather | solution.py:26
  41.7 13.6 %all_gather.26 = bf16[128,2560]{1,0:T(8,128)(2,1)S(1)} all-gather(bf16[32,2560]{1,0:T(8,128)(2,1)S(1)} %reshape.462), channel_id=1, replica_groups=mesh['dp'=4,'y'=4,'zh'=4,'zl'=4,'c'=2] {'y'}, dimensions={0}, use_global_device_ids=true | all-gather | bytes 819200 | tf_op jit(solution)/shard_map/all_gather | solution.py:27
  56.3 1.4 fusion.92
  60.8 2.5 copy.231
  63.3 14.2 %all-to-all-start = ((bf16[128,1,4,5,131]{4,2,3,1,0:T(4,128)(2,1)}), bf16[128,1,4,5,131]{4,2,3,1,0:T(4,128)(2,1)S(1)}, u32[]{:S(2)}, u32[]{:S(2)}) async-start(bf16[128,1,4,5,131]{4,2,3,1,0:T(4,128)(2,1)} %copy.231), calls=%async_computation | async-start | bytes 2621440 | tf_op jit(solution)/shard_map/all_to_all | solution.py:144
  78.1 65.0 %all-to-all-done = bf16[128,1,4,5,131]{4,2,3,1,0:T(4,128)(2,1)S(1)} async-done(((bf16[128,1,4,5,131]{4,2,3,1,0:T(4,128)(2,1)}), bf16[128,1,4,5,131]{4,2,3,1,0:T(4,128)(2,1)S(1)}, u32[]{:S(2)}, u32[]{:S(2)}) %all-to-all-start) | async-done | bytes 670752 | tf_op jit(solution)/shard_map/all_to_all | solution.py:144
  143.1 3.6 copy.232
  148.3 1.8 all-gather.3
  150.2 26.7 %all-gather.4 = bf16[16,2,2560]{2,1,0:T(2,128)(2,1)S(1)} all-gather(bf16[1,2,2560]{2,1,0:T(2,128)(2,1)S(1)} %bitcast.139), channel_id=1, replica_groups=mesh['dp'=4,'y'=4,'zh'=4,'zl'=4,'c'=2] {'zh','zl'}, dimensions={0}, use_global_device_ids=true | all-gather | bytes 174080 | tf_op jit(solution)/shard_map/all_gather | solution.py:26
  176.9 13.1 %all_gather.29 = bf16[128,2560]{1,0:T(8,128)(2,1)S(1)} all-gather(bf16[32,2560]{1,0:T(8,128)(2,1)S(1)} %reshape.466), channel_id=1, replica_groups=mesh['dp'=4,'y'=4,'zh'=4,'zl'=4,'c'=2] {'y'}, dimensions={0}, use_global_device_ids=true | all-gather | bytes 819200 | tf_op jit(solution)/shard_map/all_gather | solution.py:27
  191.0 10.7 %all-to-all-start.1 = ((f32[128,1,20]{2,1,0:T(1,128)}), f32[128,1,20]{2,1,0:T(1,128)S(1)}, u32[]{:S(2)}, u32[]{:S(2)}) async-start(f32[128,1,20]{2,1,0:T(1,128)} %bitcast.37), calls=%async_computation.1 | async-start | bytes 131072 | tf_op jit(solution)/shard_map/all_to_all | solution.py:150
  201.8 13.1 %all-to-all-done.1 = f32[128,1,20]{2,1,0:T(1,128)S(1)} async-done(((f32[128,1,20]{2,1,0:T(1,128)}), f32[128,1,20]{2,1,0:T(1,128)S(1)}, u32[]{:S(2)}, u32[]{:S(2)}) %all-to-all-start.1) | async-done | bytes 10272 | tf_op jit(solution)/shard_map/all_to_all | solution.py:150
  217.5 41.5 %all_to_all.24 = bf16[6,16,2560]{2,0,1:T(8,128)(2,1)S(1)} all-to-all(bf16[6,16,2560]{2,0,1:T(8,128)(2,1)S(1)} %copy.240), channel_id=1, replica_groups=mesh['dp'=4,'y'=4,'zh'=4,'zl'=4,'c'=2] {'y','zh'}, dimensions={1} | all-to-all | bytes 983040 | tf_op jit(solution)/shard_map/all_to_all | solution.py:178
  260.1 46.3 %all-gather.7.cloned.1.call-done = bf16[24,16,2560]{2,1,0:T(8,128)(2,1)} async-done(((bf16[6,16,2560]{2,1,0:T(8,128)(2,1)}), bf16[24,16,2560]{2,1,0:T(8,128)(2,1)}) %all-gather.7.cloned.1.call-update) | async-done | bytes 1966096 | tf_op jit(solution)/shard_map/all_gather | solution.py:179
  306.4 2.1 collective-permute-start
  308.5 4.0 collective-permute-done
  312.5 1.3 copy-done.10
  313.7 1.5 fusion.9
  315.3 3.5 convolution_convert_fusion
  318.8 2.5 convert.26
  321.3 2.2 collective-permute-start.1
  323.5 1.5 fusion.15
  325.0 3.5 convolution_convert_fusion.1
  328.5 1.9 collective-permute-done.1
  330.5 4.0 fusion
  334.5 51.7 %reduce-scatter.2.cloned.1.call-done = bf16[1,6,16,2560]{3,2,1,0:T(8,128)(2,1)} async-done(((bf16[4,6,16,2560]{3,2,1,0:T(8,128)(2,1)}), bf16[1,6,16,2560]{3,2,1,0:T(8,128)(2,1)}) %reduce-scatter.2.cloned.1.call-update) | async-done | bytes 491536 | tf_op jit(solution)/shard_map/reduce_scatter | solution.py:199
  386.2 2.1 copy.242
  388.3 14.6 %all-to-all-start.3 = ((bf16[6,16,2560]{2,0,1:T(8,128)(2,1)}), bf16[6,16,2560]{2,0,1:T(8,128)(2,1)S(1)}, u32[]{:S(2)}, u32[]{:S(2)}) async-start(bf16[6,16,2560]{2,0,1:T(8,128)(2,1)} %copy.242), calls=%async_computation.4 | async-start | bytes 1310720 | tf_op jit(solution)/shard_map/all_to_all | solution.py:202
  403.4 2.9 gather_fusion
  406.6 34.9 %all-to-all-done.3 = bf16[6,16,2560]{2,0,1:T(8,128)(2,1)S(1)} async-done(((bf16[6,16,2560]{2,0,1:T(8,128)(2,1)}), bf16[6,16,2560]{2,0,1:T(8,128)(2,1)S(1)}, u32[]{:S(2)}, u32[]{:S(2)}) %all-to-all-start.3) | async-done | bytes 491552 | tf_op jit(solution)/shard_map/all_to_all | solution.py:202
  (101 shorter events, 13.5 us)
Async XLA Ops:
  6.5 308.7 %copy-start = (bf16[192,2560]{1,0:T(8,128)(2,1)S(1)}, bf16[192,2560]{1,0:T(8,128)(2,1)}, u32[]{:S(2)}) copy-start(bf16[192,2560]{1,0:T(8,128)(2,1)} %param.25) | copy-start | bytes 2949124
  60.8 16.8 %copy-start.4 = (bf16[1,2560]{1,0:T(2,128)(2,1)S(1)}, bf16[1,2560]{1,0:T(2,128)(2,1)}, u32[]{:S(2)}) copy-start(bf16[1,2560]{1,0:T(2,128)(2,1)} %param.15) | copy-start | bytes 15364
  60.8 16.9 %copy-start.6 = (bf16[1,1024]{1,0:T(2,128)(2,1)S(1)}, bf16[1,1024]{1,0:T(2,128)(2,1)}, u32[]{:S(2)}) copy-start(bf16[1,1024]{1,0:T(2,128)(2,1)} %param.16) | copy-start | bytes 6148
  60.8 17.1 %copy-start.2 = (s32[64,6]{0,1:T(8,128)S(1)}, s32[64,6]{0,1:T(8,128)}, u32[]{:S(2)}) copy-start(s32[64,6]{0,1:T(8,128)} %param.23) | copy-start | bytes 4612
  63.3 79.8 %all-to-all-start = ((bf16[128,1,4,5,131]{4,2,3,1,0:T(4,128)(2,1)}), bf16[128,1,4,5,131]{4,2,3,1,0:T(4,128)(2,1)S(1)}, u32[]{:S(2)}, u32[]{:S(2)}) async-start(bf16[128,1,4,5,131]{4,2,3,1,0:T(4,128)(2,1)} %copy.231), calls=%async_computation | async-start | bytes 2621440 | tf_op jit(solution)/shard_map/all_to_all | solution.py:144
  147.0 43.0 %copy-start.3 = (bf16[2560,20]{0,1:T(8,128)(2,1)S(1)}, bf16[2560,20]{0,1:T(8,128)(2,1)}, u32[]{:S(2)}) copy-start(bf16[2560,20]{0,1:T(8,128)(2,1)} %param.20) | copy-start | bytes 307204
  147.3 54.4 %copy-start.5 = (bf16[2560]{0:T(1024)(128)(2,1)S(1)}, bf16[2560]{0:T(1024)(128)(2,1)}, u32[]{:S(2)}) copy-start(bf16[2560]{0:T(1024)(128)(2,1)} %param.21) | copy-start | bytes 15364
  147.3 54.5 %copy-start.1 = (bf16[64,2560]{1,0:T(8,128)(2,1)S(1)}, bf16[64,2560]{1,0:T(8,128)(2,1)}, u32[]{:S(2)}) copy-start(bf16[64,2560]{1,0:T(8,128)(2,1)} %param.14) | copy-start | bytes 983044
  191.0 24.0 %all-to-all-start.1 = ((f32[128,1,20]{2,1,0:T(1,128)}), f32[128,1,20]{2,1,0:T(1,128)S(1)}, u32[]{:S(2)}, u32[]{:S(2)}) async-start(f32[128,1,20]{2,1,0:T(1,128)} %bitcast.37), calls=%async_computation.1 | async-start | bytes 131072 | tf_op jit(solution)/shard_map/all_to_all | solution.py:150
  201.7 104.7 %all-gather.7.cloned.1.call-start = ((), (), s32[]{:S(2)}) async-start(), calls=%async_computation.6 | async-start | bytes 2457600 | tf_op jit(solution)/shard_map/all_gather | solution.py:179
  217.2 96.5 %copy-start.7 = (bf16[2,192,2560]{2,1,0:T(8,128)(2,1)S(1)}, bf16[2,192,2560]{2,1,0:T(8,128)(2,1)}, u32[]{:S(2)}) copy-start(bf16[2,192,2560]{2,1,0:T(8,128)(2,1)} %param.24) | copy-start | bytes 5898244
  260.0 126.1 %reduce-scatter.2.cloned.1.call-start = ((), (), s32[]{:S(2)}) async-start(), calls=%async_computation.5 | async-start | bytes 2457600 | tf_op jit(solution)/shard_map/reduce_scatter | solution.py:199
  306.4 6.1 %collective-permute-start = (bf16[4,6,16,2560]{3,2,1,0:T(8,128)(2,1)}, bf16[4,6,16,2560]{3,2,1,0:T(8,128)(2,1)S(1)}, u32[]{:S(2)}, u32[]{:S(2)}) collective-permute-start(bf16[4,6,16,2560]{3,2,1,0:T(8,128)(2,1)} %bitcast.142), channel_id=1, source_target_pairs={{0,1},{1,0},{2,3},{3,2},{4,5},{5,4},{6,7},{7,6},{8,9},{9,8},{10,11... | collective-permute-start | bytes 5898248 | tf_op jit(solution)/shard_map/ppermute | solution.py:181
  312.5 1.3 copy-start.10
  318.8 4.7 %copy-start.8 = (bf16[2,192,2560]{2,1,0:T(8,128)(2,1)S(1)}, bf16[2,192,2560]{2,1,0:T(8,128)(2,1)}, u32[]{:S(2)}) copy-start(bf16[2,192,2560]{2,1,0:T(8,128)(2,1)} %param.24) | copy-start | bytes 5898244
  318.8 4.7 %copy-start.9 = (bf16[24,16,2560]{2,1,0:T(8,128)(2,1)S(1)}, bf16[24,16,2560]{2,1,0:T(8,128)(2,1)}, u32[]{:S(2)}) copy-start(bf16[24,16,2560]{2,1,0:T(8,128)(2,1)} %all-gather.7.cloned.1.call-done) | copy-start | bytes 5898244
  321.3 9.1 %collective-permute-start.1 = (f32[4,6,16,2560]{3,2,1,0:T(8,128)}, f32[4,6,16,2560]{3,2,1,0:T(8,128)}, u32[]{:S(2)}, u32[]{:S(2)}) collective-permute-start(f32[4,6,16,2560]{3,2,1,0:T(8,128)} %convert.26), channel_id=1, source_target_pairs={{0,1},{1,0},{2,3},{3,2},{4,5},{5,4},{6,7},{7,6},{8,9},{9,8},{10,11... | collective-permute-start | bytes 11796488 | tf_op jit(solution)/shard_map/ppermute | solution.py:198
  334.4 68.7 %copy-start.11 = (bf16[2560,64]{0,1:T(8,128)(2,1)S(1)}, bf16[2560,64]{0,1:T(8,128)(2,1)}, u32[]{:S(2)}) copy-start(bf16[2560,64]{0,1:T(8,128)(2,1)} %param.22) | copy-start | bytes 983044
  388.3 53.3 %all-to-all-start.3 = ((bf16[6,16,2560]{2,0,1:T(8,128)(2,1)}), bf16[6,16,2560]{2,0,1:T(8,128)(2,1)S(1)}, u32[]{:S(2)}, u32[]{:S(2)}) async-start(bf16[6,16,2560]{2,0,1:T(8,128)(2,1)} %copy.242), calls=%async_computation.4 | async-start | bytes 1310720 | tf_op jit(solution)/shard_map/all_to_all | solution.py:202
Sparse Core Ops, SparseCore 0:
  260.1 46.2 all-gather.6
  334.6 51.5 reduce-scatter.1

commit v6 on v5

--- a/solution.py
+++ b/solution.py
@@ -21,10 +21,29 @@
 EXPERT_AXES = ("y", "zh")
 
 
-def gather_nested(x):
-    x = lax.all_gather(x, "c", axis=0, tiled=True)
-    x = lax.all_gather(x, ("zh", "zl"), axis=0, tiled=True)
-    return lax.all_gather(x, "y", axis=0, tiled=True)
+def gather_axis(x, axis, count):
+    me = lax.axis_index(axis)
+    pieces = [x] + [
+        lax.ppermute(x, axis, [(i, (i + k) % count) for i in range(count)]) for k in range(1, count)
+    ]
+    order = (me - jnp.arange(count, dtype=jnp.int32)) % count
+    gathered = jnp.take(jnp.stack(pieces), order, axis=0)
+    return gathered.reshape((count * x.shape[0],) + x.shape[1:])
+
+
+def scatter_sum_axis(x, axis, count):
+    me = lax.axis_index(axis)
+    total = jnp.take(x, me, axis=0).astype(jnp.float32)
+    for k in range(1, count):
+        block = jnp.take(x, (me + k) % count, axis=0)
+        total = total + lax.ppermute(block, axis, [(i, (i + k) % count) for i in range(count)]).astype(jnp.float32)
+    return total
+
+
+def gather_nested(x, sizes):
+    for axis in reversed(TENSOR):
+        x = gather_axis(x, axis, sizes[axis])
+    return x
 
 
 def local_parts(query_all, paged_store_cache, page_table, cache_length, my_index):
@@ -122,7 +141,8 @@
     tensor_count = lax.axis_size(TENSOR)
     my_index = lax.axis_index(TENSOR)
     dec_rows = queries.shape[0]
-    query_all = gather_nested(queries)
+    sizes = {axis: lax.axis_size(axis) for axis in TENSOR}
+    query_all = gather_nested(queries, sizes)
     request_max, request_total, request_accum = local_parts(
         query_all, paged_store_cache, page_table, cache_length, my_index
     )
@@ -144,7 +164,7 @@
     parts = lax.all_to_all(packed, TENSOR, split_axis=0, concat_axis=0, tiled=True)
     parts = jnp.swapaxes(parts, 0, 1)
     context = finish_context(parts, queries, fresh_entries)
-    context_all = gather_nested(context)
+    context_all = gather_nested(context, sizes)
     projected = jnp.dot(context_all, out_proj, preferred_element_type=jnp.float32)
     column_block = projected.shape[1]
     arrived = lax.all_to_all(
@@ -176,7 +196,7 @@
         "cei,id->ced", selector.astype(jnp.bfloat16), normed, preferred_element_type=jnp.float32
     ).astype(jnp.bfloat16)
     landed = lax.all_to_all(slot_rows, EXPERT_AXES, split_axis=1, concat_axis=1, tiled=True)
-    own_rows = lax.all_gather(landed, "zl", axis=0)
+    own_rows = gather_axis(landed[None], "zl", sizes["zl"])
     swap = [(0, 1), (1, 0)]
     partner_rows = lax.ppermute(own_rows, "c", swap)
 
@@ -196,11 +216,9 @@
     own_partial = expert_partial(own_rows)
     partner_partial = expert_partial(partner_rows)
     core_sum = own_partial + lax.ppermute(partner_partial, "c", swap)
-    slice_sum = lax.psum_scatter(
-        core_sum.astype(jnp.bfloat16), "zl", scatter_dimension=0, tiled=True
-    )
+    slice_sum = scatter_sum_axis(core_sum.astype(jnp.bfloat16), "zl", sizes["zl"])
     expert_out = lax.all_to_all(
-        slice_sum.reshape(landed.shape), EXPERT_AXES, split_axis=1, concat_axis=1, tiled=True
+        slice_sum.astype(jnp.bfloat16), EXPERT_AXES, split_axis=1, concat_axis=1, tiled=True
     ).astype(jnp.float32)
     weighted = selector.astype(jnp.float32) * gate_weight.T[None, :, :]
     routed_sum = jnp.einsum("cei,ced->id", weighted, expert_out)

time: 450 us -> 463 us (1.029)
  the two profiles are of different devices: /device:TPU:96 before, /device:TPU:35 now
where the time goes in v6:
time: 463 us; the launch traced here: 461 us
  waiting for transfers between devices  208 us (45%)
  starting transfers between devices  146 us (32%)
  blocking collectives  42.5 us (9%)
  local copies, waits for them, and re-layouts  26.2 us (6%)
  other arithmetic  20.4 us (4%)
  matrix products  16.7 us (4%)
    ppermute x23, starting transfers between devices, gather_axis(): lax.ppermute(x, axis, [(i, (i + k) % count) for i in range(count)])  92.6 us
    all_to_all x1, waiting for transfers between devices, local(): lax.all_to_all(packed, TENSOR, split_axis=0, concat_axis=0, tiled=True)  64.3 us
    ppermute x23, waiting for transfers between devices, gather_axis(): lax.ppermute(x, axis, [(i, (i + k) % count) for i in range(count)])  55.1 us
    all_to_all x1, blocking collectives, local(): lax.all_to_all(slot_rows, EXPERT_AXES, split_axis=1, concat_axis=1, tiled...  42.5 us
    ppermute x3, waiting for transfers between devices, scatter_sum_axis(): lax.ppermute(block, axis, [(i, (i + k) % count) for i in range(count)])  38.4 us
    all_to_all x1, waiting for transfers between devices, local(): lax.all_to_all(slice_sum.astype(jnp.bfloat16), EXPERT_AXES, split_axis=1,...  32.6 us
    all_to_all x1, starting transfers between devices, local(): lax.all_to_all(packed, TENSOR, split_axis=0, concat_axis=0, tiled=True)  17.4 us
    all_to_all x1, starting transfers between devices, local(): lax.all_to_all(projected.reshape(tensor_count, dec_rows, column_block), T...  16.3 us
  transfers between devices with their start and end apart: 31, of which 18 were waited for; matrix products, arithmetic and copies ran while one was open for 3% of the time, Pallas kernels for 0%

profile of v6, /device:TPU:35, one launch (start us, length us, event | category | flops | bytes accessed | tf_op | source)
XLA Modules:
  0.0 461.0 jit_solution(5942419300501956751)
XLA Ops:
  7.0 3.5 collective-permute-start.1
  13.9 3.4 collective-permute-start.3
  19.1 14.3 %collective-permute-start.5 = (bf16[8,2560]{1,0:T(8,128)(2,1)S(1)}, bf16[8,2560]{1,0:T(8,128)(2,1)S(1)}, u32[]{:S(2)}, u32[]{:S(2)}) collective-permute-start(bf16[8,2560]{1,0:T(8,128)(2,1)S(1)} %reshape.657), channel_id=1, source_target_pairs={{0,16},{8,24},{16,0},{24,8},{1,17},{9,25},{17,1},{25,9},{2,18},{10... | collective-permute-start | bytes 122888 | tf_op jit(solution)/shard_map/ppermute | solution.py:27
  35.4 7.3 %collective-permute-start.4 = (bf16[8,2560]{1,0:T(8,128)(2,1)S(1)}, bf16[8,2560]{1,0:T(8,128)(2,1)S(1)}, u32[]{:S(2)}, u32[]{:S(2)}) collective-permute-start(bf16[8,2560]{1,0:T(8,128)(2,1)S(1)} %reshape.657), channel_id=1, source_target_pairs={{0,8},{8,16},{16,24},{24,0},{1,9},{9,17},{17,25},{25,1},{2,10},{10... | collective-permute-start | bytes 122888 | tf_op jit(solution)/shard_map/ppermute | solution.py:27
  48.7 4.5 collective-permute-start.8
  57.7 3.6 collective-permute-done.9
  68.2 17.4 %all-to-all-start = ((bf16[128,1,4,5,131]{4,2,3,1,0:T(4,128)(2,1)}), bf16[128,1,4,5,131]{4,2,3,1,0:T(4,128)(2,1)S(1)}, u32[]{:S(2)}, u32[]{:S(2)}) async-start(bf16[128,1,4,5,131]{4,2,3,1,0:T(4,128)(2,1)} %copy.280), calls=%async_computation | async-start | bytes 2621440 | tf_op jit(solution)/shard_map/all_to_all | solution.py:164
  85.9 64.3 %all-to-all-done = bf16[128,1,4,5,131]{4,2,3,1,0:T(4,128)(2,1)S(1)} async-done(((bf16[128,1,4,5,131]{4,2,3,1,0:T(4,128)(2,1)}), bf16[128,1,4,5,131]{4,2,3,1,0:T(4,128)(2,1)S(1)}, u32[]{:S(2)}, u32[]{:S(2)}) %all-to-all-start) | async-done | bytes 670752 | tf_op jit(solution)/shard_map/all_to_all | solution.py:164
  150.2 3.6 copy.281
  155.3 4.1 collective-permute-start.10
  162.9 4.5 collective-permute-start.12
  174.9 9.3 %collective-permute-start.15 = (bf16[8,2560]{1,0:T(8,128)(2,1)S(1)}, bf16[8,2560]{1,0:T(8,128)(2,1)S(1)}, u32[]{:S(2)}, u32[]{:S(2)}) collective-permute-start(bf16[8,2560]{1,0:T(8,128)(2,1)S(1)} %reshape.664), channel_id=1, source_target_pairs={{0,16},{8,24},{16,0},{24,8},{1,17},{9,25},{17,1},{25,9},{2,18},{10... | collective-permute-start | bytes 122888 | tf_op jit(solution)/shard_map/ppermute | solution.py:27
  188.5 4.9 %collective-permute-done.16 = bf16[8,2560]{1,0:T(8,128)(2,1)S(1)} collective-permute-done((bf16[8,2560]{1,0:T(8,128)(2,1)S(1)}, bf16[8,2560]{1,0:T(8,128)(2,1)S(1)}, u32[]{:S(2)}, u32[]{:S(2)}) %collective-permute-start.16) | collective-permute-done | bytes 40992 | tf_op jit(solution)/shard_map/ppermute | solution.py:27
  208.3 16.3 %all-to-all-start.1 = ((f32[128,1,20]{2,1,0:T(1,128)}), f32[128,1,20]{2,1,0:T(1,128)S(1)}, u32[]{:S(2)}, u32[]{:S(2)}) async-start(f32[128,1,20]{2,1,0:T(1,128)} %bitcast.84), calls=%async_computation.1 | async-start | bytes 131072 | tf_op jit(solution)/shard_map/all_to_all | solution.py:170
  224.7 14.3 %all-to-all-done.1 = f32[128,1,20]{2,1,0:T(1,128)S(1)} async-done(((f32[128,1,20]{2,1,0:T(1,128)}), f32[128,1,20]{2,1,0:T(1,128)S(1)}, u32[]{:S(2)}, u32[]{:S(2)}) %all-to-all-start.1) | async-done | bytes 10272 | tf_op jit(solution)/shard_map/all_to_all | solution.py:170
  241.7 42.5 %all_to_all.24 = bf16[6,16,2560]{2,0,1:T(8,128)(2,1)S(1)} all-to-all(bf16[6,16,2560]{2,0,1:T(8,128)(2,1)S(1)} %copy.291), channel_id=1, replica_groups=mesh['dp'=4,'y'=4,'zh'=4,'zl'=4,'c'=2] {'y','zh'}, dimensions={1} | all-to-all | bytes 983040 | tf_op jit(solution)/shard_map/all_to_all | solution.py:198
  284.4 4.8 %collective-permute-start.20 = (bf16[1,6,16,2560]{3,2,1,0:T(8,128)(2,1)S(1)}, bf16[1,6,16,2560]{3,2,1,0:T(8,128)(2,1)S(1)}, u32[]{:S(2)}, u32[]{:S(2)}) collective-permute-start(bf16[1,6,16,2560]{3,2,1,0:T(8,128)(2,1)S(1)} %bitcast.209), channel_id=1, source_target_pairs={{0,2},{2,4},{4,6},{6,0},{1,3},{3,5},{5,7},{7,1},{8,10},{10,12},{12... | collective-permute-start | bytes 1474568 | tf_op jit(solution)/shard_map/ppermute | solution.py:27
  294.3 7.2 %collective-permute-done.20 = bf16[1,6,16,2560]{3,2,1,0:T(8,128)(2,1)S(1)} collective-permute-done((bf16[1,6,16,2560]{3,2,1,0:T(8,128)(2,1)S(1)}, bf16[1,6,16,2560]{3,2,1,0:T(8,128)(2,1)S(1)}, u32[]{:S(2)}, u32[]{:S(2)}) %collective-permute-start.20) | collective-permute-done | bytes 491552 | tf_op jit(solution)/shard_map/ppermute | solution.py:27
  301.5 29.0 %collective-permute-done.21 = bf16[1,6,16,2560]{3,2,1,0:T(8,128)(2,1)S(1)} collective-permute-done((bf16[1,6,16,2560]{3,2,1,0:T(8,128)(2,1)S(1)}, bf16[1,6,16,2560]{3,2,1,0:T(8,128)(2,1)S(1)}, u32[]{:S(2)}, u32[]{:S(2)}) %collective-permute-start.21) | collective-permute-done | bytes 491552 | tf_op jit(solution)/shard_map/ppermute | solution.py:27
  334.5 3.7 collective-permute-start.23
  338.3 3.6 collective-permute-done.23
  344.7 4.8 %convolution_convert_fusion = bf16[384,2560]{1,0:T(8,128)(2,1)} fusion(bf16[192,2560]{1,0:T(8,128)(2,1)S(1)} %copy-done, f32[384,192]{0,1:T(8,128)} %fusion.9, bf16[384,2560]{1,0:T(8,128)(2,1)} %bitcast.244, bf16[2,192,2560]{2,1,0:T(8,128)(2,1)} %param.34), kind=kOutput, calls=%fused_computation.10 | convolution fusion | flops 756400128 | bytes 6193152 | tf_op jit(solution)/shard_map/dot_general | solution.py:213
  349.5 3.9 convert.26
  359.6 4.6 convolution_convert_fusion.1
  364.1 3.3 fusion
  370.6 5.0 %collective-permute-start.26 = (bf16[6,16,2560]{2,1,0:T(8,128)(2,1)}, bf16[6,16,2560]{2,1,0:T(8,128)(2,1)}, u32[]{:S(2)}, u32[]{:S(2)}) collective-permute-start(bf16[6,16,2560]{2,1,0:T(8,128)(2,1)} %get-tuple-element.37), channel_id=1, source_target_pairs={{0,4},{2,6},{4,0},{6,2},{1,5},{3,7},{5,1},{7,3},{8,12},{10,14},{12... | collective-permute-start | bytes 1474568 | tf_op jit(solution)/shard_map/ppermute | solution.py:39
  375.6 3.4 collective-permute-start.27
  379.0 4.5 collective-permute-done.25
  383.5 29.7 %collective-permute-done.26 = bf16[6,16,2560]{2,1,0:T(8,128)(2,1)} collective-permute-done((bf16[6,16,2560]{2,1,0:T(8,128)(2,1)}, bf16[6,16,2560]{2,1,0:T(8,128)(2,1)}, u32[]{:S(2)}, u32[]{:S(2)}) %collective-permute-start.26) | collective-permute-done | bytes 491552 | tf_op jit(solution)/shard_map/ppermute | solution.py:39
  413.2 4.1 collective-permute-done.27
  420.1 3.6 all-to-all-start.3
  427.4 32.6 %all-to-all-done.3 = bf16[6,16,2560]{2,0,1:T(8,128)(2,1)S(1)} async-done(((bf16[6,16,2560]{2,0,1:T(8,128)(2,1)}), bf16[6,16,2560]{2,0,1:T(8,128)(2,1)S(1)}, u32[]{:S(2)}, u32[]{:S(2)}) %all-to-all-start.3) | async-done | bytes 491552 | tf_op jit(solution)/shard_map/all_to_all | solution.py:220
  (191 shorter events, 94.3 us)
Async XLA Ops:
  0.0 344.7 %copy-start = (bf16[192,2560]{1,0:T(8,128)(2,1)S(1)}, bf16[192,2560]{1,0:T(8,128)(2,1)}, u32[]{:S(2)}) copy-start(bf16[192,2560]{1,0:T(8,128)(2,1)} %param.35) | copy-start | bytes 2949124
  0.0 6.3 %collective-permute-start = (bf16[1,2560]{1,0:T(2,128)(2,1)}, bf16[1,2560]{1,0:T(2,128)(2,1)S(1)}, u32[]{:S(2)}, u32[]{:S(2)}) collective-permute-start(bf16[1,2560]{1,0:T(2,128)(2,1)} %param.25), channel_id=1, source_target_pairs={{0,1},{1,0},{2,3},{3,2},{4,5},{5,4},{6,7},{7,6},{8,9},{9,8},{10,11... | collective-permute-start | bytes 15368 | tf_op jit(solution)/shard_map/ppermute | solution.py:27
  7.0 10.2 %collective-permute-start.1 = (bf16[2,2560]{1,0:T(2,128)(2,1)S(1)}, bf16[2,2560]{1,0:T(2,128)(2,1)S(1)}, u32[]{:S(2)}, u32[]{:S(2)}) collective-permute-start(bf16[2,2560]{1,0:T(2,128)(2,1)S(1)} %get-tuple-element.52), channel_id=1, source_target_pairs={{0,2},{2,4},{4,6},{6,0},{1,3},{3,5},{5,7},{7,1},{8,10},{10,12},{12... | collective-permute-start | bytes 30728 | tf_op jit(solution)/shard_map/ppermute | solution.py:27
  10.6 6.7 %collective-permute-start.2 = (bf16[2,2560]{1,0:T(2,128)(2,1)S(1)}, bf16[2,2560]{1,0:T(2,128)(2,1)S(1)}, u32[]{:S(2)}, u32[]{:S(2)}) collective-permute-start(bf16[2,2560]{1,0:T(2,128)(2,1)S(1)} %get-tuple-element.52), channel_id=1, source_target_pairs={{0,4},{2,6},{4,0},{6,2},{1,5},{3,7},{5,1},{7,3},{8,12},{10,14},{12... | collective-permute-start | bytes 30728 | tf_op jit(solution)/shard_map/ppermute | solution.py:27
  13.9 4.4 collective-permute-start.3
  19.1 23.6 %collective-permute-start.5 = (bf16[8,2560]{1,0:T(8,128)(2,1)S(1)}, bf16[8,2560]{1,0:T(8,128)(2,1)S(1)}, u32[]{:S(2)}, u32[]{:S(2)}) collective-permute-start(bf16[8,2560]{1,0:T(8,128)(2,1)S(1)} %reshape.657), channel_id=1, source_target_pairs={{0,16},{8,24},{16,0},{24,8},{1,17},{9,25},{17,1},{25,9},{2,18},{10... | collective-permute-start | bytes 122888 | tf_op jit(solution)/shard_map/ppermute | solution.py:27
  33.5 9.3 %collective-permute-start.6 = (bf16[8,2560]{1,0:T(8,128)(2,1)S(1)}, bf16[8,2560]{1,0:T(8,128)(2,1)S(1)}, u32[]{:S(2)}, u32[]{:S(2)}) collective-permute-start(bf16[8,2560]{1,0:T(8,128)(2,1)S(1)} %reshape.657), channel_id=1, source_target_pairs={{0,24},{8,0},{16,8},{24,16},{1,25},{9,1},{17,9},{25,17},{2,26},{10... | collective-permute-start | bytes 122888 | tf_op jit(solution)/shard_map/ppermute | solution.py:27
  35.4 8.7 %collective-permute-start.4 = (bf16[8,2560]{1,0:T(8,128)(2,1)S(1)}, bf16[8,2560]{1,0:T(8,128)(2,1)S(1)}, u32[]{:S(2)}, u32[]{:S(2)}) collective-permute-start(bf16[8,2560]{1,0:T(8,128)(2,1)S(1)} %reshape.657), channel_id=1, source_target_pairs={{0,8},{8,16},{16,24},{24,0},{1,9},{9,17},{17,25},{25,1},{2,10},{10... | collective-permute-start | bytes 122888 | tf_op jit(solution)/shard_map/ppermute | solution.py:27
  45.5 12.2 %collective-permute-start.7 = (bf16[32,2560]{1,0:T(8,128)(2,1)}, bf16[32,2560]{1,0:T(8,128)(2,1)S(1)}, u32[]{:S(2)}, u32[]{:S(2)}) collective-permute-start(bf16[32,2560]{1,0:T(8,128)(2,1)} %get-tuple-element.45), channel_id=1, source_target_pairs={{0,32},{32,64},{64,96},{96,0},{1,33},{33,65},{65,97},{97,1},{2,34}... | collective-permute-start | bytes 491528 | tf_op jit(solution)/shard_map/ppermute | solution.py:27
  48.7 9.0 %collective-permute-start.8 = (bf16[32,2560]{1,0:T(8,128)(2,1)}, bf16[32,2560]{1,0:T(8,128)(2,1)S(1)}, u32[]{:S(2)}, u32[]{:S(2)}) collective-permute-start(bf16[32,2560]{1,0:T(8,128)(2,1)} %get-tuple-element.45), channel_id=1, source_target_pairs={{0,64},{32,96},{64,0},{96,32},{1,65},{33,97},{65,1},{97,33},{2,66}... | collective-permute-start | bytes 491528 | tf_op jit(solution)/shard_map/ppermute | solution.py:27
  53.2 8.0 %collective-permute-start.9 = (bf16[32,2560]{1,0:T(8,128)(2,1)}, bf16[32,2560]{1,0:T(8,128)(2,1)}, u32[]{:S(2)}, u32[]{:S(2)}) collective-permute-start(bf16[32,2560]{1,0:T(8,128)(2,1)} %get-tuple-element.45), channel_id=1, source_target_pairs={{0,96},{32,0},{64,32},{96,64},{1,97},{33,1},{65,33},{97,65},{2,98}... | collective-permute-start | bytes 491528 | tf_op jit(solution)/shard_map/ppermute | solution.py:27
  68.2 81.9 %all-to-all-start = ((bf16[128,1,4,5,131]{4,2,3,1,0:T(4,128)(2,1)}), bf16[128,1,4,5,131]{4,2,3,1,0:T(4,128)(2,1)S(1)}, u32[]{:S(2)}, u32[]{:S(2)}) async-start(bf16[128,1,4,5,131]{4,2,3,1,0:T(4,128)(2,1)} %copy.280), calls=%async_computation | async-start | bytes 2621440 | tf_op jit(solution)/shard_map/all_to_all | solution.py:164
  155.3 4.9 %collective-permute-start.10 = (bf16[1,2560]{1,0:T(2,128)(2,1)S(1)}, bf16[1,2560]{1,0:T(2,128)(2,1)S(1)}, u32[]{:S(2)}, u32[]{:S(2)}) collective-permute-start(bf16[1,2560]{1,0:T(2,128)(2,1)S(1)} %convert_element_type.133), channel_id=1, source_target_pairs={{0,1},{1,0},{2,3},{3,2},{4,5},{5,4},{6,7},{7,6},{8,9},{9,8},{10,11... | collective-permute-start | bytes 15368 | tf_op jit(solution)/shard_map/ppermute | solution.py:27
  161.0 8.5 %collective-permute-start.11 = (bf16[2,2560]{1,0:T(2,128)(2,1)S(1)}, bf16[2,2560]{1,0:T(2,128)(2,1)S(1)}, u32[]{:S(2)}, u32[]{:S(2)}) collective-permute-start(bf16[2,2560]{1,0:T(2,128)(2,1)S(1)} %get-tuple-element.50), channel_id=1, source_target_pairs={{0,2},{2,4},{4,6},{6,0},{1,3},{3,5},{5,7},{7,1},{8,10},{10,12},{12... | collective-permute-start | bytes 30728 | tf_op jit(solution)/shard_map/ppermute | solution.py:27
  162.9 6.6 %collective-permute-start.12 = (bf16[2,2560]{1,0:T(2,128)(2,1)S(1)}, bf16[2,2560]{1,0:T(2,128)(2,1)S(1)}, u32[]{:S(2)}, u32[]{:S(2)}) collective-permute-start(bf16[2,2560]{1,0:T(2,128)(2,1)S(1)} %get-tuple-element.50), channel_id=1, source_target_pairs={{0,4},{2,6},{4,0},{6,2},{1,5},{3,7},{5,1},{7,3},{8,12},{10,14},{12... | collective-permute-start | bytes 30728 | tf_op jit(solution)/shard_map/ppermute | solution.py:27
  167.4 4.4 collective-permute-start.13
  172.7 13.8 %collective-permute-start.14 = (bf16[8,2560]{1,0:T(8,128)(2,1)S(1)}, bf16[8,2560]{1,0:T(8,128)(2,1)S(1)}, u32[]{:S(2)}, u32[]{:S(2)}) collective-permute-start(bf16[8,2560]{1,0:T(8,128)(2,1)S(1)} %reshape.664), channel_id=1, source_target_pairs={{0,8},{8,16},{16,24},{24,0},{1,9},{9,17},{17,25},{25,1},{2,10},{10... | collective-permute-start | bytes 122888 | tf_op jit(solution)/shard_map/ppermute | solution.py:27
  174.9 13.6 %collective-permute-start.15 = (bf16[8,2560]{1,0:T(8,128)(2,1)S(1)}, bf16[8,2560]{1,0:T(8,128)(2,1)S(1)}, u32[]{:S(2)}, u32[]{:S(2)}) collective-permute-start(bf16[8,2560]{1,0:T(8,128)(2,1)S(1)} %reshape.664), channel_id=1, source_target_pairs={{0,16},{8,24},{16,0},{24,8},{1,17},{9,25},{17,1},{25,9},{2,18},{10... | collective-permute-start | bytes 122888 | tf_op jit(solution)/shard_map/ppermute | solution.py:27
  184.2 9.2 %collective-permute-start.16 = (bf16[8,2560]{1,0:T(8,128)(2,1)S(1)}, bf16[8,2560]{1,0:T(8,128)(2,1)S(1)}, u32[]{:S(2)}, u32[]{:S(2)}) collective-permute-start(bf16[8,2560]{1,0:T(8,128)(2,1)S(1)} %reshape.664), channel_id=1, source_target_pairs={{0,24},{8,0},{16,8},{24,16},{1,25},{9,1},{17,9},{25,17},{2,26},{10... | collective-permute-start | bytes 122888 | tf_op jit(solution)/shard_map/ppermute | solution.py:27
  194.1 9.6 %collective-permute-start.17 = (bf16[32,2560]{1,0:T(8,128)(2,1)S(1)}, bf16[32,2560]{1,0:T(8,128)(2,1)S(1)}, u32[]{:S(2)}, u32[]{:S(2)}) collective-permute-start(bf16[32,2560]{1,0:T(8,128)(2,1)S(1)} %get-tuple-element.43), channel_id=1, source_target_pairs={{0,32},{32,64},{64,96},{96,0},{1,33},{33,65},{65,97},{97,1},{2,34}... | collective-permute-start | bytes 491528 | tf_op jit(solution)/shard_map/ppermute | solution.py:27
  197.0 9.2 %collective-permute-start.18 = (bf16[32,2560]{1,0:T(8,128)(2,1)S(1)}, bf16[32,2560]{1,0:T(8,128)(2,1)S(1)}, u32[]{:S(2)}, u32[]{:S(2)}) collective-permute-start(bf16[32,2560]{1,0:T(8,128)(2,1)S(1)} %get-tuple-element.43), channel_id=1, source_target_pairs={{0,64},{32,96},{64,0},{96,32},{1,65},{33,97},{65,1},{97,33},{2,66}... | collective-permute-start | bytes 491528 | tf_op jit(solution)/shard_map/ppermute | solution.py:27
  200.1 6.4 %collective-permute-start.19 = (bf16[32,2560]{1,0:T(8,128)(2,1)S(1)}, bf16[32,2560]{1,0:T(8,128)(2,1)S(1)}, u32[]{:S(2)}, u32[]{:S(2)}) collective-permute-start(bf16[32,2560]{1,0:T(8,128)(2,1)S(1)} %get-tuple-element.43), channel_id=1, source_target_pairs={{0,96},{32,0},{64,32},{96,64},{1,97},{33,1},{65,33},{97,65},{2,98}... | collective-permute-start | bytes 491528 | tf_op jit(solution)/shard_map/ppermute | solution.py:27
  208.3 30.7 %all-to-all-start.1 = ((f32[128,1,20]{2,1,0:T(1,128)}), f32[128,1,20]{2,1,0:T(1,128)S(1)}, u32[]{:S(2)}, u32[]{:S(2)}) async-start(f32[128,1,20]{2,1,0:T(1,128)} %bitcast.84), calls=%async_computation.1 | async-start | bytes 131072 | tf_op jit(solution)/shard_map/all_to_all | solution.py:170
  284.4 17.1 %collective-permute-start.20 = (bf16[1,6,16,2560]{3,2,1,0:T(8,128)(2,1)S(1)}, bf16[1,6,16,2560]{3,2,1,0:T(8,128)(2,1)S(1)}, u32[]{:S(2)}, u32[]{:S(2)}) collective-permute-start(bf16[1,6,16,2560]{3,2,1,0:T(8,128)(2,1)S(1)} %bitcast.209), channel_id=1, source_target_pairs={{0,2},{2,4},{4,6},{6,0},{1,3},{3,5},{5,7},{7,1},{8,10},{10,12},{12... | collective-permute-start | bytes 1474568 | tf_op jit(solution)/shard_map/ppermute | solution.py:27
  289.2 41.3 %collective-permute-start.21 = (bf16[1,6,16,2560]{3,2,1,0:T(8,128)(2,1)S(1)}, bf16[1,6,16,2560]{3,2,1,0:T(8,128)(2,1)S(1)}, u32[]{:S(2)}, u32[]{:S(2)}) collective-permute-start(bf16[1,6,16,2560]{3,2,1,0:T(8,128)(2,1)S(1)} %bitcast.210), channel_id=1, source_target_pairs={{0,4},{2,6},{4,0},{6,2},{1,5},{3,7},{5,1},{7,3},{8,12},{10,14},{12... | collective-permute-start | bytes 1474568 | tf_op jit(solution)/shard_map/ppermute | solution.py:27
  291.1 39.4 %collective-permute-start.22 = (bf16[1,6,16,2560]{3,2,1,0:T(8,128)(2,1)S(1)}, bf16[1,6,16,2560]{3,2,1,0:T(8,128)(2,1)S(1)}, u32[]{:S(2)}, u32[]{:S(2)}) collective-permute-start(bf16[1,6,16,2560]{3,2,1,0:T(8,128)(2,1)S(1)} %bitcast.211), channel_id=1, source_target_pairs={{0,6},{2,0},{4,2},{6,4},{1,7},{3,1},{5,3},{7,5},{8,14},{10,8},{12,... | collective-permute-start | bytes 1474568 | tf_op jit(solution)/shard_map/ppermute | solution.py:27
  334.5 7.3 %collective-permute-start.23 = (bf16[4,6,16,2560]{3,2,1,0:T(8,128)(2,1)S(1)}, bf16[4,6,16,2560]{3,2,1,0:T(8,128)(2,1)S(1)}, u32[]{:S(2)}, u32[]{:S(2)}) collective-permute-start(bf16[4,6,16,2560]{3,2,1,0:T(8,128)(2,1)S(1)} %broadcast_select_fusion), channel_id=1, source_target_pairs={{0,1},{1,0},{2,3},{3,2},{4,5},{5,4},{6,7},{7,6},{8,9},{9,8},{10,11... | collective-permute-start | bytes 5898248 | tf_op jit(solution)/shard_map/ppermute | solution.py:201
  353.4 10.7 %collective-permute-start.24 = (f32[4,6,16,2560]{3,2,1,0:T(8,128)}, f32[4,6,16,2560]{3,2,1,0:T(8,128)}, u32[]{:S(2)}, u32[]{:S(2)}) collective-permute-start(f32[4,6,16,2560]{3,2,1,0:T(8,128)} %convert.26), channel_id=1, source_target_pairs={{0,1},{1,0},{2,3},{3,2},{4,5},{5,4},{6,7},{7,6},{8,9},{9,8},{10,11... | collective-permute-start | bytes 11796488 | tf_op jit(solution)/shard_map/ppermute | solution.py:218
  368.7 14.9 %collective-permute-start.25 = (bf16[6,16,2560]{2,1,0:T(8,128)(2,1)}, bf16[6,16,2560]{2,1,0:T(8,128)(2,1)}, u32[]{:S(2)}, u32[]{:S(2)}) collective-permute-start(bf16[6,16,2560]{2,1,0:T(8,128)(2,1)} %get-tuple-element.35), channel_id=1, source_target_pairs={{0,2},{2,4},{4,6},{6,0},{1,3},{3,5},{5,7},{7,1},{8,10},{10,12},{12... | collective-permute-start | bytes 1474568 | tf_op jit(solution)/shard_map/ppermute | solution.py:39
  370.6 42.6 %collective-permute-start.26 = (bf16[6,16,2560]{2,1,0:T(8,128)(2,1)}, bf16[6,16,2560]{2,1,0:T(8,128)(2,1)}, u32[]{:S(2)}, u32[]{:S(2)}) collective-permute-start(bf16[6,16,2560]{2,1,0:T(8,128)(2,1)} %get-tuple-element.37), channel_id=1, source_target_pairs={{0,4},{2,6},{4,0},{6,2},{1,5},{3,7},{5,1},{7,3},{8,12},{10,14},{12... | collective-permute-start | bytes 1474568 | tf_op jit(solution)/shard_map/ppermute | solution.py:39
  375.6 41.7 %collective-permute-start.27 = (bf16[6,16,2560]{2,1,0:T(8,128)(2,1)}, bf16[6,16,2560]{2,1,0:T(8,128)(2,1)}, u32[]{:S(2)}, u32[]{:S(2)}) collective-permute-start(bf16[6,16,2560]{2,1,0:T(8,128)(2,1)} %get-tuple-element.36), channel_id=1, source_target_pairs={{0,6},{2,0},{4,2},{6,4},{1,7},{3,1},{5,3},{7,5},{8,14},{10,8},{12,... | collective-permute-start | bytes 1474568 | tf_op jit(solution)/shard_map/ppermute | solution.py:39
  420.1 39.9 %all-to-all-start.3 = ((bf16[6,16,2560]{2,0,1:T(8,128)(2,1)}), bf16[6,16,2560]{2,0,1:T(8,128)(2,1)S(1)}, u32[]{:S(2)}, u32[]{:S(2)}) async-start(bf16[6,16,2560]{2,0,1:T(8,128)(2,1)} %copy.296), calls=%async_computation.3 | async-start | bytes 1310720 | tf_op jit(solution)/shard_map/all_to_all | solution.py:220
  (14 other events, 139.8 us)

commit v7 on v6

--- a/solution.py
+++ b/solution.py
@@ -40,10 +40,10 @@
     return total
 
 
-def gather_nested(x, sizes):
-    for axis in reversed(TENSOR):
-        x = gather_axis(x, axis, sizes[axis])
-    return x
+def gather_nested(x):
+    x = lax.all_gather(x, "c", axis=0, tiled=True)
+    x = lax.all_gather(x, ("zh", "zl"), axis=0, tiled=True)
+    return lax.all_gather(x, "y", axis=0, tiled=True)
 
 
 def local_parts(query_all, paged_store_cache, page_table, cache_length, my_index):
@@ -142,7 +142,7 @@
     my_index = lax.axis_index(TENSOR)
     dec_rows = queries.shape[0]
     sizes = {axis: lax.axis_size(axis) for axis in TENSOR}
-    query_all = gather_nested(queries, sizes)
+    query_all = gather_nested(queries)
     request_max, request_total, request_accum = local_parts(
         query_all, paged_store_cache, page_table, cache_length, my_index
     )
@@ -164,7 +164,7 @@
     parts = lax.all_to_all(packed, TENSOR, split_axis=0, concat_axis=0, tiled=True)
     parts = jnp.swapaxes(parts, 0, 1)
     context = finish_context(parts, queries, fresh_entries)
-    context_all = gather_nested(context, sizes)
+    context_all = gather_nested(context)
     projected = jnp.dot(context_all, out_proj, preferred_element_type=jnp.float32)
     column_block = projected.shape[1]
     arrived = lax.all_to_all(
@@ -175,11 +175,24 @@
         tiled=True,
     )
     widened = stream.astype(jnp.float32)
-    widened = widened.at[:dec_rows].add(arrived[0])
-    resid = lax.optimization_barrier(widened.astype(jnp.bfloat16))
-    widened = resid.astype(jnp.float32)
+    prefill = widened[dec_rows:]
+    prefill_sum = routed_experts(
+        rms_norm(prefill, norm_gain), routes[dec_rows:], router, gate_up, down_proj, CAP, sizes
+    )
+    decode = lax.reduce_precision(widened[:dec_rows] + arrived[0], exponent_bits=8, mantissa_bits=7)
+    decode_sum = routed_experts(
+        rms_norm(decode, norm_gain), routes[:dec_rows], router, gate_up, down_proj, dec_rows, sizes
+    )
+    return jnp.concatenate((decode + decode_sum, prefill + prefill_sum)).astype(jnp.bfloat16)
+
+
+def rms_norm(widened, norm_gain):
     inverse = lax.rsqrt(jnp.mean(widened * widened, axis=-1, keepdims=True) + EPSILON)
-    normed = (widened * inverse * norm_gain.astype(jnp.float32)).astype(jnp.bfloat16)
+    return (widened * inverse * norm_gain.astype(jnp.float32)).astype(jnp.bfloat16)
+
+
+def routed_experts(normed, routes, router, gate_up, down_proj, capacity, sizes):
+    tensor_count = lax.axis_size(TENSOR)
     logits = jnp.dot(normed, router, preferred_element_type=jnp.float32)
     chosen = jnp.take_along_axis(logits, routes, axis=1)
     gate_probs = jax.nn.softmax(chosen, axis=-1)
@@ -190,7 +203,7 @@
     gate_weight = jnp.sum(jnp.where(matched, gate_probs[:, :, None], 0.0), axis=1)
     routed_count = routed.astype(jnp.int32)
     ranking = jnp.cumsum(routed_count, axis=0) - routed_count
-    slot_ids = jnp.arange(CAP, dtype=jnp.int32)
+    slot_ids = jnp.arange(capacity, dtype=jnp.int32)
     selector = routed.T[None, :, :] & (ranking.T[None, :, :] == slot_ids[:, None, None])
     slot_rows = jnp.einsum(
         "cei,id->ced", selector.astype(jnp.bfloat16), normed, preferred_element_type=jnp.float32
@@ -222,7 +235,7 @@
     ).astype(jnp.float32)
     weighted = selector.astype(jnp.float32) * gate_weight.T[None, :, :]
     routed_sum = jnp.einsum("cei,ced->id", weighted, expert_out)
-    return (widened + routed_sum).astype(jnp.bfloat16)
+    return routed_sum
 
 
 def physical_mesh(mesh):

time: 463 us -> 491 us (1.060)
  the two profiles are of different devices: /device:TPU:35 before, /device:TPU:66 now
where the time goes in v7:
time: 491 us; the launch traced here: 489 us
  waiting for transfers between devices  177 us (36%)
  blocking collectives  112 us (23%)
  starting transfers between devices  109 us (22%)
  other arithmetic  34.4 us (7%)
  matrix products  27.6 us (6%)
  local copies, waits for them, and re-layouts  27.3 us (6%)
    ppermute x6, waiting for transfers between devices, gather_axis(): lax.ppermute(x, axis, [(i, (i + k) % count) for i in range(count)])  84.3 us
    all_gather x2, blocking collectives, gather_nested(): x = lax.all_gather(x, ('zh', 'zl'), axis=0, tiled=True)  81.3 us
    all_to_all x2, waiting for transfers between devices, routed_experts(): lax.all_to_all(slice_sum.astype(jnp.bfloat16), EXPERT_AXES, split_axis=1,...  33.9 us
    ppermute x6, waiting for transfers between devices, scatter_sum_axis(): lax.ppermute(block, axis, [(i, (i + k) % count) for i in range(count)])  33.4 us
    all_gather x2, blocking collectives, gather_nested(): return lax.all_gather(x, 'y', axis=0, tiled=True)  27.2 us
    ppermute x6, starting transfers between devices, scatter_sum_axis(): lax.ppermute(block, axis, [(i, (i + k) % count) for i in range(count)])  22.6 us
    all_to_all x2, starting transfers between devices, routed_experts(): lax.all_to_all(slot_rows, EXPERT_AXES, split_axis=1, concat_axis=1, tiled...  20.9 us
    ppermute x6, starting transfers between devices, gather_axis(): lax.ppermute(x, axis, [(i, (i + k) % count) for i in range(count)])  16.6 us
  transfers between devices with their start and end apart: 22, of which 8 were waited for; matrix products, arithmetic and copies ran while one was open for 13% of the time, Pallas kernels for 0%

profile of v7, /device:TPU:66, one launch (start us, length us, event | category | flops | bytes accessed | tf_op | source)
XLA Modules:
  0.0 488.9 jit_solution(11925770092025504174)
XLA Ops:
  4.6 16.1 %all-to-all-start.4 = ((bf16[6,16,2560]{2,0,1:T(8,128)(2,1)}), bf16[6,16,2560]{2,0,1:T(8,128)(2,1)}, u32[]{:S(2)}, u32[]{:S(2)}) async-start(bf16[6,16,2560]{2,0,1:T(8,128)(2,1)} %copy.288), calls=%async_computation.4 | async-start | bytes 1310720 | tf_op jit(solution)/shard_map/all_to_all | solution.py:211
  22.9 52.4 %all-gather.1 = bf16[16,2,2560]{2,1,0:T(2,128)(2,1)S(1)} all-gather(bf16[1,2,2560]{2,1,0:T(2,128)(2,1)S(1)} %bitcast.270), channel_id=1, replica_groups=mesh['dp'=4,'y'=4,'zh'=4,'zl'=4,'c'=2] {'zh','zl'}, dimensions={0}, use_global_device_ids=true | all-gather | bytes 174080 | tf_op jit(solution)/shard_map/all_gather | solution.py:45
  75.4 13.5 %all_gather.20 = bf16[128,2560]{1,0:T(8,128)(2,1)S(1)} all-gather(bf16[32,2560]{1,0:T(8,128)(2,1)S(1)} %reshape.1009), channel_id=1, replica_groups=mesh['dp'=4,'y'=4,'zh'=4,'zl'=4,'c'=2] {'y'}, dimensions={0}, use_global_device_ids=true | all-gather | bytes 819200 | tf_op jit(solution)/shard_map/all_gather | solution.py:46
  98.2 15.3 %all-to-all-start = ((bf16[128,1,4,5,131]{4,2,3,1,0:T(4,128)(2,1)}), bf16[128,1,4,5,131]{4,2,3,1,0:T(4,128)(2,1)}, u32[]{:S(2)}, u32[]{:S(2)}) async-start(bf16[128,1,4,5,131]{4,2,3,1,0:T(4,128)(2,1)} %copy.273), calls=%async_computation | async-start | bytes 2621440 | tf_op jit(solution)/shard_map/all_to_all | solution.py:164
  118.4 3.0 collective-permute-start.8
  121.4 2.9 collective-permute-start.10
  124.7 4.1 gather_fusion.3
  129.1 72.3 %collective-permute-done.9 = bf16[1,6,16,2560]{3,2,1,0:T(8,128)(2,1)S(1)} collective-permute-done((bf16[1,6,16,2560]{3,2,1,0:T(8,128)(2,1)S(1)}, bf16[1,6,16,2560]{3,2,1,0:T(8,128)(2,1)S(1)}, u32[]{:S(2)}, u32[]{:S(2)}) %collective-permute-start.9) | collective-permute-done | bytes 491552 | tf_op jit(solution)/shard_map/ppermute | solution.py:27
  201.3 10.9 %collective-permute-done.8 = bf16[1,6,16,2560]{3,2,1,0:T(8,128)(2,1)S(1)} collective-permute-done((bf16[1,6,16,2560]{3,2,1,0:T(8,128)(2,1)S(1)}, bf16[1,6,16,2560]{3,2,1,0:T(8,128)(2,1)S(1)}, u32[]{:S(2)}, u32[]{:S(2)}) %collective-permute-start.8) | collective-permute-done | bytes 491552 | tf_op jit(solution)/shard_map/ppermute | solution.py:27
  216.0 4.0 copy.274
  224.5 28.9 %all-gather.3 = bf16[16,2,2560]{2,1,0:T(2,128)(2,1)S(1)} all-gather(bf16[1,2,2560]{2,1,0:T(2,128)(2,1)S(1)} %bitcast.271), channel_id=1, replica_groups=mesh['dp'=4,'y'=4,'zh'=4,'zl'=4,'c'=2] {'zh','zl'}, dimensions={0}, use_global_device_ids=true | all-gather | bytes 174080 | tf_op jit(solution)/shard_map/all_gather | solution.py:45
  253.5 13.7 %all_gather.23 = bf16[128,2560]{1,0:T(8,128)(2,1)S(1)} all-gather(bf16[32,2560]{1,0:T(8,128)(2,1)S(1)} %reshape.1013), channel_id=1, replica_groups=mesh['dp'=4,'y'=4,'zh'=4,'zl'=4,'c'=2] {'y'}, dimensions={0}, use_global_device_ids=true | all-gather | bytes 819200 | tf_op jit(solution)/shard_map/all_gather | solution.py:46
  269.1 14.1 %all-to-all-start.1 = ((f32[128,1,20]{2,1,0:T(1,128)}), f32[128,1,20]{2,1,0:T(1,128)S(1)}, u32[]{:S(2)}, u32[]{:S(2)}) async-start(f32[128,1,20]{2,1,0:T(1,128)} %bitcast.84), calls=%async_computation.1 | async-start | bytes 131072 | tf_op jit(solution)/shard_map/all_to_all | solution.py:170
  286.7 10.3 %all-to-all-done.1 = f32[128,1,20]{2,1,0:T(1,128)S(1)} async-done(((f32[128,1,20]{2,1,0:T(1,128)}), f32[128,1,20]{2,1,0:T(1,128)S(1)}, u32[]{:S(2)}, u32[]{:S(2)}) %all-to-all-start.1) | async-done | bytes 10272 | tf_op jit(solution)/shard_map/all_to_all | solution.py:170
  303.1 4.8 all-to-all-start.2
  309.6 14.9 %all-to-all-done.2 = bf16[16,2,1280]{2,1,0:T(2,128)(2,1)S(1)} async-done(((bf16[16,2,1280]{2,1,0:T(2,128)(2,1)}), bf16[16,2,1280]{2,1,0:T(2,128)(2,1)S(1)}, u32[]{:S(2)}, u32[]{:S(2)}) %all-to-all-start.2) | async-done | bytes 81952 | tf_op jit(solution)/shard_map/all_to_all | solution.py:211
  326.6 3.2 collective-permute-start
  332.4 3.5 fusion.21
  339.4 3.1 fusion.11
  342.5 4.5 convolution_convert_fusion
  347.0 3.9 convert.48
  356.0 4.5 convolution_convert_fusion.1
  372.7 5.7 %collective-permute-start.5 = (bf16[1,16,2560]{2,1,0:T(8,128)(2,1)S(1)}, bf16[1,16,2560]{2,1,0:T(8,128)(2,1)S(1)}, u32[]{:S(2)}, u32[]{:S(2)}) collective-permute-start(bf16[1,16,2560]{2,1,0:T(8,128)(2,1)S(1)} %get-tuple-element.42), channel_id=1, source_target_pairs={{0,2},{2,4},{4,6},{6,0},{1,3},{3,5},{5,7},{7,1},{8,10},{10,12},{12... | collective-permute-start | bytes 245768 | tf_op jit(solution)/shard_map/ppermute | solution.py:39
  380.4 5.4 %collective-permute-start.6 = (bf16[1,16,2560]{2,1,0:T(8,128)(2,1)S(1)}, bf16[1,16,2560]{2,1,0:T(8,128)(2,1)S(1)}, u32[]{:S(2)}, u32[]{:S(2)}) collective-permute-start(bf16[1,16,2560]{2,1,0:T(8,128)(2,1)S(1)} %get-tuple-element.44), channel_id=1, source_target_pairs={{0,4},{2,6},{4,0},{6,2},{1,5},{3,7},{5,1},{7,3},{8,12},{10,14},{12... | collective-permute-start | bytes 245768 | tf_op jit(solution)/shard_map/ppermute | solution.py:39
  385.7 3.3 fusion
  392.2 3.9 collective-permute-start.15
  396.1 3.7 collective-permute-start.14
  401.8 3.5 all-to-all-start.3
  405.3 25.4 %collective-permute-done.13 = bf16[6,16,2560]{2,1,0:T(8,128)(2,1)} collective-permute-done((bf16[6,16,2560]{2,1,0:T(8,128)(2,1)}, bf16[6,16,2560]{2,1,0:T(8,128)(2,1)}, u32[]{:S(2)}, u32[]{:S(2)}) %collective-permute-start.13) | collective-permute-done | bytes 491552 | tf_op jit(solution)/shard_map/ppermute | solution.py:39
  430.7 8.0 %collective-permute-done.14 = bf16[6,16,2560]{2,1,0:T(8,128)(2,1)} collective-permute-done((bf16[6,16,2560]{2,1,0:T(8,128)(2,1)}, bf16[6,16,2560]{2,1,0:T(8,128)(2,1)}, u32[]{:S(2)}, u32[]{:S(2)}) %collective-permute-start.14) | collective-permute-done | bytes 491552 | tf_op jit(solution)/shard_map/ppermute | solution.py:39
  441.4 7.7 %all-to-all-start.5 = ((bf16[6,16,2560]{2,0,1:T(8,128)(2,1)}), bf16[6,16,2560]{2,0,1:T(8,128)(2,1)S(1)}, u32[]{:S(2)}, u32[]{:S(2)}) async-start(bf16[6,16,2560]{2,0,1:T(8,128)(2,1)} %copy.293), calls=%async_computation.5 | async-start | bytes 1310720 | tf_op jit(solution)/shard_map/all_to_all | solution.py:233
  453.8 33.9 %all-to-all-done.5 = bf16[6,16,2560]{2,0,1:T(8,128)(2,1)S(1)} async-done(((bf16[6,16,2560]{2,0,1:T(8,128)(2,1)}), bf16[6,16,2560]{2,0,1:T(8,128)(2,1)S(1)}, u32[]{:S(2)}, u32[]{:S(2)}) %all-to-all-start.5) | async-done | bytes 491552 | tf_op jit(solution)/shard_map/all_to_all | solution.py:233
  (174 shorter events, 82.8 us)
Async XLA Ops:
  0.0 342.5 %copy-start = (bf16[192,2560]{1,0:T(8,128)(2,1)S(1)}, bf16[192,2560]{1,0:T(8,128)(2,1)}, u32[]{:S(2)}) copy-start(bf16[192,2560]{1,0:T(8,128)(2,1)} %param.27) | copy-start | bytes 2949124
  2.9 111.1 %copy-start.1 = (f32[64,2560]{1,0:T(8,128)}, f32[64,2560]{1,0:T(8,128)S(1)}, u32[]{:S(2)}) copy-start(f32[64,2560]{1,0:T(8,128)S(1)} %convert_element_type.153) | copy-start | bytes 1966084
  3.1 17.6 %copy-start.8 = (s32[128,32]{0,1:T(8,128)S(1)}, s32[128,32]{0,1:T(8,128)}, u32[]{:S(2)}) copy-start(s32[128,32]{0,1:T(8,128)} %param.20) | copy-start | bytes 49156
  3.1 18.0 %copy-start.9 = (bf16[1,2560]{1,0:T(2,128)(2,1)S(1)}, bf16[1,2560]{1,0:T(2,128)(2,1)}, u32[]{:S(2)}) copy-start(bf16[1,2560]{1,0:T(2,128)(2,1)} %param.17) | copy-start | bytes 15364
  4.6 93.6 %all-to-all-start.4 = ((bf16[6,16,2560]{2,0,1:T(8,128)(2,1)}), bf16[6,16,2560]{2,0,1:T(8,128)(2,1)}, u32[]{:S(2)}, u32[]{:S(2)}) async-start(bf16[6,16,2560]{2,0,1:T(8,128)(2,1)} %copy.288), calls=%async_computation.4 | async-start | bytes 1310720 | tf_op jit(solution)/shard_map/all_to_all | solution.py:211
  75.4 15.1 %copy-start.11 = (s32[128]{0:T(128)S(1)}, s32[128]{0:T(128)}, u32[]{:S(2)}) copy-start(s32[128]{0:T(128)} %param.21) | copy-start | bytes 1540
  95.6 17.9 %copy-start.7 = (s32[64,6]{0,1:T(8,128)S(1)}, s32[64,6]{0,1:T(8,128)}, u32[]{:S(2)}) copy-start(s32[64,6]{0,1:T(8,128)} %param.25) | copy-start | bytes 4612
  95.7 18.2 %copy-start.10 = (bf16[1,1024]{1,0:T(2,128)(2,1)S(1)}, bf16[1,1024]{1,0:T(2,128)(2,1)}, u32[]{:S(2)}) copy-start(bf16[1,1024]{1,0:T(2,128)(2,1)} %param.18) | copy-start | bytes 6148
  95.7 18.3 %copy-start.4 = (bf16[2560,64]{0,1:T(8,128)(2,1)S(1)}, bf16[2560,64]{0,1:T(8,128)(2,1)}, u32[]{:S(2)}) copy-start(bf16[2560,64]{0,1:T(8,128)(2,1)} %param.24) | copy-start | bytes 983044
  98.2 117.7 %all-to-all-start = ((bf16[128,1,4,5,131]{4,2,3,1,0:T(4,128)(2,1)}), bf16[128,1,4,5,131]{4,2,3,1,0:T(4,128)(2,1)}, u32[]{:S(2)}, u32[]{:S(2)}) async-start(bf16[128,1,4,5,131]{4,2,3,1,0:T(4,128)(2,1)} %copy.273), calls=%async_computation | async-start | bytes 2621440 | tf_op jit(solution)/shard_map/all_to_all | solution.py:164
  115.6 85.8 %collective-permute-start.9 = (bf16[1,6,16,2560]{3,2,1,0:T(8,128)(2,1)S(1)}, bf16[1,6,16,2560]{3,2,1,0:T(8,128)(2,1)S(1)}, u32[]{:S(2)}, u32[]{:S(2)}) collective-permute-start(bf16[1,6,16,2560]{3,2,1,0:T(8,128)(2,1)S(1)} %bitcast.242), channel_id=1, source_target_pairs={{0,4},{2,6},{4,0},{6,2},{1,5},{3,7},{5,1},{7,3},{8,12},{10,14},{12... | collective-permute-start | bytes 1474568 | tf_op jit(solution)/shard_map/ppermute | solution.py:27
  118.4 93.8 %collective-permute-start.8 = (bf16[1,6,16,2560]{3,2,1,0:T(8,128)(2,1)S(1)}, bf16[1,6,16,2560]{3,2,1,0:T(8,128)(2,1)S(1)}, u32[]{:S(2)}, u32[]{:S(2)}) collective-permute-start(bf16[1,6,16,2560]{3,2,1,0:T(8,128)(2,1)S(1)} %bitcast.243), channel_id=1, source_target_pairs={{0,2},{2,4},{4,6},{6,0},{1,3},{3,5},{5,7},{7,1},{8,10},{10,12},{12... | collective-permute-start | bytes 1474568 | tf_op jit(solution)/shard_map/ppermute | solution.py:27
  121.4 90.8 %collective-permute-start.10 = (bf16[1,6,16,2560]{3,2,1,0:T(8,128)(2,1)S(1)}, bf16[1,6,16,2560]{3,2,1,0:T(8,128)(2,1)S(1)}, u32[]{:S(2)}, u32[]{:S(2)}) collective-permute-start(bf16[1,6,16,2560]{3,2,1,0:T(8,128)(2,1)S(1)} %bitcast.244), channel_id=1, source_target_pairs={{0,6},{2,0},{4,2},{6,4},{1,7},{3,1},{5,3},{7,5},{8,14},{10,8},{12,... | collective-permute-start | bytes 1474568 | tf_op jit(solution)/shard_map/ppermute | solution.py:27
  269.1 28.0 %all-to-all-start.1 = ((f32[128,1,20]{2,1,0:T(1,128)}), f32[128,1,20]{2,1,0:T(1,128)S(1)}, u32[]{:S(2)}, u32[]{:S(2)}) async-start(f32[128,1,20]{2,1,0:T(1,128)} %bitcast.84), calls=%async_computation.1 | async-start | bytes 131072 | tf_op jit(solution)/shard_map/all_to_all | solution.py:170
  284.6 54.7 %collective-permute-start.11 = (bf16[4,6,16,2560]{3,2,1,0:T(8,128)(2,1)}, bf16[4,6,16,2560]{3,2,1,0:T(8,128)(2,1)}, u32[]{:S(2)}, u32[]{:S(2)}) collective-permute-start(bf16[4,6,16,2560]{3,2,1,0:T(8,128)(2,1)} %broadcast_select_fusion), channel_id=1, source_target_pairs={{0,1},{1,0},{2,3},{3,2},{4,5},{5,4},{6,7},{7,6},{8,9},{9,8},{10,11... | collective-permute-start | bytes 5898248 | tf_op jit(solution)/shard_map/ppermute | solution.py:214
  303.1 21.3 %all-to-all-start.2 = ((bf16[16,2,1280]{2,1,0:T(2,128)(2,1)}), bf16[16,2,1280]{2,1,0:T(2,128)(2,1)S(1)}, u32[]{:S(2)}, u32[]{:S(2)}) async-start(bf16[16,2,1280]{2,1,0:T(2,128)(2,1)} %reshape.1047), calls=%async_computation.2 | async-start | bytes 163840 | tf_op jit(solution)/shard_map/all_to_all | solution.py:211
  324.5 11.4 %collective-permute-start.1 = (bf16[1,1,16,2560]{3,2,1,0:T(8,128)(2,1)S(1)}, bf16[1,1,16,2560]{3,2,1,0:T(8,128)(2,1)S(1)}, u32[]{:S(2)}, u32[]{:S(2)}) collective-permute-start(bf16[1,1,16,2560]{3,2,1,0:T(8,128)(2,1)S(1)} %bitcast.258), channel_id=1, source_target_pairs={{0,4},{2,6},{4,0},{6,2},{1,5},{3,7},{5,1},{7,3},{8,12},{10,14},{12... | collective-permute-start | bytes 245768 | tf_op jit(solution)/shard_map/ppermute | solution.py:27
  326.6 9.3 %collective-permute-start = (bf16[1,1,16,2560]{3,2,1,0:T(8,128)(2,1)S(1)}, bf16[1,1,16,2560]{3,2,1,0:T(8,128)(2,1)S(1)}, u32[]{:S(2)}, u32[]{:S(2)}) collective-permute-start(bf16[1,1,16,2560]{3,2,1,0:T(8,128)(2,1)S(1)} %bitcast.259), channel_id=1, source_target_pairs={{0,2},{2,4},{4,6},{6,0},{1,3},{3,5},{5,7},{7,1},{8,10},{10,12},{12... | collective-permute-start | bytes 245768 | tf_op jit(solution)/shard_map/ppermute | solution.py:27
  329.8 7.3 %collective-permute-start.2 = (bf16[1,1,16,2560]{3,2,1,0:T(8,128)(2,1)S(1)}, bf16[1,1,16,2560]{3,2,1,0:T(8,128)(2,1)S(1)}, u32[]{:S(2)}, u32[]{:S(2)}) collective-permute-start(bf16[1,1,16,2560]{3,2,1,0:T(8,128)(2,1)S(1)} %bitcast.260), channel_id=1, source_target_pairs={{0,6},{2,0},{4,2},{6,4},{1,7},{3,1},{5,3},{7,5},{8,14},{10,8},{12,... | collective-permute-start | bytes 245768 | tf_op jit(solution)/shard_map/ppermute | solution.py:27
  350.9 34.8 %collective-permute-start.12 = (f32[4,6,16,2560]{3,2,1,0:T(8,128)}, f32[4,6,16,2560]{3,2,1,0:T(8,128)}, u32[]{:S(2)}, u32[]{:S(2)}) collective-permute-start(f32[4,6,16,2560]{3,2,1,0:T(8,128)} %convert.48), channel_id=1, source_target_pairs={{0,1},{1,0},{2,3},{3,2},{4,5},{5,4},{6,7},{7,6},{8,9},{9,8},{10,11... | collective-permute-start | bytes 11796488 | tf_op jit(solution)/shard_map/ppermute | solution.py:231
  353.6 6.9 %collective-permute-start.3 = (bf16[4,1,16,2560]{3,2,0,1:T(8,128)(2,1)}, bf16[4,1,16,2560]{3,2,0,1:T(8,128)(2,1)}, u32[]{:S(2)}, u32[]{:S(2)}) collective-permute-start(bf16[4,1,16,2560]{3,2,0,1:T(8,128)(2,1)} %bitcast_select_fusion.1), channel_id=1, source_target_pairs={{0,1},{1,0},{2,3},{3,2},{4,5},{5,4},{6,7},{7,6},{8,9},{9,8},{10,11... | collective-permute-start | bytes 983048 | tf_op jit(solution)/shard_map/ppermute | solution.py:214
  366.4 5.1 %collective-permute-start.4 = (f32[4,1,16,2560]{3,2,1,0:T(8,128)}, f32[4,1,16,2560]{3,2,1,0:T(8,128)}, u32[]{:S(2)}, u32[]{:S(2)}) collective-permute-start(f32[4,1,16,2560]{3,2,1,0:T(8,128)} %convert.46), channel_id=1, source_target_pairs={{0,1},{1,0},{2,3},{3,2},{4,5},{5,4},{6,7},{7,6},{8,9},{9,8},{10,11... | collective-permute-start | bytes 1966088 | tf_op jit(solution)/shard_map/ppermute | solution.py:231
  372.7 23.4 %collective-permute-start.5 = (bf16[1,16,2560]{2,1,0:T(8,128)(2,1)S(1)}, bf16[1,16,2560]{2,1,0:T(8,128)(2,1)S(1)}, u32[]{:S(2)}, u32[]{:S(2)}) collective-permute-start(bf16[1,16,2560]{2,1,0:T(8,128)(2,1)S(1)} %get-tuple-element.42), channel_id=1, source_target_pairs={{0,2},{2,4},{4,6},{6,0},{1,3},{3,5},{5,7},{7,1},{8,10},{10,12},{12... | collective-permute-start | bytes 245768 | tf_op jit(solution)/shard_map/ppermute | solution.py:39
  378.4 21.4 %collective-permute-start.7 = (bf16[1,16,2560]{2,1,0:T(8,128)(2,1)S(1)}, bf16[1,16,2560]{2,1,0:T(8,128)(2,1)S(1)}, u32[]{:S(2)}, u32[]{:S(2)}) collective-permute-start(bf16[1,16,2560]{2,1,0:T(8,128)(2,1)S(1)} %get-tuple-element.43), channel_id=1, source_target_pairs={{0,6},{2,0},{4,2},{6,4},{1,7},{3,1},{5,3},{7,5},{8,14},{10,8},{12,... | collective-permute-start | bytes 245768 | tf_op jit(solution)/shard_map/ppermute | solution.py:39
  380.4 19.5 %collective-permute-start.6 = (bf16[1,16,2560]{2,1,0:T(8,128)(2,1)S(1)}, bf16[1,16,2560]{2,1,0:T(8,128)(2,1)S(1)}, u32[]{:S(2)}, u32[]{:S(2)}) collective-permute-start(bf16[1,16,2560]{2,1,0:T(8,128)(2,1)S(1)} %get-tuple-element.44), channel_id=1, source_target_pairs={{0,4},{2,6},{4,0},{6,2},{1,5},{3,7},{5,1},{7,3},{8,12},{10,14},{12... | collective-permute-start | bytes 245768 | tf_op jit(solution)/shard_map/ppermute | solution.py:39
  390.3 40.4 %collective-permute-start.13 = (bf16[6,16,2560]{2,1,0:T(8,128)(2,1)}, bf16[6,16,2560]{2,1,0:T(8,128)(2,1)}, u32[]{:S(2)}, u32[]{:S(2)}) collective-permute-start(bf16[6,16,2560]{2,1,0:T(8,128)(2,1)} %get-tuple-element.35), channel_id=1, source_target_pairs={{0,2},{2,4},{4,6},{6,0},{1,3},{3,5},{5,7},{7,1},{8,10},{10,12},{12... | collective-permute-start | bytes 1474568 | tf_op jit(solution)/shard_map/ppermute | solution.py:39
  392.2 38.5 %collective-permute-start.15 = (bf16[6,16,2560]{2,1,0:T(8,128)(2,1)}, bf16[6,16,2560]{2,1,0:T(8,128)(2,1)}, u32[]{:S(2)}, u32[]{:S(2)}) collective-permute-start(bf16[6,16,2560]{2,1,0:T(8,128)(2,1)} %get-tuple-element.36), channel_id=1, source_target_pairs={{0,6},{2,0},{4,2},{6,4},{1,7},{3,1},{5,3},{7,5},{8,14},{10,8},{12,... | collective-permute-start | bytes 1474568 | tf_op jit(solution)/shard_map/ppermute | solution.py:39
  396.1 42.6 %collective-permute-start.14 = (bf16[6,16,2560]{2,1,0:T(8,128)(2,1)}, bf16[6,16,2560]{2,1,0:T(8,128)(2,1)}, u32[]{:S(2)}, u32[]{:S(2)}) collective-permute-start(bf16[6,16,2560]{2,1,0:T(8,128)(2,1)} %get-tuple-element.37), channel_id=1, source_target_pairs={{0,4},{2,6},{4,0},{6,2},{1,5},{3,7},{5,1},{7,3},{8,12},{10,14},{12... | collective-permute-start | bytes 1474568 | tf_op jit(solution)/shard_map/ppermute | solution.py:39
  401.8 39.7 %all-to-all-start.3 = ((bf16[16,2,1280]{2,1,0:T(2,128)(2,1)}), bf16[16,2,1280]{2,1,0:T(2,128)(2,1)S(1)}, u32[]{:S(2)}, u32[]{:S(2)}) async-start(bf16[16,2,1280]{2,1,0:T(2,128)(2,1)} %reshape.1049), calls=%async_computation.3 | async-start | bytes 163840 | tf_op jit(solution)/shard_map/all_to_all | solution.py:233
  405.3 44.3 %copy-start.5 = (bf16[2560,64]{0,1:T(8,128)(2,1)S(1)}, bf16[2560,64]{0,1:T(8,128)(2,1)}, u32[]{:S(2)}) copy-start(bf16[2560,64]{0,1:T(8,128)(2,1)} %param.24) | copy-start | bytes 983044
  440.3 47.4 %copy-start.2 = (f32[64,2560]{1,0:T(8,128)S(1)}, f32[64,2560]{1,0:T(8,128)}, u32[]{:S(2)}) copy-start(f32[64,2560]{1,0:T(8,128)} %copy-done.1) | copy-start | bytes 1966084
  441.4 46.3 %all-to-all-start.5 = ((bf16[6,16,2560]{2,0,1:T(8,128)(2,1)}), bf16[6,16,2560]{2,0,1:T(8,128)(2,1)S(1)}, u32[]{:S(2)}, u32[]{:S(2)}) async-start(bf16[6,16,2560]{2,0,1:T(8,128)(2,1)} %copy.293), calls=%async_computation.5 | async-start | bytes 1310720 | tf_op jit(solution)/shard_map/all_to_all | solution.py:233
  (2 other events, 7.7 us)

commit v8 on v6

--- a/solution.py
+++ b/solution.py
@@ -40,10 +40,10 @@
     return total
 
 
-def gather_nested(x, sizes):
-    for axis in reversed(TENSOR):
-        x = gather_axis(x, axis, sizes[axis])
-    return x
+def gather_nested(x):
+    x = lax.all_gather(x, "c", axis=0, tiled=True)
+    x = lax.all_gather(x, ("zh", "zl"), axis=0, tiled=True)
+    return lax.all_gather(x, "y", axis=0, tiled=True)
 
 
 def local_parts(query_all, paged_store_cache, page_table, cache_length, my_index):
@@ -141,8 +141,7 @@
     tensor_count = lax.axis_size(TENSOR)
     my_index = lax.axis_index(TENSOR)
     dec_rows = queries.shape[0]
-    sizes = {axis: lax.axis_size(axis) for axis in TENSOR}
-    query_all = gather_nested(queries, sizes)
+    query_all = gather_nested(queries)
     request_max, request_total, request_accum = local_parts(
         query_all, paged_store_cache, page_table, cache_length, my_index
     )
@@ -164,7 +163,7 @@
     parts = lax.all_to_all(packed, TENSOR, split_axis=0, concat_axis=0, tiled=True)
     parts = jnp.swapaxes(parts, 0, 1)
     context = finish_context(parts, queries, fresh_entries)
-    context_all = gather_nested(context, sizes)
+    context_all = gather_nested(context)
     projected = jnp.dot(context_all, out_proj, preferred_element_type=jnp.float32)
     column_block = projected.shape[1]
     arrived = lax.all_to_all(
@@ -196,7 +195,8 @@
         "cei,id->ced", selector.astype(jnp.bfloat16), normed, preferred_element_type=jnp.float32
     ).astype(jnp.bfloat16)
     landed = lax.all_to_all(slot_rows, EXPERT_AXES, split_axis=1, concat_axis=1, tiled=True)
-    own_rows = gather_axis(landed[None], "zl", sizes["zl"])
+    z_low = lax.axis_size("zl")
+    own_rows = gather_axis(landed[None], "zl", z_low)
     swap = [(0, 1), (1, 0)]
     partner_rows = lax.ppermute(own_rows, "c", swap)
 
@@ -216,7 +216,7 @@
     own_partial = expert_partial(own_rows)
     partner_partial = expert_partial(partner_rows)
     core_sum = own_partial + lax.ppermute(partner_partial, "c", swap)
-    slice_sum = scatter_sum_axis(core_sum.astype(jnp.bfloat16), "zl", sizes["zl"])
+    slice_sum = scatter_sum_axis(core_sum.astype(jnp.bfloat16), "zl", z_low)
     expert_out = lax.all_to_all(
         slice_sum.astype(jnp.bfloat16), EXPERT_AXES, split_axis=1, concat_axis=1, tiled=True
     ).astype(jnp.float32)

time: 463 us -> 433 us (0.935)
  the two profiles are of different devices: /device:TPU:35 before, /device:TPU:33 now
where the time goes in v8:
time: 433 us
  waiting for transfers between devices  189 us (44%)
  blocking collectives  117 us (27%)
  starting transfers between devices  70.5 us (16%)
  local copies, waits for them, and re-layouts  20.4 us (5%)
  other arithmetic  18.2 us (4%)
  matrix products  16.7 us (4%)
    all_to_all x1, waiting for transfers between devices, local(): lax.all_to_all(packed, TENSOR, split_axis=0, concat_axis=0, tiled=True)  64 us
    all_gather x2, blocking collectives, gather_nested(): x = lax.all_gather(x, ('zh', 'zl'), axis=0, tiled=True)  47.8 us
    all_to_all x1, blocking collectives, local(): lax.all_to_all(slot_rows, EXPERT_AXES, split_axis=1, concat_axis=1, tiled...  42.5 us
    ppermute x3, waiting for transfers between devices, scatter_sum_axis(): lax.ppermute(block, axis, [(i, (i + k) % count) for i in range(count)])  38.4 us
    ppermute x3, waiting for transfers between devices, gather_axis(): lax.ppermute(x, axis, [(i, (i + k) % count) for i in range(count)])  36.2 us
    all_to_all x1, waiting for transfers between devices, local(): lax.all_to_all(slice_sum.astype(jnp.bfloat16), EXPERT_AXES, split_axis=1,...  32.6 us
    all_to_all x1, starting transfers between devices, local(): lax.all_to_all(packed, TENSOR, split_axis=0, concat_axis=0, tiled=True)  22 us
    all_gather x2, blocking collectives, gather_nested(): return lax.all_gather(x, 'y', axis=0, tiled=True)  20.9 us
  transfers between devices with their start and end apart: 11, of which 9 were waited for; matrix products, arithmetic and copies ran while one was open for 2% of the time, Pallas kernels for 0%

profile of v8, /device:TPU:33, one launch (start us, length us, event | category | flops | bytes accessed | tf_op | source)
XLA Modules:
  0.0 432.5 jit_solution(9906897564877386935)
XLA Ops:
  1.9 2.4 all-gather
  4.3 27.1 %all-gather.1 = bf16[16,2,2560]{2,1,0:T(2,128)(2,1)S(1)} all-gather(bf16[1,2,2560]{2,1,0:T(2,128)(2,1)S(1)} %bitcast.170), channel_id=1, replica_groups=mesh['dp'=4,'y'=4,'zh'=4,'zl'=4,'c'=2] {'zh','zl'}, dimensions={0}, use_global_device_ids=true | all-gather | bytes 174080 | tf_op jit(solution)/shard_map/all_gather | solution.py:45
  31.4 10.7 %all_gather.20 = bf16[128,2560]{1,0:T(8,128)(2,1)S(1)} all-gather(bf16[32,2560]{1,0:T(8,128)(2,1)S(1)} %reshape.657), channel_id=1, replica_groups=mesh['dp'=4,'y'=4,'zh'=4,'zl'=4,'c'=2] {'y'}, dimensions={0}, use_global_device_ids=true | all-gather | bytes 819200 | tf_op jit(solution)/shard_map/all_gather | solution.py:46
  47.7 2.5 copy.270
  50.2 22.0 %all-to-all-start = ((bf16[128,1,4,5,131]{4,2,3,1,0:T(4,128)(2,1)}), bf16[128,1,4,5,131]{4,2,3,1,0:T(4,128)(2,1)S(1)}, u32[]{:S(2)}, u32[]{:S(2)}) async-start(bf16[128,1,4,5,131]{4,2,3,1,0:T(4,128)(2,1)} %copy.270), calls=%async_computation | async-start | bytes 2621440 | tf_op jit(solution)/shard_map/all_to_all | solution.py:163
  72.8 64.0 %all-to-all-done = bf16[128,1,4,5,131]{4,2,3,1,0:T(4,128)(2,1)S(1)} async-done(((bf16[128,1,4,5,131]{4,2,3,1,0:T(4,128)(2,1)}), bf16[128,1,4,5,131]{4,2,3,1,0:T(4,128)(2,1)S(1)}, u32[]{:S(2)}, u32[]{:S(2)}) %all-to-all-start) | async-done | bytes 670752 | tf_op jit(solution)/shard_map/all_to_all | solution.py:163
  136.8 3.6 copy.271
  142.0 3.7 all-gather.2
  145.7 20.7 %all-gather.3 = bf16[16,2,2560]{2,1,0:T(2,128)(2,1)S(1)} all-gather(bf16[1,2,2560]{2,1,0:T(2,128)(2,1)S(1)} %bitcast.171), channel_id=1, replica_groups=mesh['dp'=4,'y'=4,'zh'=4,'zl'=4,'c'=2] {'zh','zl'}, dimensions={0}, use_global_device_ids=true | all-gather | bytes 174080 | tf_op jit(solution)/shard_map/all_gather | solution.py:45
  166.5 10.3 %all_gather.23 = bf16[128,2560]{1,0:T(8,128)(2,1)S(1)} all-gather(bf16[32,2560]{1,0:T(8,128)(2,1)S(1)} %reshape.661), channel_id=1, replica_groups=mesh['dp'=4,'y'=4,'zh'=4,'zl'=4,'c'=2] {'y'}, dimensions={0}, use_global_device_ids=true | all-gather | bytes 819200 | tf_op jit(solution)/shard_map/all_gather | solution.py:46
  177.7 18.6 %all-to-all-start.1 = ((f32[128,1,20]{2,1,0:T(1,128)}), f32[128,1,20]{2,1,0:T(1,128)S(1)}, u32[]{:S(2)}, u32[]{:S(2)}) async-start(f32[128,1,20]{2,1,0:T(1,128)} %bitcast.51), calls=%async_computation.1 | async-start | bytes 131072 | tf_op jit(solution)/shard_map/all_to_all | solution.py:169
  196.4 14.3 %all-to-all-done.1 = f32[128,1,20]{2,1,0:T(1,128)S(1)} async-done(((f32[128,1,20]{2,1,0:T(1,128)}), f32[128,1,20]{2,1,0:T(1,128)S(1)}, u32[]{:S(2)}, u32[]{:S(2)}) %all-to-all-start.1) | async-done | bytes 10272 | tf_op jit(solution)/shard_map/all_to_all | solution.py:169
  213.3 42.5 %all_to_all.24 = bf16[6,16,2560]{2,0,1:T(8,128)(2,1)S(1)} all-to-all(bf16[6,16,2560]{2,0,1:T(8,128)(2,1)S(1)} %copy.279), channel_id=1, replica_groups=mesh['dp'=4,'y'=4,'zh'=4,'zl'=4,'c'=2] {'y','zh'}, dimensions={1} | all-to-all | bytes 983040 | tf_op jit(solution)/shard_map/all_to_all | solution.py:197
  255.9 4.8 %collective-permute-start = (bf16[1,6,16,2560]{3,2,1,0:T(8,128)(2,1)S(1)}, bf16[1,6,16,2560]{3,2,1,0:T(8,128)(2,1)S(1)}, u32[]{:S(2)}, u32[]{:S(2)}) collective-permute-start(bf16[1,6,16,2560]{3,2,1,0:T(8,128)(2,1)S(1)} %bitcast.158), channel_id=1, source_target_pairs={{0,2},{2,4},{4,6},{6,0},{1,3},{3,5},{5,7},{7,1},{8,10},{10,12},{12... | collective-permute-start | bytes 1474568 | tf_op jit(solution)/shard_map/ppermute | solution.py:27
  262.7 3.1 collective-permute-start.2
  265.8 7.2 %collective-permute-done = bf16[1,6,16,2560]{3,2,1,0:T(8,128)(2,1)S(1)} collective-permute-done((bf16[1,6,16,2560]{3,2,1,0:T(8,128)(2,1)S(1)}, bf16[1,6,16,2560]{3,2,1,0:T(8,128)(2,1)S(1)}, u32[]{:S(2)}, u32[]{:S(2)}) %collective-permute-start) | collective-permute-done | bytes 491552 | tf_op jit(solution)/shard_map/ppermute | solution.py:27
  273.0 29.0 %collective-permute-done.1 = bf16[1,6,16,2560]{3,2,1,0:T(8,128)(2,1)S(1)} collective-permute-done((bf16[1,6,16,2560]{3,2,1,0:T(8,128)(2,1)S(1)}, bf16[1,6,16,2560]{3,2,1,0:T(8,128)(2,1)S(1)}, u32[]{:S(2)}, u32[]{:S(2)}) %collective-permute-start.1) | collective-permute-done | bytes 491552 | tf_op jit(solution)/shard_map/ppermute | solution.py:27
  306.1 3.9 collective-permute-start.3
  310.0 3.4 collective-permute-done.3
  316.2 4.8 %convolution_convert_fusion = bf16[384,2560]{1,0:T(8,128)(2,1)} fusion(bf16[192,2560]{1,0:T(8,128)(2,1)S(1)} %copy-done, f32[384,192]{0,1:T(8,128)} %fusion.9, bf16[384,2560]{1,0:T(8,128)(2,1)} %bitcast.175, bf16[2,192,2560]{2,1,0:T(8,128)(2,1)} %param.26), kind=kOutput, calls=%fused_computation.2 | convolution fusion | flops 756400128 | bytes 6193152 | tf_op jit(solution)/shard_map/dot_general | solution.py:213
  321.0 3.9 convert.26
  324.9 2.3 collective-permute-start.4
  331.1 4.6 %convolution_convert_fusion.1 = bf16[384,2560]{1,0:T(8,128)(2,1)} fusion(bf16[192,2560]{1,0:T(8,128)(2,1)S(1)} %copy-done, bf16[384,2560]{1,0:T(8,128)(2,1)} %bitcast.156, bf16[2,192,2560]{2,1,0:T(8,128)(2,1)S(1)} %copy-done.10, f32[384,192]{0,1:T(8,128)} %fusion.15), kind=kOutput, calls=%fused_computation.3 | convolution fusion | flops 756400128 | bytes 6193152 | tf_op jit(solution)/shard_map/dot_general | solution.py:213
  335.6 3.3 fusion
  342.1 5.0 %collective-permute-start.6 = (bf16[6,16,2560]{2,1,0:T(8,128)(2,1)}, bf16[6,16,2560]{2,1,0:T(8,128)(2,1)}, u32[]{:S(2)}, u32[]{:S(2)}) collective-permute-start(bf16[6,16,2560]{2,1,0:T(8,128)(2,1)} %get-tuple-element.33), channel_id=1, source_target_pairs={{0,4},{2,6},{4,0},{6,2},{1,5},{3,7},{5,1},{7,3},{8,12},{10,14},{12... | collective-permute-start | bytes 1474568 | tf_op jit(solution)/shard_map/ppermute | solution.py:39
  347.1 3.4 collective-permute-start.7
  350.5 4.5 %collective-permute-done.5 = bf16[6,16,2560]{2,1,0:T(8,128)(2,1)} collective-permute-done((bf16[6,16,2560]{2,1,0:T(8,128)(2,1)}, bf16[6,16,2560]{2,1,0:T(8,128)(2,1)}, u32[]{:S(2)}, u32[]{:S(2)}) %collective-permute-start.5) | collective-permute-done | bytes 491552 | tf_op jit(solution)/shard_map/ppermute | solution.py:39
  355.0 29.7 %collective-permute-done.6 = bf16[6,16,2560]{2,1,0:T(8,128)(2,1)} collective-permute-done((bf16[6,16,2560]{2,1,0:T(8,128)(2,1)}, bf16[6,16,2560]{2,1,0:T(8,128)(2,1)}, u32[]{:S(2)}, u32[]{:S(2)}) %collective-permute-start.6) | collective-permute-done | bytes 491552 | tf_op jit(solution)/shard_map/ppermute | solution.py:39
  384.7 4.1 collective-permute-done.7
  391.6 3.6 all-to-all-start.3
  395.7 2.9 gather_fusion.1
  398.9 32.6 %all-to-all-done.3 = bf16[6,16,2560]{2,0,1:T(8,128)(2,1)S(1)} async-done(((bf16[6,16,2560]{2,0,1:T(8,128)(2,1)}), bf16[6,16,2560]{2,0,1:T(8,128)(2,1)S(1)}, u32[]{:S(2)}, u32[]{:S(2)}) %all-to-all-start.3) | async-done | bytes 491552 | tf_op jit(solution)/shard_map/all_to_all | solution.py:220
  (118 shorter events, 33.5 us)
Async XLA Ops:
  0.0 316.2 %copy-start = (bf16[192,2560]{1,0:T(8,128)(2,1)S(1)}, bf16[192,2560]{1,0:T(8,128)(2,1)}, u32[]{:S(2)}) copy-start(bf16[192,2560]{1,0:T(8,128)(2,1)} %param.27) | copy-start | bytes 2949124
  47.6 24.6 %copy-start.5 = (bf16[1,2560]{1,0:T(2,128)(2,1)S(1)}, bf16[1,2560]{1,0:T(2,128)(2,1)}, u32[]{:S(2)}) copy-start(bf16[1,2560]{1,0:T(2,128)(2,1)} %param.17) | copy-start | bytes 15364
  47.7 24.6 %copy-start.7 = (bf16[1,1024]{1,0:T(2,128)(2,1)S(1)}, bf16[1,1024]{1,0:T(2,128)(2,1)}, u32[]{:S(2)}) copy-start(bf16[1,1024]{1,0:T(2,128)(2,1)} %param.18) | copy-start | bytes 6148
  47.7 24.9 %copy-start.3 = (s32[64,6]{0,1:T(8,128)S(1)}, s32[64,6]{0,1:T(8,128)}, u32[]{:S(2)}) copy-start(s32[64,6]{0,1:T(8,128)} %param.25) | copy-start | bytes 4612
  50.2 86.6 %all-to-all-start = ((bf16[128,1,4,5,131]{4,2,3,1,0:T(4,128)(2,1)}), bf16[128,1,4,5,131]{4,2,3,1,0:T(4,128)(2,1)S(1)}, u32[]{:S(2)}, u32[]{:S(2)}) async-start(bf16[128,1,4,5,131]{4,2,3,1,0:T(4,128)(2,1)} %copy.270), calls=%async_computation | async-start | bytes 2621440 | tf_op jit(solution)/shard_map/all_to_all | solution.py:163
  140.7 36.1 %copy-start.4 = (bf16[2560,20]{0,1:T(8,128)(2,1)S(1)}, bf16[2560,20]{0,1:T(8,128)(2,1)}, u32[]{:S(2)}) copy-start(bf16[2560,20]{0,1:T(8,128)(2,1)} %param.22) | copy-start | bytes 307204
  140.9 55.4 %copy-start.2 = (bf16[64,2560]{1,0:T(8,128)(2,1)S(1)}, bf16[64,2560]{1,0:T(8,128)(2,1)}, u32[]{:S(2)}) copy-start(bf16[64,2560]{1,0:T(8,128)(2,1)} %param.16) | copy-start | bytes 983044
  141.7 54.7 %copy-start.6 = (bf16[2560]{0:T(1024)(128)(2,1)S(1)}, bf16[2560]{0:T(1024)(128)(2,1)}, u32[]{:S(2)}) copy-start(bf16[2560]{0:T(1024)(128)(2,1)} %param.23) | copy-start | bytes 15364
  177.7 33.0 %all-to-all-start.1 = ((f32[128,1,20]{2,1,0:T(1,128)}), f32[128,1,20]{2,1,0:T(1,128)S(1)}, u32[]{:S(2)}, u32[]{:S(2)}) async-start(f32[128,1,20]{2,1,0:T(1,128)} %bitcast.51), calls=%async_computation.1 | async-start | bytes 131072 | tf_op jit(solution)/shard_map/all_to_all | solution.py:169
  255.9 17.1 %collective-permute-start = (bf16[1,6,16,2560]{3,2,1,0:T(8,128)(2,1)S(1)}, bf16[1,6,16,2560]{3,2,1,0:T(8,128)(2,1)S(1)}, u32[]{:S(2)}, u32[]{:S(2)}) collective-permute-start(bf16[1,6,16,2560]{3,2,1,0:T(8,128)(2,1)S(1)} %bitcast.158), channel_id=1, source_target_pairs={{0,2},{2,4},{4,6},{6,0},{1,3},{3,5},{5,7},{7,1},{8,10},{10,12},{12... | collective-permute-start | bytes 1474568 | tf_op jit(solution)/shard_map/ppermute | solution.py:27
  260.7 41.3 %collective-permute-start.1 = (bf16[1,6,16,2560]{3,2,1,0:T(8,128)(2,1)S(1)}, bf16[1,6,16,2560]{3,2,1,0:T(8,128)(2,1)S(1)}, u32[]{:S(2)}, u32[]{:S(2)}) collective-permute-start(bf16[1,6,16,2560]{3,2,1,0:T(8,128)(2,1)S(1)} %bitcast.159), channel_id=1, source_target_pairs={{0,4},{2,6},{4,0},{6,2},{1,5},{3,7},{5,1},{7,3},{8,12},{10,14},{12... | collective-permute-start | bytes 1474568 | tf_op jit(solution)/shard_map/ppermute | solution.py:27
  262.7 39.4 %collective-permute-start.2 = (bf16[1,6,16,2560]{3,2,1,0:T(8,128)(2,1)S(1)}, bf16[1,6,16,2560]{3,2,1,0:T(8,128)(2,1)S(1)}, u32[]{:S(2)}, u32[]{:S(2)}) collective-permute-start(bf16[1,6,16,2560]{3,2,1,0:T(8,128)(2,1)S(1)} %bitcast.160), channel_id=1, source_target_pairs={{0,6},{2,0},{4,2},{6,4},{1,7},{3,1},{5,3},{7,5},{8,14},{10,8},{12,... | collective-permute-start | bytes 1474568 | tf_op jit(solution)/shard_map/ppermute | solution.py:27
  305.8 8.9 %copy-start.8 = (bf16[2,192,2560]{2,1,0:T(8,128)(2,1)S(1)}, bf16[2,192,2560]{2,1,0:T(8,128)(2,1)}, u32[]{:S(2)}) copy-start(bf16[2,192,2560]{2,1,0:T(8,128)(2,1)} %param.26) | copy-start | bytes 5898244
  306.1 7.3 %collective-permute-start.3 = (bf16[4,6,16,2560]{3,2,1,0:T(8,128)(2,1)S(1)}, bf16[4,6,16,2560]{3,2,1,0:T(8,128)(2,1)S(1)}, u32[]{:S(2)}, u32[]{:S(2)}) collective-permute-start(bf16[4,6,16,2560]{3,2,1,0:T(8,128)(2,1)S(1)} %broadcast_select_fusion), channel_id=1, source_target_pairs={{0,1},{1,0},{2,3},{3,2},{4,5},{5,4},{6,7},{7,6},{8,9},{9,8},{10,11... | collective-permute-start | bytes 5898248 | tf_op jit(solution)/shard_map/ppermute | solution.py:201
  313.4 1.3 copy-start.11
  324.9 10.7 %collective-permute-start.4 = (f32[4,6,16,2560]{3,2,1,0:T(8,128)}, f32[4,6,16,2560]{3,2,1,0:T(8,128)}, u32[]{:S(2)}, u32[]{:S(2)}) collective-permute-start(f32[4,6,16,2560]{3,2,1,0:T(8,128)} %convert.26), channel_id=1, source_target_pairs={{0,1},{1,0},{2,3},{3,2},{4,5},{5,4},{6,7},{7,6},{8,9},{9,8},{10,11... | collective-permute-start | bytes 11796488 | tf_op jit(solution)/shard_map/ppermute | solution.py:218
  327.3 2.3 copy-start.9
  327.5 1.3 copy-start.1
  329.5 1.5 copy-start.10
  340.2 14.9 %collective-permute-start.5 = (bf16[6,16,2560]{2,1,0:T(8,128)(2,1)}, bf16[6,16,2560]{2,1,0:T(8,128)(2,1)}, u32[]{:S(2)}, u32[]{:S(2)}) collective-permute-start(bf16[6,16,2560]{2,1,0:T(8,128)(2,1)} %get-tuple-element.31), channel_id=1, source_target_pairs={{0,2},{2,4},{4,6},{6,0},{1,3},{3,5},{5,7},{7,1},{8,10},{10,12},{12... | collective-permute-start | bytes 1474568 | tf_op jit(solution)/shard_map/ppermute | solution.py:39
  342.1 42.6 %collective-permute-start.6 = (bf16[6,16,2560]{2,1,0:T(8,128)(2,1)}, bf16[6,16,2560]{2,1,0:T(8,128)(2,1)}, u32[]{:S(2)}, u32[]{:S(2)}) collective-permute-start(bf16[6,16,2560]{2,1,0:T(8,128)(2,1)} %get-tuple-element.33), channel_id=1, source_target_pairs={{0,4},{2,6},{4,0},{6,2},{1,5},{3,7},{5,1},{7,3},{8,12},{10,14},{12... | collective-permute-start | bytes 1474568 | tf_op jit(solution)/shard_map/ppermute | solution.py:39
  347.1 41.7 %collective-permute-start.7 = (bf16[6,16,2560]{2,1,0:T(8,128)(2,1)}, bf16[6,16,2560]{2,1,0:T(8,128)(2,1)}, u32[]{:S(2)}, u32[]{:S(2)}) collective-permute-start(bf16[6,16,2560]{2,1,0:T(8,128)(2,1)} %get-tuple-element.32), channel_id=1, source_target_pairs={{0,6},{2,0},{4,2},{6,4},{1,7},{3,1},{5,3},{7,5},{8,14},{10,8},{12,... | collective-permute-start | bytes 1474568 | tf_op jit(solution)/shard_map/ppermute | solution.py:39
  390.4 5.0 %copy-start.12 = (bf16[2560,64]{0,1:T(8,128)(2,1)S(1)}, bf16[2560,64]{0,1:T(8,128)(2,1)}, u32[]{:S(2)}) copy-start(bf16[2560,64]{0,1:T(8,128)(2,1)} %param.24) | copy-start | bytes 983044
  391.6 39.9 %all-to-all-start.3 = ((bf16[6,16,2560]{2,0,1:T(8,128)(2,1)}), bf16[6,16,2560]{2,0,1:T(8,128)(2,1)S(1)}, u32[]{:S(2)}, u32[]{:S(2)}) async-start(bf16[6,16,2560]{2,0,1:T(8,128)(2,1)} %copy.284), calls=%async_computation.3 | async-start | bytes 1310720 | tf_op jit(solution)/shard_map/all_to_all | solution.py:220

commit v9 on v8

--- a/solution.py
+++ b/solution.py
@@ -42,7 +42,8 @@
 
 def gather_nested(x):
     x = lax.all_gather(x, "c", axis=0, tiled=True)
-    x = lax.all_gather(x, ("zh", "zl"), axis=0, tiled=True)
+    x = lax.all_gather(x, "zl", axis=0, tiled=True)
+    x = lax.all_gather(x, "zh", axis=0, tiled=True)
     return lax.all_gather(x, "y", axis=0, tiled=True)
 
 

time: 433 us -> 443 us (1.023)
  the two profiles are of different devices: /device:TPU:33 before, /device:TPU:35 now
where the time goes in v9:
time: 443 us; the launch traced here: 442 us
  waiting for transfers between devices  189 us (43%)
  blocking collectives  126 us (28%)
  starting transfers between devices  70.8 us (16%)
  local copies, waits for them, and re-layouts  20.3 us (5%)
  other arithmetic  18.2 us (4%)
  matrix products  16.7 us (4%)
    all_to_all x1, waiting for transfers between devices, local(): lax.all_to_all(packed, TENSOR, split_axis=0, concat_axis=0, tiled=True)  64 us
    all_to_all x1, blocking collectives, local(): lax.all_to_all(slot_rows, EXPERT_AXES, split_axis=1, concat_axis=1, tiled...  42.5 us
    ppermute x3, waiting for transfers between devices, scatter_sum_axis(): lax.ppermute(block, axis, [(i, (i + k) % count) for i in range(count)])  38.4 us
    ppermute x3, waiting for transfers between devices, gather_axis(): lax.ppermute(x, axis, [(i, (i + k) % count) for i in range(count)])  36.2 us
    all_gather x2, blocking collectives, gather_nested(): x = lax.all_gather(x, 'zh', axis=0, tiled=True)  35.6 us
    all_to_all x1, waiting for transfers between devices, local(): lax.all_to_all(slice_sum.astype(jnp.bfloat16), EXPERT_AXES, split_axis=1,...  32.5 us
    all_gather x2, blocking collectives, gather_nested(): return lax.all_gather(x, 'y', axis=0, tiled=True)  21.7 us
    all_gather x2, blocking collectives, gather_nested(): x = lax.all_gather(x, 'zl', axis=0, tiled=True)  20.6 us
  transfers between devices with their start and end apart: 11, of which 9 were waited for; matrix products, arithmetic and copies ran while one was open for 2% of the time, Pallas kernels for 0%

profile of v9, /device:TPU:35, one launch (start us, length us, event | category | flops | bytes accessed | tf_op | source)
XLA Modules:
  0.0 441.9 jit_solution(3608636277221688397)
XLA Ops:
  4.3 11.2 %all-gather.1 = bf16[4,2,2560]{2,1,0:T(2,128)(2,1)S(1)} all-gather(bf16[1,2,2560]{2,1,0:T(2,128)(2,1)S(1)} %bitcast.170), channel_id=1, replica_groups=mesh['dp'=4,'y'=4,'zh'=4,'zl'=4,'c'=2] {'zl'}, dimensions={0}, use_global_device_ids=true | all-gather | bytes 51200 | tf_op jit(solution)/shard_map/all_gather | solution.py:45
  15.5 20.9 %all_gather.26 = bf16[32,2560]{1,0:T(8,128)(2,1)S(1)} all-gather(bf16[8,2560]{1,0:T(8,128)(2,1)S(1)} %reshape.657), channel_id=1, replica_groups=mesh['dp'=4,'y'=4,'zh'=4,'zl'=4,'c'=2] {'zh'}, dimensions={0}, use_global_device_ids=true | all-gather | bytes 204800 | tf_op jit(solution)/shard_map/all_gather | solution.py:46
  36.4 11.3 %all_gather.27 = bf16[128,2560]{1,0:T(8,128)(2,1)S(1)} all-gather(bf16[32,2560]{1,0:T(8,128)(2,1)S(1)} %all_gather.26), channel_id=1, replica_groups=mesh['dp'=4,'y'=4,'zh'=4,'zl'=4,'c'=2] {'y'}, dimensions={0}, use_global_device_ids=true | all-gather | bytes 819200 | tf_op jit(solution)/shard_map/all_gather | solution.py:47
  53.2 2.5 copy.270
  55.8 20.5 %all-to-all-start = ((bf16[128,1,4,5,131]{4,2,3,1,0:T(4,128)(2,1)}), bf16[128,1,4,5,131]{4,2,3,1,0:T(4,128)(2,1)S(1)}, u32[]{:S(2)}, u32[]{:S(2)}) async-start(bf16[128,1,4,5,131]{4,2,3,1,0:T(4,128)(2,1)} %copy.270), calls=%async_computation | async-start | bytes 2621440 | tf_op jit(solution)/shard_map/all_to_all | solution.py:164
  76.9 64.0 %all-to-all-done = bf16[128,1,4,5,131]{4,2,3,1,0:T(4,128)(2,1)S(1)} async-done(((bf16[128,1,4,5,131]{4,2,3,1,0:T(4,128)(2,1)}), bf16[128,1,4,5,131]{4,2,3,1,0:T(4,128)(2,1)S(1)}, u32[]{:S(2)}, u32[]{:S(2)}) %all-to-all-start) | async-done | bytes 670752 | tf_op jit(solution)/shard_map/all_to_all | solution.py:164
  140.9 3.6 copy.271
  146.1 3.7 all-gather.2
  149.8 9.4 %all-gather.3 = bf16[4,2,2560]{2,1,0:T(2,128)(2,1)S(1)} all-gather(bf16[1,2,2560]{2,1,0:T(2,128)(2,1)S(1)} %bitcast.171), channel_id=1, replica_groups=mesh['dp'=4,'y'=4,'zh'=4,'zl'=4,'c'=2] {'zl'}, dimensions={0}, use_global_device_ids=true | all-gather | bytes 51200 | tf_op jit(solution)/shard_map/all_gather | solution.py:45
  159.2 14.6 %all_gather.30 = bf16[32,2560]{1,0:T(8,128)(2,1)S(1)} all-gather(bf16[8,2560]{1,0:T(8,128)(2,1)S(1)} %reshape.661), channel_id=1, replica_groups=mesh['dp'=4,'y'=4,'zh'=4,'zl'=4,'c'=2] {'zh'}, dimensions={0}, use_global_device_ids=true | all-gather | bytes 204800 | tf_op jit(solution)/shard_map/all_gather | solution.py:46
  173.9 10.4 %all_gather.31 = bf16[128,2560]{1,0:T(8,128)(2,1)S(1)} all-gather(bf16[32,2560]{1,0:T(8,128)(2,1)S(1)} %all_gather.30), channel_id=1, replica_groups=mesh['dp'=4,'y'=4,'zh'=4,'zl'=4,'c'=2] {'y'}, dimensions={0}, use_global_device_ids=true | all-gather | bytes 819200 | tf_op jit(solution)/shard_map/all_gather | solution.py:47
  185.3 20.4 %all-to-all-start.1 = ((f32[128,1,20]{2,1,0:T(1,128)}), f32[128,1,20]{2,1,0:T(1,128)S(1)}, u32[]{:S(2)}, u32[]{:S(2)}) async-start(f32[128,1,20]{2,1,0:T(1,128)} %bitcast.51), calls=%async_computation.1 | async-start | bytes 131072 | tf_op jit(solution)/shard_map/all_to_all | solution.py:170
  205.8 14.3 %all-to-all-done.1 = f32[128,1,20]{2,1,0:T(1,128)S(1)} async-done(((f32[128,1,20]{2,1,0:T(1,128)}), f32[128,1,20]{2,1,0:T(1,128)S(1)}, u32[]{:S(2)}, u32[]{:S(2)}) %all-to-all-start.1) | async-done | bytes 10272 | tf_op jit(solution)/shard_map/all_to_all | solution.py:170
  222.7 42.5 %all_to_all.24 = bf16[6,16,2560]{2,0,1:T(8,128)(2,1)S(1)} all-to-all(bf16[6,16,2560]{2,0,1:T(8,128)(2,1)S(1)} %copy.279), channel_id=1, replica_groups=mesh['dp'=4,'y'=4,'zh'=4,'zl'=4,'c'=2] {'y','zh'}, dimensions={1} | all-to-all | bytes 983040 | tf_op jit(solution)/shard_map/all_to_all | solution.py:198
  265.3 4.8 %collective-permute-start = (bf16[1,6,16,2560]{3,2,1,0:T(8,128)(2,1)S(1)}, bf16[1,6,16,2560]{3,2,1,0:T(8,128)(2,1)S(1)}, u32[]{:S(2)}, u32[]{:S(2)}) collective-permute-start(bf16[1,6,16,2560]{3,2,1,0:T(8,128)(2,1)S(1)} %bitcast.158), channel_id=1, source_target_pairs={{0,2},{2,4},{4,6},{6,0},{1,3},{3,5},{5,7},{7,1},{8,10},{10,12},{12... | collective-permute-start | bytes 1474568 | tf_op jit(solution)/shard_map/ppermute | solution.py:27
  272.0 3.1 collective-permute-start.2
  275.2 7.2 %collective-permute-done = bf16[1,6,16,2560]{3,2,1,0:T(8,128)(2,1)S(1)} collective-permute-done((bf16[1,6,16,2560]{3,2,1,0:T(8,128)(2,1)S(1)}, bf16[1,6,16,2560]{3,2,1,0:T(8,128)(2,1)S(1)}, u32[]{:S(2)}, u32[]{:S(2)}) %collective-permute-start) | collective-permute-done | bytes 491552 | tf_op jit(solution)/shard_map/ppermute | solution.py:27
  282.4 29.0 %collective-permute-done.1 = bf16[1,6,16,2560]{3,2,1,0:T(8,128)(2,1)S(1)} collective-permute-done((bf16[1,6,16,2560]{3,2,1,0:T(8,128)(2,1)S(1)}, bf16[1,6,16,2560]{3,2,1,0:T(8,128)(2,1)S(1)}, u32[]{:S(2)}, u32[]{:S(2)}) %collective-permute-start.1) | collective-permute-done | bytes 491552 | tf_op jit(solution)/shard_map/ppermute | solution.py:27
  315.4 3.9 collective-permute-start.3
  319.4 3.4 collective-permute-done.3
  325.6 4.8 %convolution_convert_fusion = bf16[384,2560]{1,0:T(8,128)(2,1)} fusion(bf16[192,2560]{1,0:T(8,128)(2,1)S(1)} %copy-done, f32[384,192]{0,1:T(8,128)} %fusion.9, bf16[384,2560]{1,0:T(8,128)(2,1)} %bitcast.175, bf16[2,192,2560]{2,1,0:T(8,128)(2,1)} %param.26), kind=kOutput, calls=%fused_computation.2 | convolution fusion | flops 756400128 | bytes 6193152 | tf_op jit(solution)/shard_map/dot_general | solution.py:214
  330.4 3.9 convert.26
  340.5 4.6 %convolution_convert_fusion.1 = bf16[384,2560]{1,0:T(8,128)(2,1)} fusion(bf16[192,2560]{1,0:T(8,128)(2,1)S(1)} %copy-done, bf16[384,2560]{1,0:T(8,128)(2,1)} %bitcast.156, bf16[2,192,2560]{2,1,0:T(8,128)(2,1)S(1)} %copy-done.10, f32[384,192]{0,1:T(8,128)} %fusion.15), kind=kOutput, calls=%fused_computation.3 | convolution fusion | flops 756400128 | bytes 6193152 | tf_op jit(solution)/shard_map/dot_general | solution.py:214
  345.0 3.3 fusion
  351.5 5.0 %collective-permute-start.6 = (bf16[6,16,2560]{2,1,0:T(8,128)(2,1)}, bf16[6,16,2560]{2,1,0:T(8,128)(2,1)}, u32[]{:S(2)}, u32[]{:S(2)}) collective-permute-start(bf16[6,16,2560]{2,1,0:T(8,128)(2,1)} %get-tuple-element.33), channel_id=1, source_target_pairs={{0,4},{2,6},{4,0},{6,2},{1,5},{3,7},{5,1},{7,3},{8,12},{10,14},{12... | collective-permute-start | bytes 1474568 | tf_op jit(solution)/shard_map/ppermute | solution.py:39
  356.5 3.4 collective-permute-start.7
  359.9 4.5 %collective-permute-done.5 = bf16[6,16,2560]{2,1,0:T(8,128)(2,1)} collective-permute-done((bf16[6,16,2560]{2,1,0:T(8,128)(2,1)}, bf16[6,16,2560]{2,1,0:T(8,128)(2,1)}, u32[]{:S(2)}, u32[]{:S(2)}) %collective-permute-start.5) | collective-permute-done | bytes 491552 | tf_op jit(solution)/shard_map/ppermute | solution.py:39
  364.4 29.7 %collective-permute-done.6 = bf16[6,16,2560]{2,1,0:T(8,128)(2,1)} collective-permute-done((bf16[6,16,2560]{2,1,0:T(8,128)(2,1)}, bf16[6,16,2560]{2,1,0:T(8,128)(2,1)}, u32[]{:S(2)}, u32[]{:S(2)}) %collective-permute-start.6) | collective-permute-done | bytes 491552 | tf_op jit(solution)/shard_map/ppermute | solution.py:39
  394.1 4.1 collective-permute-done.7
  401.0 3.6 all-to-all-start.3
  405.1 2.9 gather_fusion.1
  408.3 32.5 %all-to-all-done.3 = bf16[6,16,2560]{2,0,1:T(8,128)(2,1)S(1)} async-done(((bf16[6,16,2560]{2,0,1:T(8,128)(2,1)}), bf16[6,16,2560]{2,0,1:T(8,128)(2,1)S(1)}, u32[]{:S(2)}, u32[]{:S(2)}) %all-to-all-start.3) | async-done | bytes 491552 | tf_op jit(solution)/shard_map/all_to_all | solution.py:221
  (120 shorter events, 38.0 us)
Async XLA Ops:
  0.0 325.6 %copy-start = (bf16[192,2560]{1,0:T(8,128)(2,1)S(1)}, bf16[192,2560]{1,0:T(8,128)(2,1)}, u32[]{:S(2)}) copy-start(bf16[192,2560]{1,0:T(8,128)(2,1)} %param.27) | copy-start | bytes 2949124
  53.2 23.1 %copy-start.5 = (bf16[1,2560]{1,0:T(2,128)(2,1)S(1)}, bf16[1,2560]{1,0:T(2,128)(2,1)}, u32[]{:S(2)}) copy-start(bf16[1,2560]{1,0:T(2,128)(2,1)} %param.17) | copy-start | bytes 15364
  53.2 23.1 %copy-start.7 = (bf16[1,1024]{1,0:T(2,128)(2,1)S(1)}, bf16[1,1024]{1,0:T(2,128)(2,1)}, u32[]{:S(2)}) copy-start(bf16[1,1024]{1,0:T(2,128)(2,1)} %param.18) | copy-start | bytes 6148
  53.2 23.4 %copy-start.3 = (s32[64,6]{0,1:T(8,128)S(1)}, s32[64,6]{0,1:T(8,128)}, u32[]{:S(2)}) copy-start(s32[64,6]{0,1:T(8,128)} %param.25) | copy-start | bytes 4612
  55.8 85.1 %all-to-all-start = ((bf16[128,1,4,5,131]{4,2,3,1,0:T(4,128)(2,1)}), bf16[128,1,4,5,131]{4,2,3,1,0:T(4,128)(2,1)S(1)}, u32[]{:S(2)}, u32[]{:S(2)}) async-start(bf16[128,1,4,5,131]{4,2,3,1,0:T(4,128)(2,1)} %copy.270), calls=%async_computation | async-start | bytes 2621440 | tf_op jit(solution)/shard_map/all_to_all | solution.py:164
  144.6 39.7 %copy-start.4 = (bf16[2560,20]{0,1:T(8,128)(2,1)S(1)}, bf16[2560,20]{0,1:T(8,128)(2,1)}, u32[]{:S(2)}) copy-start(bf16[2560,20]{0,1:T(8,128)(2,1)} %param.22) | copy-start | bytes 307204
  145.0 60.7 %copy-start.2 = (bf16[64,2560]{1,0:T(8,128)(2,1)S(1)}, bf16[64,2560]{1,0:T(8,128)(2,1)}, u32[]{:S(2)}) copy-start(bf16[64,2560]{1,0:T(8,128)(2,1)} %param.16) | copy-start | bytes 983044
  145.8 60.0 %copy-start.6 = (bf16[2560]{0:T(1024)(128)(2,1)S(1)}, bf16[2560]{0:T(1024)(128)(2,1)}, u32[]{:S(2)}) copy-start(bf16[2560]{0:T(1024)(128)(2,1)} %param.23) | copy-start | bytes 15364
  185.3 34.8 %all-to-all-start.1 = ((f32[128,1,20]{2,1,0:T(1,128)}), f32[128,1,20]{2,1,0:T(1,128)S(1)}, u32[]{:S(2)}, u32[]{:S(2)}) async-start(f32[128,1,20]{2,1,0:T(1,128)} %bitcast.51), calls=%async_computation.1 | async-start | bytes 131072 | tf_op jit(solution)/shard_map/all_to_all | solution.py:170
  265.3 17.1 %collective-permute-start = (bf16[1,6,16,2560]{3,2,1,0:T(8,128)(2,1)S(1)}, bf16[1,6,16,2560]{3,2,1,0:T(8,128)(2,1)S(1)}, u32[]{:S(2)}, u32[]{:S(2)}) collective-permute-start(bf16[1,6,16,2560]{3,2,1,0:T(8,128)(2,1)S(1)} %bitcast.158), channel_id=1, source_target_pairs={{0,2},{2,4},{4,6},{6,0},{1,3},{3,5},{5,7},{7,1},{8,10},{10,12},{12... | collective-permute-start | bytes 1474568 | tf_op jit(solution)/shard_map/ppermute | solution.py:27
  270.1 41.3 %collective-permute-start.1 = (bf16[1,6,16,2560]{3,2,1,0:T(8,128)(2,1)S(1)}, bf16[1,6,16,2560]{3,2,1,0:T(8,128)(2,1)S(1)}, u32[]{:S(2)}, u32[]{:S(2)}) collective-permute-start(bf16[1,6,16,2560]{3,2,1,0:T(8,128)(2,1)S(1)} %bitcast.159), channel_id=1, source_target_pairs={{0,4},{2,6},{4,0},{6,2},{1,5},{3,7},{5,1},{7,3},{8,12},{10,14},{12... | collective-permute-start | bytes 1474568 | tf_op jit(solution)/shard_map/ppermute | solution.py:27
  272.0 39.4 %collective-permute-start.2 = (bf16[1,6,16,2560]{3,2,1,0:T(8,128)(2,1)S(1)}, bf16[1,6,16,2560]{3,2,1,0:T(8,128)(2,1)S(1)}, u32[]{:S(2)}, u32[]{:S(2)}) collective-permute-start(bf16[1,6,16,2560]{3,2,1,0:T(8,128)(2,1)S(1)} %bitcast.160), channel_id=1, source_target_pairs={{0,6},{2,0},{4,2},{6,4},{1,7},{3,1},{5,3},{7,5},{8,14},{10,8},{12,... | collective-permute-start | bytes 1474568 | tf_op jit(solution)/shard_map/ppermute | solution.py:27
  315.2 8.9 %copy-start.8 = (bf16[2,192,2560]{2,1,0:T(8,128)(2,1)S(1)}, bf16[2,192,2560]{2,1,0:T(8,128)(2,1)}, u32[]{:S(2)}) copy-start(bf16[2,192,2560]{2,1,0:T(8,128)(2,1)} %param.26) | copy-start | bytes 5898244
  315.4 7.3 %collective-permute-start.3 = (bf16[4,6,16,2560]{3,2,1,0:T(8,128)(2,1)S(1)}, bf16[4,6,16,2560]{3,2,1,0:T(8,128)(2,1)S(1)}, u32[]{:S(2)}, u32[]{:S(2)}) collective-permute-start(bf16[4,6,16,2560]{3,2,1,0:T(8,128)(2,1)S(1)} %broadcast_select_fusion), channel_id=1, source_target_pairs={{0,1},{1,0},{2,3},{3,2},{4,5},{5,4},{6,7},{7,6},{8,9},{9,8},{10,11... | collective-permute-start | bytes 5898248 | tf_op jit(solution)/shard_map/ppermute | solution.py:202
  322.8 1.3 copy-start.11
  334.3 10.7 %collective-permute-start.4 = (f32[4,6,16,2560]{3,2,1,0:T(8,128)}, f32[4,6,16,2560]{3,2,1,0:T(8,128)}, u32[]{:S(2)}, u32[]{:S(2)}) collective-permute-start(f32[4,6,16,2560]{3,2,1,0:T(8,128)} %convert.26), channel_id=1, source_target_pairs={{0,1},{1,0},{2,3},{3,2},{4,5},{5,4},{6,7},{7,6},{8,9},{9,8},{10,11... | collective-permute-start | bytes 11796488 | tf_op jit(solution)/shard_map/ppermute | solution.py:219
  336.7 2.3 copy-start.9
  336.9 1.3 copy-start.1
  338.9 1.5 copy-start.10
  349.6 14.9 %collective-permute-start.5 = (bf16[6,16,2560]{2,1,0:T(8,128)(2,1)}, bf16[6,16,2560]{2,1,0:T(8,128)(2,1)}, u32[]{:S(2)}, u32[]{:S(2)}) collective-permute-start(bf16[6,16,2560]{2,1,0:T(8,128)(2,1)} %get-tuple-element.31), channel_id=1, source_target_pairs={{0,2},{2,4},{4,6},{6,0},{1,3},{3,5},{5,7},{7,1},{8,10},{10,12},{12... | collective-permute-start | bytes 1474568 | tf_op jit(solution)/shard_map/ppermute | solution.py:39
  351.5 42.6 %collective-permute-start.6 = (bf16[6,16,2560]{2,1,0:T(8,128)(2,1)}, bf16[6,16,2560]{2,1,0:T(8,128)(2,1)}, u32[]{:S(2)}, u32[]{:S(2)}) collective-permute-start(bf16[6,16,2560]{2,1,0:T(8,128)(2,1)} %get-tuple-element.33), channel_id=1, source_target_pairs={{0,4},{2,6},{4,0},{6,2},{1,5},{3,7},{5,1},{7,3},{8,12},{10,14},{12... | collective-permute-start | bytes 1474568 | tf_op jit(solution)/shard_map/ppermute | solution.py:39
  356.5 41.7 %collective-permute-start.7 = (bf16[6,16,2560]{2,1,0:T(8,128)(2,1)}, bf16[6,16,2560]{2,1,0:T(8,128)(2,1)}, u32[]{:S(2)}, u32[]{:S(2)}) collective-permute-start(bf16[6,16,2560]{2,1,0:T(8,128)(2,1)} %get-tuple-element.32), channel_id=1, source_target_pairs={{0,6},{2,0},{4,2},{6,4},{1,7},{3,1},{5,3},{7,5},{8,14},{10,8},{12,... | collective-permute-start | bytes 1474568 | tf_op jit(solution)/shard_map/ppermute | solution.py:39
  399.8 5.0 %copy-start.12 = (bf16[2560,64]{0,1:T(8,128)(2,1)S(1)}, bf16[2560,64]{0,1:T(8,128)(2,1)}, u32[]{:S(2)}) copy-start(bf16[2560,64]{0,1:T(8,128)(2,1)} %param.24) | copy-start | bytes 983044
  401.0 39.9 %all-to-all-start.3 = ((bf16[6,16,2560]{2,0,1:T(8,128)(2,1)}), bf16[6,16,2560]{2,0,1:T(8,128)(2,1)S(1)}, u32[]{:S(2)}, u32[]{:S(2)}) async-start(bf16[6,16,2560]{2,0,1:T(8,128)(2,1)} %copy.284), calls=%async_computation.3 | async-start | bytes 1310720 | tf_op jit(solution)/shard_map/all_to_all | solution.py:221

commit v10 on v8

--- a/solution.py
+++ b/solution.py
@@ -159,9 +159,10 @@
         ),
         axis=-1,
     ).astype(jnp.bfloat16)
-    packed = packed.reshape((tensor_count, dec_rows) + packed.shape[1:])
+    part_shape = packed.shape[1:]
+    packed = packed.reshape(tensor_count, dec_rows, -1)
     parts = lax.all_to_all(packed, TENSOR, split_axis=0, concat_axis=0, tiled=True)
-    parts = jnp.swapaxes(parts, 0, 1)
+    parts = jnp.swapaxes(parts.reshape((tensor_count, dec_rows) + part_shape), 0, 1)
     context = finish_context(parts, queries, fresh_entries)
     context_all = gather_nested(context)
     projected = jnp.dot(context_all, out_proj, preferred_element_type=jnp.float32)

time: 433 us -> 431 us (level)
  the two profiles are of different devices: /device:TPU:33 before, /device:TPU:35 now
where the time goes in v10:
time: 431 us; the launch traced here: 430 us
  waiting for transfers between devices  165 us (38%)
  blocking collectives  117 us (27%)
  starting transfers between devices  70.3 us (16%)
  other arithmetic  34.4 us (8%)
  local copies, waits for them, and re-layouts  26.9 us (6%)
  matrix products  16.7 us (4%)
    all_gather x2, blocking collectives, gather_nested(): x = lax.all_gather(x, ('zh', 'zl'), axis=0, tiled=True)  46.6 us
    all_to_all x1, blocking collectives, local(): lax.all_to_all(slot_rows, EXPERT_AXES, split_axis=1, concat_axis=1, tiled...  42.5 us
    all_to_all x1, waiting for transfers between devices, local(): lax.all_to_all(packed, TENSOR, split_axis=0, concat_axis=0, tiled=True)  40 us
    ppermute x3, waiting for transfers between devices, scatter_sum_axis(): lax.ppermute(block, axis, [(i, (i + k) % count) for i in range(count)])  38.4 us
    ppermute x3, waiting for transfers between devices, gather_axis(): lax.ppermute(x, axis, [(i, (i + k) % count) for i in range(count)])  36 us
    all_to_all x1, waiting for transfers between devices, local(): lax.all_to_all(slice_sum.astype(jnp.bfloat16), EXPERT_AXES, split_axis=1,...  32.5 us
    all_to_all x1, starting transfers between devices, local(): lax.all_to_all(packed, TENSOR, split_axis=0, concat_axis=0, tiled=True)  22 us
    all_gather x2, blocking collectives, gather_nested(): return lax.all_gather(x, 'y', axis=0, tiled=True)  21.2 us
  transfers between devices with their start and end apart: 11, of which 9 were waited for; matrix products, arithmetic and copies ran while one was open for 2% of the time, Pallas kernels for 0%

profile of v10, /device:TPU:35, one launch (start us, length us, event | category | flops | bytes accessed | tf_op | source)
XLA Modules:
  0.0 430.3 jit_solution(14583593296952785753)
XLA Ops:
  1.9 2.4 all-gather
  4.3 27.1 %all-gather.1 = bf16[16,2,2560]{2,1,0:T(2,128)(2,1)S(1)} all-gather(bf16[1,2,2560]{2,1,0:T(2,128)(2,1)S(1)} %bitcast.154), channel_id=1, replica_groups=mesh['dp'=4,'y'=4,'zh'=4,'zl'=4,'c'=2] {'zh','zl'}, dimensions={0}, use_global_device_ids=true | all-gather | bytes 174080 | tf_op jit(solution)/shard_map/all_gather | solution.py:45
  31.4 10.7 %all_gather.20 = bf16[128,2560]{1,0:T(8,128)(2,1)S(1)} all-gather(bf16[32,2560]{1,0:T(8,128)(2,1)S(1)} %reshape.603), channel_id=1, replica_groups=mesh['dp'=4,'y'=4,'zh'=4,'zl'=4,'c'=2] {'y'}, dimensions={0}, use_global_device_ids=true | all-gather | bytes 819200 | tf_op jit(solution)/shard_map/all_gather | solution.py:46
  51.5 22.0 %all-to-all-start = ((bf16[128,2,1310]{2,1,0:T(2,128)(2,1)}), bf16[128,2,1310]{2,1,0:T(2,128)(2,1)S(1)}, u32[]{:S(2)}, u32[]{:S(2)}) async-start(bf16[128,2,1310]{2,1,0:T(2,128)(2,1)} %reshape.631), calls=%async_computation | async-start | bytes 1441792 | tf_op jit(solution)/shard_map/all_to_all | solution.py:164
  74.0 40.0 %all-to-all-done = bf16[128,2,1310]{2,1,0:T(2,128)(2,1)S(1)} async-done(((bf16[128,2,1310]{2,1,0:T(2,128)(2,1)}), bf16[128,2,1310]{2,1,0:T(2,128)(2,1)S(1)}, u32[]{:S(2)}, u32[]{:S(2)}) %all-to-all-start) | async-done | bytes 670752 | tf_op jit(solution)/shard_map/all_to_all | solution.py:164
  116.1 5.6 %copy.237 = bf16[128,1,2620]{0,1,2:T(2,128)(2,1)S(1)} copy(bf16[128,1,2620]{2,1,0:T(2,128)(2,1)} %reshape.632) | data formatting | bytes 1341440 | tf_op jit(solution)/shard_map/all_to_all | solution.py:164
  121.8 14.0 %convert_reduce_fusion = f32[128,2620]{0,1:T(8,128)} fusion(bf16[128,1,2620]{0,1,2:T(2,128)(2,1)S(1)} %copy.237), kind=kLoop, calls=%fused_computation.144 | loop fusion | flops 335360 | bytes 2012160 | tf_op jit(solution)/shard_map/convert_element_type | solution.py:108
  135.8 2.4 reshape.560
  140.7 3.9 all-gather.2
  144.6 19.5 %all-gather.3 = bf16[16,2,2560]{2,1,0:T(2,128)(2,1)S(1)} all-gather(bf16[1,2,2560]{2,1,0:T(2,128)(2,1)S(1)} %bitcast.155), channel_id=1, replica_groups=mesh['dp'=4,'y'=4,'zh'=4,'zl'=4,'c'=2] {'zh','zl'}, dimensions={0}, use_global_device_ids=true | all-gather | bytes 174080 | tf_op jit(solution)/shard_map/all_gather | solution.py:45
  164.2 10.6 %all_gather.23 = bf16[128,2560]{1,0:T(8,128)(2,1)S(1)} all-gather(bf16[32,2560]{1,0:T(8,128)(2,1)S(1)} %reshape.607), channel_id=1, replica_groups=mesh['dp'=4,'y'=4,'zh'=4,'zl'=4,'c'=2] {'y'}, dimensions={0}, use_global_device_ids=true | all-gather | bytes 819200 | tf_op jit(solution)/shard_map/all_gather | solution.py:46
  175.7 18.4 %all-to-all-start.1 = ((f32[128,1,20]{2,1,0:T(1,128)}), f32[128,1,20]{2,1,0:T(1,128)S(1)}, u32[]{:S(2)}, u32[]{:S(2)}) async-start(f32[128,1,20]{2,1,0:T(1,128)} %bitcast.48), calls=%async_computation.1 | async-start | bytes 131072 | tf_op jit(solution)/shard_map/all_to_all | solution.py:170
  194.2 14.3 %all-to-all-done.1 = f32[128,1,20]{2,1,0:T(1,128)S(1)} async-done(((f32[128,1,20]{2,1,0:T(1,128)}), f32[128,1,20]{2,1,0:T(1,128)S(1)}, u32[]{:S(2)}, u32[]{:S(2)}) %all-to-all-start.1) | async-done | bytes 10272 | tf_op jit(solution)/shard_map/all_to_all | solution.py:170
  211.0 42.5 %all_to_all.24 = bf16[6,16,2560]{2,0,1:T(8,128)(2,1)S(1)} all-to-all(bf16[6,16,2560]{2,0,1:T(8,128)(2,1)S(1)} %copy.247), channel_id=1, replica_groups=mesh['dp'=4,'y'=4,'zh'=4,'zl'=4,'c'=2] {'y','zh'}, dimensions={1} | all-to-all | bytes 983040 | tf_op jit(solution)/shard_map/all_to_all | solution.py:198
  253.7 4.8 %collective-permute-start = (bf16[1,6,16,2560]{3,2,1,0:T(8,128)(2,1)S(1)}, bf16[1,6,16,2560]{3,2,1,0:T(8,128)(2,1)S(1)}, u32[]{:S(2)}, u32[]{:S(2)}) collective-permute-start(bf16[1,6,16,2560]{3,2,1,0:T(8,128)(2,1)S(1)} %bitcast.141), channel_id=1, source_target_pairs={{0,2},{2,4},{4,6},{6,0},{1,3},{3,5},{5,7},{7,1},{8,10},{10,12},{12... | collective-permute-start | bytes 1474568 | tf_op jit(solution)/shard_map/ppermute | solution.py:27
  260.4 3.3 collective-permute-start.2
  263.8 7.0 %collective-permute-done = bf16[1,6,16,2560]{3,2,1,0:T(8,128)(2,1)S(1)} collective-permute-done((bf16[1,6,16,2560]{3,2,1,0:T(8,128)(2,1)S(1)}, bf16[1,6,16,2560]{3,2,1,0:T(8,128)(2,1)S(1)}, u32[]{:S(2)}, u32[]{:S(2)}) %collective-permute-start) | collective-permute-done | bytes 491552 | tf_op jit(solution)/shard_map/ppermute | solution.py:27
  270.8 29.0 %collective-permute-done.1 = bf16[1,6,16,2560]{3,2,1,0:T(8,128)(2,1)S(1)} collective-permute-done((bf16[1,6,16,2560]{3,2,1,0:T(8,128)(2,1)S(1)}, bf16[1,6,16,2560]{3,2,1,0:T(8,128)(2,1)S(1)}, u32[]{:S(2)}, u32[]{:S(2)}) %collective-permute-start.1) | collective-permute-done | bytes 491552 | tf_op jit(solution)/shard_map/ppermute | solution.py:27
  303.8 3.7 collective-permute-start.3
  307.6 3.6 collective-permute-done.3
  314.0 4.8 %convolution_convert_fusion = bf16[384,2560]{1,0:T(8,128)(2,1)} fusion(bf16[192,2560]{1,0:T(8,128)(2,1)S(1)} %copy-done, f32[384,192]{0,1:T(8,128)} %fusion.8, bf16[384,2560]{1,0:T(8,128)(2,1)} %bitcast.161, bf16[2,192,2560]{2,1,0:T(8,128)(2,1)} %param.26), kind=kOutput, calls=%fused_computation.2 | convolution fusion | flops 756400128 | bytes 6193152 | tf_op jit(solution)/shard_map/dot_general | solution.py:214
  318.8 3.9 convert.21
  328.8 4.6 %convolution_convert_fusion.1 = bf16[384,2560]{1,0:T(8,128)(2,1)} fusion(bf16[192,2560]{1,0:T(8,128)(2,1)S(1)} %copy-done, bf16[384,2560]{1,0:T(8,128)(2,1)} %bitcast.139, bf16[2,192,2560]{2,1,0:T(8,128)(2,1)S(1)} %copy-done.11, f32[384,192]{0,1:T(8,128)} %fusion.14), kind=kOutput, calls=%fused_computation.3 | convolution fusion | flops 756400128 | bytes 6193152 | tf_op jit(solution)/shard_map/dot_general | solution.py:214
  333.4 3.3 fusion
  339.8 5.0 %collective-permute-start.6 = (bf16[6,16,2560]{2,1,0:T(8,128)(2,1)}, bf16[6,16,2560]{2,1,0:T(8,128)(2,1)}, u32[]{:S(2)}, u32[]{:S(2)}) collective-permute-start(bf16[6,16,2560]{2,1,0:T(8,128)(2,1)} %get-tuple-element.35), channel_id=1, source_target_pairs={{0,4},{2,6},{4,0},{6,2},{1,5},{3,7},{5,1},{7,3},{8,12},{10,14},{12... | collective-permute-start | bytes 1474568 | tf_op jit(solution)/shard_map/ppermute | solution.py:39
  344.9 3.4 collective-permute-start.7
  348.2 4.5 %collective-permute-done.5 = bf16[6,16,2560]{2,1,0:T(8,128)(2,1)} collective-permute-done((bf16[6,16,2560]{2,1,0:T(8,128)(2,1)}, bf16[6,16,2560]{2,1,0:T(8,128)(2,1)}, u32[]{:S(2)}, u32[]{:S(2)}) %collective-permute-start.5) | collective-permute-done | bytes 491552 | tf_op jit(solution)/shard_map/ppermute | solution.py:39
  352.8 29.7 %collective-permute-done.6 = bf16[6,16,2560]{2,1,0:T(8,128)(2,1)} collective-permute-done((bf16[6,16,2560]{2,1,0:T(8,128)(2,1)}, bf16[6,16,2560]{2,1,0:T(8,128)(2,1)}, u32[]{:S(2)}, u32[]{:S(2)}) %collective-permute-start.6) | collective-permute-done | bytes 491552 | tf_op jit(solution)/shard_map/ppermute | solution.py:39
  382.4 4.1 collective-permute-done.7
  389.3 3.6 all-to-all-start.3
  393.5 2.9 gather_fusion.1
  396.7 32.5 %all-to-all-done.3 = bf16[6,16,2560]{2,0,1:T(8,128)(2,1)S(1)} async-done(((bf16[6,16,2560]{2,0,1:T(8,128)(2,1)}), bf16[6,16,2560]{2,0,1:T(8,128)(2,1)S(1)}, u32[]{:S(2)}, u32[]{:S(2)}) %all-to-all-start.3) | async-done | bytes 491552 | tf_op jit(solution)/shard_map/all_to_all | solution.py:221
  (126 shorter events, 42.4 us)
Async XLA Ops:
  0.0 314.0 %copy-start = (bf16[192,2560]{1,0:T(8,128)(2,1)S(1)}, bf16[192,2560]{1,0:T(8,128)(2,1)}, u32[]{:S(2)}) copy-start(bf16[192,2560]{1,0:T(8,128)(2,1)} %param.27) | copy-start | bytes 2949124
  49.6 24.0 %copy-start.6 = (bf16[1,2560]{1,0:T(2,128)(2,1)S(1)}, bf16[1,2560]{1,0:T(2,128)(2,1)}, u32[]{:S(2)}) copy-start(bf16[1,2560]{1,0:T(2,128)(2,1)} %param.17) | copy-start | bytes 15364
  49.6 24.0 %copy-start.4 = (s32[64,6]{0,1:T(8,128)S(1)}, s32[64,6]{0,1:T(8,128)}, u32[]{:S(2)}) copy-start(s32[64,6]{0,1:T(8,128)} %param.25) | copy-start | bytes 4612
  49.6 24.3 %copy-start.8 = (bf16[1,1024]{1,0:T(2,128)(2,1)S(1)}, bf16[1,1024]{1,0:T(2,128)(2,1)}, u32[]{:S(2)}) copy-start(bf16[1,1024]{1,0:T(2,128)(2,1)} %param.18) | copy-start | bytes 6148
  51.5 62.5 %all-to-all-start = ((bf16[128,2,1310]{2,1,0:T(2,128)(2,1)}), bf16[128,2,1310]{2,1,0:T(2,128)(2,1)S(1)}, u32[]{:S(2)}, u32[]{:S(2)}) async-start(bf16[128,2,1310]{2,1,0:T(2,128)(2,1)} %reshape.631), calls=%async_computation | async-start | bytes 1441792 | tf_op jit(solution)/shard_map/all_to_all | solution.py:164
  138.3 1.6 copy-start.1
  139.6 35.1 %copy-start.5 = (bf16[2560,20]{0,1:T(8,128)(2,1)S(1)}, bf16[2560,20]{0,1:T(8,128)(2,1)}, u32[]{:S(2)}) copy-start(bf16[2560,20]{0,1:T(8,128)(2,1)} %param.22) | copy-start | bytes 307204
  139.6 54.4 %copy-start.3 = (bf16[64,2560]{1,0:T(8,128)(2,1)S(1)}, bf16[64,2560]{1,0:T(8,128)(2,1)}, u32[]{:S(2)}) copy-start(bf16[64,2560]{1,0:T(8,128)(2,1)} %param.16) | copy-start | bytes 983044
  140.6 53.6 %copy-start.7 = (bf16[2560]{0:T(1024)(128)(2,1)S(1)}, bf16[2560]{0:T(1024)(128)(2,1)}, u32[]{:S(2)}) copy-start(bf16[2560]{0:T(1024)(128)(2,1)} %param.23) | copy-start | bytes 15364
  175.7 32.8 %all-to-all-start.1 = ((f32[128,1,20]{2,1,0:T(1,128)}), f32[128,1,20]{2,1,0:T(1,128)S(1)}, u32[]{:S(2)}, u32[]{:S(2)}) async-start(f32[128,1,20]{2,1,0:T(1,128)} %bitcast.48), calls=%async_computation.1 | async-start | bytes 131072 | tf_op jit(solution)/shard_map/all_to_all | solution.py:170
  253.7 17.1 %collective-permute-start = (bf16[1,6,16,2560]{3,2,1,0:T(8,128)(2,1)S(1)}, bf16[1,6,16,2560]{3,2,1,0:T(8,128)(2,1)S(1)}, u32[]{:S(2)}, u32[]{:S(2)}) collective-permute-start(bf16[1,6,16,2560]{3,2,1,0:T(8,128)(2,1)S(1)} %bitcast.141), channel_id=1, source_target_pairs={{0,2},{2,4},{4,6},{6,0},{1,3},{3,5},{5,7},{7,1},{8,10},{10,12},{12... | collective-permute-start | bytes 1474568 | tf_op jit(solution)/shard_map/ppermute | solution.py:27
  258.5 41.3 %collective-permute-start.1 = (bf16[1,6,16,2560]{3,2,1,0:T(8,128)(2,1)S(1)}, bf16[1,6,16,2560]{3,2,1,0:T(8,128)(2,1)S(1)}, u32[]{:S(2)}, u32[]{:S(2)}) collective-permute-start(bf16[1,6,16,2560]{3,2,1,0:T(8,128)(2,1)S(1)} %bitcast.142), channel_id=1, source_target_pairs={{0,4},{2,6},{4,0},{6,2},{1,5},{3,7},{5,1},{7,3},{8,12},{10,14},{12... | collective-permute-start | bytes 1474568 | tf_op jit(solution)/shard_map/ppermute | solution.py:27
  260.4 39.4 %collective-permute-start.2 = (bf16[1,6,16,2560]{3,2,1,0:T(8,128)(2,1)S(1)}, bf16[1,6,16,2560]{3,2,1,0:T(8,128)(2,1)S(1)}, u32[]{:S(2)}, u32[]{:S(2)}) collective-permute-start(bf16[1,6,16,2560]{3,2,1,0:T(8,128)(2,1)S(1)} %bitcast.143), channel_id=1, source_target_pairs={{0,6},{2,0},{4,2},{6,4},{1,7},{3,1},{5,3},{7,5},{8,14},{10,8},{12,... | collective-permute-start | bytes 1474568 | tf_op jit(solution)/shard_map/ppermute | solution.py:27
  303.6 8.9 %copy-start.9 = (bf16[2,192,2560]{2,1,0:T(8,128)(2,1)S(1)}, bf16[2,192,2560]{2,1,0:T(8,128)(2,1)}, u32[]{:S(2)}) copy-start(bf16[2,192,2560]{2,1,0:T(8,128)(2,1)} %param.26) | copy-start | bytes 5898244
  303.8 7.3 %collective-permute-start.3 = (bf16[4,6,16,2560]{3,2,1,0:T(8,128)(2,1)S(1)}, bf16[4,6,16,2560]{3,2,1,0:T(8,128)(2,1)S(1)}, u32[]{:S(2)}, u32[]{:S(2)}) collective-permute-start(bf16[4,6,16,2560]{3,2,1,0:T(8,128)(2,1)S(1)} %broadcast_select_fusion), channel_id=1, source_target_pairs={{0,1},{1,0},{2,3},{3,2},{4,5},{5,4},{6,7},{7,6},{8,9},{9,8},{10,11... | collective-permute-start | bytes 5898248 | tf_op jit(solution)/shard_map/ppermute | solution.py:202
  311.2 1.3 copy-start.12
  322.7 10.7 %collective-permute-start.4 = (f32[4,6,16,2560]{3,2,1,0:T(8,128)}, f32[4,6,16,2560]{3,2,1,0:T(8,128)}, u32[]{:S(2)}, u32[]{:S(2)}) collective-permute-start(f32[4,6,16,2560]{3,2,1,0:T(8,128)} %convert.21), channel_id=1, source_target_pairs={{0,1},{1,0},{2,3},{3,2},{4,5},{5,4},{6,7},{7,6},{8,9},{9,8},{10,11... | collective-permute-start | bytes 11796488 | tf_op jit(solution)/shard_map/ppermute | solution.py:219
  325.0 2.3 copy-start.10
  325.3 1.3 copy-start.2
  327.3 1.5 copy-start.11
  337.9 14.8 %collective-permute-start.5 = (bf16[6,16,2560]{2,1,0:T(8,128)(2,1)}, bf16[6,16,2560]{2,1,0:T(8,128)(2,1)}, u32[]{:S(2)}, u32[]{:S(2)}) collective-permute-start(bf16[6,16,2560]{2,1,0:T(8,128)(2,1)} %get-tuple-element.33), channel_id=1, source_target_pairs={{0,2},{2,4},{4,6},{6,0},{1,3},{3,5},{5,7},{7,1},{8,10},{10,12},{12... | collective-permute-start | bytes 1474568 | tf_op jit(solution)/shard_map/ppermute | solution.py:39
  339.8 42.6 %collective-permute-start.6 = (bf16[6,16,2560]{2,1,0:T(8,128)(2,1)}, bf16[6,16,2560]{2,1,0:T(8,128)(2,1)}, u32[]{:S(2)}, u32[]{:S(2)}) collective-permute-start(bf16[6,16,2560]{2,1,0:T(8,128)(2,1)} %get-tuple-element.35), channel_id=1, source_target_pairs={{0,4},{2,6},{4,0},{6,2},{1,5},{3,7},{5,1},{7,3},{8,12},{10,14},{12... | collective-permute-start | bytes 1474568 | tf_op jit(solution)/shard_map/ppermute | solution.py:39
  344.9 41.7 %collective-permute-start.7 = (bf16[6,16,2560]{2,1,0:T(8,128)(2,1)}, bf16[6,16,2560]{2,1,0:T(8,128)(2,1)}, u32[]{:S(2)}, u32[]{:S(2)}) collective-permute-start(bf16[6,16,2560]{2,1,0:T(8,128)(2,1)} %get-tuple-element.34), channel_id=1, source_target_pairs={{0,6},{2,0},{4,2},{6,4},{1,7},{3,1},{5,3},{7,5},{8,14},{10,8},{12,... | collective-permute-start | bytes 1474568 | tf_op jit(solution)/shard_map/ppermute | solution.py:39
  388.2 5.0 %copy-start.13 = (bf16[2560,64]{0,1:T(8,128)(2,1)S(1)}, bf16[2560,64]{0,1:T(8,128)(2,1)}, u32[]{:S(2)}) copy-start(bf16[2560,64]{0,1:T(8,128)(2,1)} %param.24) | copy-start | bytes 983044
  389.3 39.9 %all-to-all-start.3 = ((bf16[6,16,2560]{2,0,1:T(8,128)(2,1)}), bf16[6,16,2560]{2,0,1:T(8,128)(2,1)S(1)}, u32[]{:S(2)}, u32[]{:S(2)}) async-start(bf16[6,16,2560]{2,0,1:T(8,128)(2,1)} %copy.252), calls=%async_computation.3 | async-start | bytes 1310720 | tf_op jit(solution)/shard_map/all_to_all | solution.py:221

commit v11 on v8

--- a/solution.py
+++ b/solution.py
@@ -93,30 +93,30 @@
 def finish_context(parts, local_queries, local_entries):
     entry_count = local_queries.shape[0]
     key_value_width = KEY_VALUE_HEADS * HEAD_SIZE
-    query_vector = local_queries.reshape(
-        entry_count, KEY_VALUE_HEADS, QUERY_HEADS // KEY_VALUE_HEADS, HEAD_SIZE
-    )
+    query_groups = QUERY_HEADS // KEY_VALUE_HEADS
+    query_vector = local_queries.reshape(entry_count, KEY_VALUE_HEADS, query_groups, HEAD_SIZE)
     token_key = local_entries[:, :key_value_width].reshape(entry_count, KEY_VALUE_HEADS, HEAD_SIZE)
     token_value = (
         local_entries[:, key_value_width:]
-        .reshape(entry_count, KEY_VALUE_HEADS, HEAD_SIZE)
+        .reshape(entry_count, KEY_VALUE_HEADS, 1, HEAD_SIZE)
         .astype(jnp.float32)
     )
+    token_value = jnp.broadcast_to(
+        token_value, (entry_count, KEY_VALUE_HEADS, query_groups, HEAD_SIZE)
+    ).reshape(entry_count, QUERY_HEADS, HEAD_SIZE)
     own_score = jnp.einsum(
         "rhgd,rhd->rhg", query_vector, token_key, preferred_element_type=jnp.float32
-    ) * (1.0 / math.sqrt(HEAD_SIZE))
+    ).reshape(entry_count, QUERY_HEADS) * (1.0 / math.sqrt(HEAD_SIZE))
     parts = parts.astype(jnp.float32)
-    part_max = parts[..., 0] + parts[..., 1]
-    part_total = parts[..., 2]
-    part_accum = parts[..., 3:]
+    heads = QUERY_HEADS
+    part_max = parts[..., :heads] + parts[..., heads : 2 * heads]
+    part_total = parts[..., 2 * heads : 3 * heads]
+    part_accum = parts[..., 3 * heads :].reshape(parts.shape[:2] + (heads, HEAD_SIZE))
     joined = jnp.maximum(jnp.max(part_max, axis=1), own_score)
     coef = jnp.exp(part_max - joined[:, None])
     own_weight = jnp.exp(own_score - joined)
     totals = jnp.sum(coef * part_total, axis=1) + own_weight
-    accum = (
-        jnp.sum(coef[..., None] * part_accum, axis=1)
-        + own_weight[..., None] * token_value[:, :, None, :]
-    )
+    accum = jnp.sum(coef[..., None] * part_accum, axis=1) + own_weight[..., None] * token_value
     return (
         (accum / totals[..., None])
         .reshape(entry_count, QUERY_HEADS * HEAD_SIZE)
@@ -150,16 +150,17 @@
     rebase = jnp.where(
         request_max > 0.5 * NEG_FILL, jnp.exp(request_max - (max_high + max_low)), 0.0
     )
+    rows_out = request_max.shape[0]
     packed = jnp.concatenate(
         (
-            max_high[..., None],
-            max_low[..., None],
-            (request_total * rebase)[..., None],
-            request_accum * rebase[..., None],
+            max_high.reshape(rows_out, QUERY_HEADS),
+            max_low.reshape(rows_out, QUERY_HEADS),
+            (request_total * rebase).reshape(rows_out, QUERY_HEADS),
+            (request_accum * rebase[..., None]).reshape(rows_out, QUERY_HEADS * HEAD_SIZE),
         ),
         axis=-1,
     ).astype(jnp.bfloat16)
-    packed = packed.reshape((tensor_count, dec_rows) + packed.shape[1:])
+    packed = packed.reshape(tensor_count, dec_rows, -1)
     parts = lax.all_to_all(packed, TENSOR, split_axis=0, concat_axis=0, tiled=True)
     parts = jnp.swapaxes(parts, 0, 1)
     context = finish_context(parts, queries, fresh_entries)

time: 433 us -> 410 us (0.947)
  waiting for transfers between devices: 189 us -> 165 us
    all_to_all x1, waiting for transfers between devices: 64 us -> 39.9 us  [local(): lax.all_to_all(packed, TENSOR, split_axis=0, concat_axis=0, tiled=True)]
  transfers between devices with their start and end apart: 11 -> 11, of which waited for: 9 -> 9; matrix products, arithmetic and copies ran while one was open for 2% -> 3% of each run, Pallas kernels for 0% -> 0%
where the time goes in v11:
time: 410 us; the launch traced here: 409 us
  waiting for transfers between devices  165 us (40%)
  blocking collectives  117 us (29%)
  starting transfers between devices  70.2 us (17%)
  local copies, waits for them, and re-layouts  21 us (5%)
  other arithmetic  18.7 us (5%)
  matrix products  16.7 us (4%)
    all_gather x2, blocking collectives, gather_nested(): x = lax.all_gather(x, ('zh', 'zl'), axis=0, tiled=True)  46.6 us
    all_to_all x1, blocking collectives, local(): lax.all_to_all(slot_rows, EXPERT_AXES, split_axis=1, concat_axis=1, tiled...  42.5 us
    all_to_all x1, waiting for transfers between devices, local(): lax.all_to_all(packed, TENSOR, split_axis=0, concat_axis=0, tiled=True)  39.9 us
    ppermute x3, waiting for transfers between devices, scatter_sum_axis(): lax.ppermute(block, axis, [(i, (i + k) % count) for i in range(count)])  38.4 us
    ppermute x3, waiting for transfers between devices, gather_axis(): lax.ppermute(x, axis, [(i, (i + k) % count) for i in range(count)])  36.1 us
    all_to_all x1, waiting for transfers between devices, local(): lax.all_to_all(slice_sum.astype(jnp.bfloat16), EXPERT_AXES, split_axis=1,...  32.6 us
    all_to_all x1, starting transfers between devices, local(): lax.all_to_all(packed, TENSOR, split_axis=0, concat_axis=0, tiled=True)  22 us
    all_gather x2, blocking collectives, gather_nested(): return lax.all_gather(x, 'y', axis=0, tiled=True)  21.2 us
  transfers between devices with their start and end apart: 11, of which 9 were waited for; matrix products, arithmetic and copies ran while one was open for 3% of the time, Pallas kernels for 0%

profile of v11, /device:TPU:33, one launch (start us, length us, event | category | flops | bytes accessed | tf_op | source)
XLA Modules:
  0.0 408.6 jit_solution(14689525862067108942)
XLA Ops:
  1.9 2.4 all-gather
  4.3 27.1 %all-gather.1 = bf16[16,2,2560]{2,1,0:T(2,128)(2,1)S(1)} all-gather(bf16[1,2,2560]{2,1,0:T(2,128)(2,1)S(1)} %bitcast.158), channel_id=1, replica_groups=mesh['dp'=4,'y'=4,'zh'=4,'zl'=4,'c'=2] {'zh','zl'}, dimensions={0}, use_global_device_ids=true | all-gather | bytes 174080 | tf_op jit(solution)/shard_map/all_gather | solution.py:45
  31.4 10.7 %all_gather.20 = bf16[128,2560]{1,0:T(8,128)(2,1)S(1)} all-gather(bf16[32,2560]{1,0:T(8,128)(2,1)S(1)} %reshape.632), channel_id=1, replica_groups=mesh['dp'=4,'y'=4,'zh'=4,'zl'=4,'c'=2] {'y'}, dimensions={0}, use_global_device_ids=true | all-gather | bytes 819200 | tf_op jit(solution)/shard_map/all_gather | solution.py:46
  52.8 22.0 %all-to-all-start = ((bf16[128,2,1310]{2,1,0:T(2,128)(2,1)}), bf16[128,2,1310]{2,1,0:T(2,128)(2,1)S(1)}, u32[]{:S(2)}, u32[]{:S(2)}) async-start(bf16[128,2,1310]{2,1,0:T(2,128)(2,1)} %reshape.658), calls=%async_computation | async-start | bytes 1441792 | tf_op jit(solution)/shard_map/all_to_all | solution.py:164
  75.4 39.9 %all-to-all-done = bf16[128,2,1310]{2,1,0:T(2,128)(2,1)S(1)} async-done(((bf16[128,2,1310]{2,1,0:T(2,128)(2,1)}), bf16[128,2,1310]{2,1,0:T(2,128)(2,1)S(1)}, u32[]{:S(2)}, u32[]{:S(2)}) %all-to-all-start) | async-done | bytes 670752 | tf_op jit(solution)/shard_map/all_to_all | solution.py:164
  118.9 3.9 all-gather.2
  122.9 19.5 %all-gather.3 = bf16[16,2,2560]{2,1,0:T(2,128)(2,1)S(1)} all-gather(bf16[1,2,2560]{2,1,0:T(2,128)(2,1)S(1)} %bitcast.159), channel_id=1, replica_groups=mesh['dp'=4,'y'=4,'zh'=4,'zl'=4,'c'=2] {'zh','zl'}, dimensions={0}, use_global_device_ids=true | all-gather | bytes 174080 | tf_op jit(solution)/shard_map/all_gather | solution.py:45
  142.5 10.6 %all_gather.23 = bf16[128,2560]{1,0:T(8,128)(2,1)S(1)} all-gather(bf16[32,2560]{1,0:T(8,128)(2,1)S(1)} %reshape.636), channel_id=1, replica_groups=mesh['dp'=4,'y'=4,'zh'=4,'zl'=4,'c'=2] {'y'}, dimensions={0}, use_global_device_ids=true | all-gather | bytes 819200 | tf_op jit(solution)/shard_map/all_gather | solution.py:46
  154.0 18.4 %all-to-all-start.1 = ((f32[128,1,20]{2,1,0:T(1,128)}), f32[128,1,20]{2,1,0:T(1,128)S(1)}, u32[]{:S(2)}, u32[]{:S(2)}) async-start(f32[128,1,20]{2,1,0:T(1,128)} %bitcast.50), calls=%async_computation.1 | async-start | bytes 131072 | tf_op jit(solution)/shard_map/all_to_all | solution.py:170
  172.4 14.3 %all-to-all-done.1 = f32[128,1,20]{2,1,0:T(1,128)S(1)} async-done(((f32[128,1,20]{2,1,0:T(1,128)}), f32[128,1,20]{2,1,0:T(1,128)S(1)}, u32[]{:S(2)}, u32[]{:S(2)}) %all-to-all-start.1) | async-done | bytes 10272 | tf_op jit(solution)/shard_map/all_to_all | solution.py:170
  189.3 42.5 %all_to_all.24 = bf16[6,16,2560]{2,0,1:T(8,128)(2,1)S(1)} all-to-all(bf16[6,16,2560]{2,0,1:T(8,128)(2,1)S(1)} %copy.178), channel_id=1, replica_groups=mesh['dp'=4,'y'=4,'zh'=4,'zl'=4,'c'=2] {'y','zh'}, dimensions={1} | all-to-all | bytes 983040 | tf_op jit(solution)/shard_map/all_to_all | solution.py:198
  232.0 4.8 %collective-permute-start = (bf16[1,6,16,2560]{3,2,1,0:T(8,128)(2,1)S(1)}, bf16[1,6,16,2560]{3,2,1,0:T(8,128)(2,1)S(1)}, u32[]{:S(2)}, u32[]{:S(2)}) collective-permute-start(bf16[1,6,16,2560]{3,2,1,0:T(8,128)(2,1)S(1)} %bitcast.146), channel_id=1, source_target_pairs={{0,2},{2,4},{4,6},{6,0},{1,3},{3,5},{5,7},{7,1},{8,10},{10,12},{12... | collective-permute-start | bytes 1474568 | tf_op jit(solution)/shard_map/ppermute | solution.py:27
  236.8 1.9 collective-permute-start.1
  238.7 3.3 collective-permute-start.2
  242.0 7.0 %collective-permute-done = bf16[1,6,16,2560]{3,2,1,0:T(8,128)(2,1)S(1)} collective-permute-done((bf16[1,6,16,2560]{3,2,1,0:T(8,128)(2,1)S(1)}, bf16[1,6,16,2560]{3,2,1,0:T(8,128)(2,1)S(1)}, u32[]{:S(2)}, u32[]{:S(2)}) %collective-permute-start) | collective-permute-done | bytes 491552 | tf_op jit(solution)/shard_map/ppermute | solution.py:27
  249.1 29.0 %collective-permute-done.1 = bf16[1,6,16,2560]{3,2,1,0:T(8,128)(2,1)S(1)} collective-permute-done((bf16[1,6,16,2560]{3,2,1,0:T(8,128)(2,1)S(1)}, bf16[1,6,16,2560]{3,2,1,0:T(8,128)(2,1)S(1)}, u32[]{:S(2)}, u32[]{:S(2)}) %collective-permute-start.1) | collective-permute-done | bytes 491552 | tf_op jit(solution)/shard_map/ppermute | solution.py:27
  279.6 2.2 gather_fusion
  282.1 3.7 collective-permute-start.3
  285.8 3.6 collective-permute-done.3
  292.2 4.8 %convolution_convert_fusion = bf16[384,2560]{1,0:T(8,128)(2,1)} fusion(bf16[192,2560]{1,0:T(8,128)(2,1)S(1)} %copy-done, f32[384,192]{0,1:T(8,128)} %fusion.8, bf16[384,2560]{1,0:T(8,128)(2,1)} %bitcast.164, bf16[2,192,2560]{2,1,0:T(8,128)(2,1)} %param.26), kind=kOutput, calls=%fused_computation.2 | convolution fusion | flops 756400128 | bytes 6193152 | tf_op jit(solution)/shard_map/dot_general | solution.py:214
  297.0 3.9 convert.26
  301.0 2.3 collective-permute-start.4
  307.1 4.6 %convolution_convert_fusion.1 = bf16[384,2560]{1,0:T(8,128)(2,1)} fusion(bf16[192,2560]{1,0:T(8,128)(2,1)S(1)} %copy-done, bf16[384,2560]{1,0:T(8,128)(2,1)} %bitcast.144, bf16[2,192,2560]{2,1,0:T(8,128)(2,1)S(1)} %copy-done.10, f32[384,192]{0,1:T(8,128)} %fusion.14), kind=kOutput, calls=%fused_computation.3 | convolution fusion | flops 756400128 | bytes 6193152 | tf_op jit(solution)/shard_map/dot_general | solution.py:214
  311.7 3.3 fusion
  318.1 5.0 %collective-permute-start.6 = (bf16[6,16,2560]{2,1,0:T(8,128)(2,1)}, bf16[6,16,2560]{2,1,0:T(8,128)(2,1)}, u32[]{:S(2)}, u32[]{:S(2)}) collective-permute-start(bf16[6,16,2560]{2,1,0:T(8,128)(2,1)} %get-tuple-element.33), channel_id=1, source_target_pairs={{0,4},{2,6},{4,0},{6,2},{1,5},{3,7},{5,1},{7,3},{8,12},{10,14},{12... | collective-permute-start | bytes 1474568 | tf_op jit(solution)/shard_map/ppermute | solution.py:39
  323.1 3.4 collective-permute-start.7
  326.5 4.5 %collective-permute-done.5 = bf16[6,16,2560]{2,1,0:T(8,128)(2,1)} collective-permute-done((bf16[6,16,2560]{2,1,0:T(8,128)(2,1)}, bf16[6,16,2560]{2,1,0:T(8,128)(2,1)}, u32[]{:S(2)}, u32[]{:S(2)}) %collective-permute-start.5) | collective-permute-done | bytes 491552 | tf_op jit(solution)/shard_map/ppermute | solution.py:39
  331.0 29.7 %collective-permute-done.6 = bf16[6,16,2560]{2,1,0:T(8,128)(2,1)} collective-permute-done((bf16[6,16,2560]{2,1,0:T(8,128)(2,1)}, bf16[6,16,2560]{2,1,0:T(8,128)(2,1)}, u32[]{:S(2)}, u32[]{:S(2)}) %collective-permute-start.6) | collective-permute-done | bytes 491552 | tf_op jit(solution)/shard_map/ppermute | solution.py:39
  360.7 4.1 %collective-permute-done.7 = bf16[6,16,2560]{2,1,0:T(8,128)(2,1)} collective-permute-done((bf16[6,16,2560]{2,1,0:T(8,128)(2,1)}, bf16[6,16,2560]{2,1,0:T(8,128)(2,1)}, u32[]{:S(2)}, u32[]{:S(2)}) %collective-permute-start.7) | collective-permute-done | bytes 491552 | tf_op jit(solution)/shard_map/ppermute | solution.py:39
  367.6 3.6 all-to-all-start.3
  371.8 2.9 gather_fusion.1
  375.0 32.6 %all-to-all-done.3 = bf16[6,16,2560]{2,0,1:T(8,128)(2,1)S(1)} async-done(((bf16[6,16,2560]{2,0,1:T(8,128)(2,1)}), bf16[6,16,2560]{2,0,1:T(8,128)(2,1)S(1)}, u32[]{:S(2)}, u32[]{:S(2)}) %all-to-all-start.3) | async-done | bytes 491552 | tf_op jit(solution)/shard_map/all_to_all | solution.py:221
  (121 shorter events, 36.5 us)
Async XLA Ops:
  0.0 292.2 %copy-start = (bf16[192,2560]{1,0:T(8,128)(2,1)S(1)}, bf16[192,2560]{1,0:T(8,128)(2,1)}, u32[]{:S(2)}) copy-start(bf16[192,2560]{1,0:T(8,128)(2,1)} %param.27) | copy-start | bytes 2949124
  50.8 24.0 %copy-start.5 = (bf16[1,2560]{1,0:T(2,128)(2,1)S(1)}, bf16[1,2560]{1,0:T(2,128)(2,1)}, u32[]{:S(2)}) copy-start(bf16[1,2560]{1,0:T(2,128)(2,1)} %param.17) | copy-start | bytes 15364
  50.8 24.0 %copy-start.7 = (bf16[1,1024]{1,0:T(2,128)(2,1)S(1)}, bf16[1,1024]{1,0:T(2,128)(2,1)}, u32[]{:S(2)}) copy-start(bf16[1,1024]{1,0:T(2,128)(2,1)} %param.18) | copy-start | bytes 6148
  50.8 24.3 %copy-start.3 = (s32[64,6]{0,1:T(8,128)S(1)}, s32[64,6]{0,1:T(8,128)}, u32[]{:S(2)}) copy-start(s32[64,6]{0,1:T(8,128)} %param.25) | copy-start | bytes 4612
  52.8 62.5 %all-to-all-start = ((bf16[128,2,1310]{2,1,0:T(2,128)(2,1)}), bf16[128,2,1310]{2,1,0:T(2,128)(2,1)S(1)}, u32[]{:S(2)}, u32[]{:S(2)}) async-start(bf16[128,2,1310]{2,1,0:T(2,128)(2,1)} %reshape.658), calls=%async_computation | async-start | bytes 1441792 | tf_op jit(solution)/shard_map/all_to_all | solution.py:164
  117.9 35.1 %copy-start.4 = (bf16[2560,20]{0,1:T(8,128)(2,1)S(1)}, bf16[2560,20]{0,1:T(8,128)(2,1)}, u32[]{:S(2)}) copy-start(bf16[2560,20]{0,1:T(8,128)(2,1)} %param.22) | copy-start | bytes 307204
  118.0 54.3 %copy-start.2 = (bf16[64,2560]{1,0:T(8,128)(2,1)S(1)}, bf16[64,2560]{1,0:T(8,128)(2,1)}, u32[]{:S(2)}) copy-start(bf16[64,2560]{1,0:T(8,128)(2,1)} %param.16) | copy-start | bytes 983044
  118.8 53.6 %copy-start.6 = (bf16[2560]{0:T(1024)(128)(2,1)S(1)}, bf16[2560]{0:T(1024)(128)(2,1)}, u32[]{:S(2)}) copy-start(bf16[2560]{0:T(1024)(128)(2,1)} %param.23) | copy-start | bytes 15364
  154.0 32.8 %all-to-all-start.1 = ((f32[128,1,20]{2,1,0:T(1,128)}), f32[128,1,20]{2,1,0:T(1,128)S(1)}, u32[]{:S(2)}, u32[]{:S(2)}) async-start(f32[128,1,20]{2,1,0:T(1,128)} %bitcast.50), calls=%async_computation.1 | async-start | bytes 131072 | tf_op jit(solution)/shard_map/all_to_all | solution.py:170
  232.0 17.1 %collective-permute-start = (bf16[1,6,16,2560]{3,2,1,0:T(8,128)(2,1)S(1)}, bf16[1,6,16,2560]{3,2,1,0:T(8,128)(2,1)S(1)}, u32[]{:S(2)}, u32[]{:S(2)}) collective-permute-start(bf16[1,6,16,2560]{3,2,1,0:T(8,128)(2,1)S(1)} %bitcast.146), channel_id=1, source_target_pairs={{0,2},{2,4},{4,6},{6,0},{1,3},{3,5},{5,7},{7,1},{8,10},{10,12},{12... | collective-permute-start | bytes 1474568 | tf_op jit(solution)/shard_map/ppermute | solution.py:27
  236.8 41.3 %collective-permute-start.1 = (bf16[1,6,16,2560]{3,2,1,0:T(8,128)(2,1)S(1)}, bf16[1,6,16,2560]{3,2,1,0:T(8,128)(2,1)S(1)}, u32[]{:S(2)}, u32[]{:S(2)}) collective-permute-start(bf16[1,6,16,2560]{3,2,1,0:T(8,128)(2,1)S(1)} %bitcast.147), channel_id=1, source_target_pairs={{0,4},{2,6},{4,0},{6,2},{1,5},{3,7},{5,1},{7,3},{8,12},{10,14},{12... | collective-permute-start | bytes 1474568 | tf_op jit(solution)/shard_map/ppermute | solution.py:27
  238.7 39.4 %collective-permute-start.2 = (bf16[1,6,16,2560]{3,2,1,0:T(8,128)(2,1)S(1)}, bf16[1,6,16,2560]{3,2,1,0:T(8,128)(2,1)S(1)}, u32[]{:S(2)}, u32[]{:S(2)}) collective-permute-start(bf16[1,6,16,2560]{3,2,1,0:T(8,128)(2,1)S(1)} %bitcast.148), channel_id=1, source_target_pairs={{0,6},{2,0},{4,2},{6,4},{1,7},{3,1},{5,3},{7,5},{8,14},{10,8},{12,... | collective-permute-start | bytes 1474568 | tf_op jit(solution)/shard_map/ppermute | solution.py:27
  281.8 8.9 %copy-start.8 = (bf16[2,192,2560]{2,1,0:T(8,128)(2,1)S(1)}, bf16[2,192,2560]{2,1,0:T(8,128)(2,1)}, u32[]{:S(2)}) copy-start(bf16[2,192,2560]{2,1,0:T(8,128)(2,1)} %param.26) | copy-start | bytes 5898244
  282.1 7.3 %collective-permute-start.3 = (bf16[4,6,16,2560]{3,2,1,0:T(8,128)(2,1)S(1)}, bf16[4,6,16,2560]{3,2,1,0:T(8,128)(2,1)S(1)}, u32[]{:S(2)}, u32[]{:S(2)}) collective-permute-start(bf16[4,6,16,2560]{3,2,1,0:T(8,128)(2,1)S(1)} %broadcast_select_fusion), channel_id=1, source_target_pairs={{0,1},{1,0},{2,3},{3,2},{4,5},{5,4},{6,7},{7,6},{8,9},{9,8},{10,11... | collective-permute-start | bytes 5898248 | tf_op jit(solution)/shard_map/ppermute | solution.py:202
  289.4 1.3 copy-start.11
  301.0 10.7 %collective-permute-start.4 = (f32[4,6,16,2560]{3,2,1,0:T(8,128)}, f32[4,6,16,2560]{3,2,1,0:T(8,128)}, u32[]{:S(2)}, u32[]{:S(2)}) collective-permute-start(f32[4,6,16,2560]{3,2,1,0:T(8,128)} %convert.26), channel_id=1, source_target_pairs={{0,1},{1,0},{2,3},{3,2},{4,5},{5,4},{6,7},{7,6},{8,9},{9,8},{10,11... | collective-permute-start | bytes 11796488 | tf_op jit(solution)/shard_map/ppermute | solution.py:219
  303.3 2.3 copy-start.9
  303.6 1.3 copy-start.1
  305.6 1.5 copy-start.10
  316.2 14.8 %collective-permute-start.5 = (bf16[6,16,2560]{2,1,0:T(8,128)(2,1)}, bf16[6,16,2560]{2,1,0:T(8,128)(2,1)}, u32[]{:S(2)}, u32[]{:S(2)}) collective-permute-start(bf16[6,16,2560]{2,1,0:T(8,128)(2,1)} %get-tuple-element.31), channel_id=1, source_target_pairs={{0,2},{2,4},{4,6},{6,0},{1,3},{3,5},{5,7},{7,1},{8,10},{10,12},{12... | collective-permute-start | bytes 1474568 | tf_op jit(solution)/shard_map/ppermute | solution.py:39
  318.1 42.6 %collective-permute-start.6 = (bf16[6,16,2560]{2,1,0:T(8,128)(2,1)}, bf16[6,16,2560]{2,1,0:T(8,128)(2,1)}, u32[]{:S(2)}, u32[]{:S(2)}) collective-permute-start(bf16[6,16,2560]{2,1,0:T(8,128)(2,1)} %get-tuple-element.33), channel_id=1, source_target_pairs={{0,4},{2,6},{4,0},{6,2},{1,5},{3,7},{5,1},{7,3},{8,12},{10,14},{12... | collective-permute-start | bytes 1474568 | tf_op jit(solution)/shard_map/ppermute | solution.py:39
  323.1 41.7 %collective-permute-start.7 = (bf16[6,16,2560]{2,1,0:T(8,128)(2,1)}, bf16[6,16,2560]{2,1,0:T(8,128)(2,1)}, u32[]{:S(2)}, u32[]{:S(2)}) collective-permute-start(bf16[6,16,2560]{2,1,0:T(8,128)(2,1)} %get-tuple-element.32), channel_id=1, source_target_pairs={{0,6},{2,0},{4,2},{6,4},{1,7},{3,1},{5,3},{7,5},{8,14},{10,8},{12,... | collective-permute-start | bytes 1474568 | tf_op jit(solution)/shard_map/ppermute | solution.py:39
  366.5 5.0 %copy-start.12 = (bf16[2560,64]{0,1:T(8,128)(2,1)S(1)}, bf16[2560,64]{0,1:T(8,128)(2,1)}, u32[]{:S(2)}) copy-start(bf16[2560,64]{0,1:T(8,128)(2,1)} %param.24) | copy-start | bytes 983044
  367.6 39.9 %all-to-all-start.3 = ((bf16[6,16,2560]{2,0,1:T(8,128)(2,1)}), bf16[6,16,2560]{2,0,1:T(8,128)(2,1)S(1)}, u32[]{:S(2)}, u32[]{:S(2)}) async-start(bf16[6,16,2560]{2,0,1:T(8,128)(2,1)} %copy.183), calls=%async_computation.3 | async-start | bytes 1310720 | tf_op jit(solution)/shard_map/all_to_all | solution.py:221
